TPU v7x, 256 devices: a whole 4x4x8 slice. The times are simulated.
256 devices in a mesh: req: 64 (over x, y_lo, z), tp: 4 (over y_hi, core).
Axes of the slice: x: 4, y: 4 (y_hi: 2, y_lo: 2; y = y_hi * 2 + y_lo), z: 8, core: 2. Of those that a mesh axis runs over, the one named last changes fastest.
Arguments:
- hidden_in: bfloat16 [8192, 2048], P('req')
- attn_gain: float32 [2048], replicated, may hold values from 0.1 to 1.9
- w_query: bfloat16 [2048, 2048], P(None, 'tp'), may hold values from -0.125 to 0.125
- w_keyval: bfloat16 [2048, 4, 256], P(None, 'tp'), may hold values from -0.125 to 0.125
- w_out: bfloat16 [2048, 2048], P('tp'), may hold values from -0.125 to 0.125
- moe_gain: float32 [2048], replicated, may hold values from 0.1 to 1.9
- w_gate_up: bfloat16 [64, 2, 2048, 1408], P('req', None, None, 'tp'), may hold values from -0.125 to 0.125
- w_down: bfloat16 [64, 1408, 2048], P('req', 'tp'), may hold values from -0.15625 to 0.15625
- seg_ids: int32 [64, 128], P('req'), may hold values from 0 to 3, never falling along the last dimension, each value on 1 to 64 neighbouring positions
- cached_len: int32 [64], P('req'), may hold values from 2048 to 4096, as said below
- page_table: int32 [64, 32], P('req'), may hold values from 0 to 1023, as said below
- cache_pool: bfloat16 [1024, 4, 128, 256], P('req', 'tp')
- expert_ids: int32 [8192, 6], P('req'), may hold values from 0 to 63, all different within a row; in each aligned block of 128 rows (0 to 127, 128 to 255, ...) at most 16 rows name the same one
- expert_weights: float32 [8192, 6], P('req'), may hold values from 0.05 to 0.5
Outputs:
- layer_out: bfloat16 [8192, 2048], P('req')
Inputs may be any that keep to these rules, and one draw needn't show every extreme that they name: `seg_ids`: row r holds the prompt numbers of pack r, never falling along the row; each prompt has 1 to 64 tokens, one exactly that many. `cached_len`: some pack has exactly 4096 cached tokens. `page_table`: entry j of row r names the page holding tokens j * 128 to (j + 1) * 128 - 1 of pack r's cached prefix; page p lies on index p // 16 of req. At most 1 entries of one row lie on one owner, and in every row some owner holds exactly 1. Entries past the cached length name pages too. `expert_ids`: each row names 6 different experts. Among the rows of one pack no expert is named more than 16 times, a bound that some block reaches.
All inputs are finite; a program needn't handle non-finite values.
Results may differ from a plain program's by a relative error of at most 0.009.
Values may be sent and summed in bfloat16 or wider, within the bound.
No kernel may reach another device: no remote copies, remote signals or barrier semaphores. Data moves between devices by JAX's collectives and lax.ppermute only.
A program may use at most 128 MiB of HBM per device.

v0:
```python
import math

import jax
import jax.numpy as jnp
from jax import lax
from jax.sharding import PartitionSpec as P

eps = 1e-06
rope_base = 600000.0


def rms_scale(rows_in, gain):
    widened = rows_in.astype(jnp.float32)
    return widened * lax.rsqrt(jnp.mean(widened * widened, axis=-1, keepdims=True) + eps) * gain


def rotate(vectors, angles):
    half_dim = vectors.shape[-1] // 2
    first_half = vectors[..., :half_dim]
    second_half = vectors[..., half_dim:]
    cosine = jnp.cos(angles)[:, None, :]
    sine_vals = jnp.sin(angles)[:, None, :]
    return jnp.concatenate(
        [
            first_half * cosine - second_half * sine_vals,
            second_half * cosine + first_half * sine_vals,
        ],
        axis=-1,
    )


def positions(segment_row, cached):
    length = segment_row.shape[0]
    token_index = jnp.arange(length, dtype=jnp.int32)
    begins = jnp.concatenate([jnp.ones((1,), dtype=bool), segment_row[1:] != segment_row[:-1]])
    seg_start = lax.cummax(jnp.where(begins, token_index, 0), axis=0)
    carried = segment_row == segment_row[0]
    place = token_index - seg_start + jnp.where(carried, cached, 0)
    return (place, carried)


def make_angles(place, head_dim):
    inverse = rope_base ** (-(jnp.arange(head_dim // 2, dtype=jnp.float32) * 2.0 / head_dim))
    return place.astype(jnp.float32)[:, None] * inverse[None, :]


def admit(segment_row, carried, cached, prefix_len):
    length = segment_row.shape[0]
    token_index = jnp.arange(length, dtype=jnp.int32)
    prefix_ok = (jnp.arange(prefix_len, dtype=jnp.int32)[None, :] < cached) & carried[:, None]
    local_ok = (segment_row[:, None] == segment_row[None, :]) & (
        token_index[None, :] <= token_index[:, None]
    )
    return jnp.concatenate([prefix_ok, local_ok], axis=1)


def attend(queries, all_keys, all_values, admitted):
    scale = 1.0 / math.sqrt(queries.shape[-1])
    scores = (
        jnp.einsum("tkgd,knd->kgtn", queries, all_keys, preferred_element_type=jnp.float32) * scale
    )
    scores = jnp.where(admitted[None, None], scores, -1e30)
    highest = jnp.max(scores, axis=-1, keepdims=True)
    expo = jnp.exp(scores - highest)
    totals = jnp.sum(expo, axis=-1, keepdims=True)
    weights = (expo / totals).astype(jnp.bfloat16)
    context = jnp.einsum("kgtn,knd->tkgd", weights, all_values, preferred_element_type=jnp.float32)
    return context.astype(jnp.bfloat16)


def shards(
    hidden_in,
    attn_gain,
    w_query,
    w_keyval,
    w_out,
    moe_gain,
    w_gate_up,
    w_down,
    seg_ids,
    cached_len,
    page_table,
    cache_pool,
    expert_ids,
    expert_weights,
):
    tok_rows, model_width = hidden_in.shape
    head_dim = w_keyval.shape[2] // 2
    kv_local = w_keyval.shape[1]
    q_local = w_query.shape[1] // head_dim
    group_size = q_local // kv_local
    segment_row = seg_ids[0]
    cached = cached_len[0]
    place, carried = positions(segment_row, cached)
    angles = make_angles(place, head_dim)
    normed = rms_scale(hidden_in, attn_gain).astype(jnp.bfloat16)
    n_req = lax.axis_size("req")
    listed = page_table[0]
    pref_pages = listed.shape[0]
    pages_dev = cache_pool.shape[0]
    page_len = cache_pool.shape[2]
    cap_pages = (2 * pref_pages + n_req - 1) // n_req
    owners = listed // pages_dev
    entry_index = jnp.arange(pref_pages, dtype=jnp.int32)
    earlier = (owners[None, :] == owners[:, None]) & (entry_index[None, :] < entry_index[:, None])
    owner_rank = jnp.sum(earlier.astype(jnp.int32), axis=1)
    page_slot = listed % pages_dev
    cap_index = jnp.arange(cap_pages, dtype=jnp.int32)
    owner_index = jnp.arange(n_req, dtype=jnp.int32)
    wanted = (owners[None, None, :] == owner_index[:, None, None]) & (
        owner_rank[None, None, :] == cap_index[None, :, None]
    )
    request = jnp.sum(jnp.where(wanted, page_slot[None, None, :], 0), axis=2)
    asked_slots = lax.all_to_all(request, "req", split_axis=0, concat_axis=0, tiled=True)
    served = cache_pool[asked_slots.reshape(-1)].reshape(
        n_req, cap_pages, kv_local, page_len, 2 * head_dim
    )
    fetched = lax.all_to_all(served, "req", split_axis=0, concat_axis=0, tiled=True)
    fetched = fetched.reshape(n_req * cap_pages, kv_local, page_len, 2 * head_dim)[
        owners * cap_pages + owner_rank
    ]
    prefix = jnp.transpose(fetched, (1, 0, 2, 3)).reshape(
        kv_local, pref_pages * page_len, 2 * head_dim
    )
    queries = jnp.dot(normed, w_query, preferred_element_type=jnp.float32).reshape(
        tok_rows, q_local, head_dim
    )
    queries = (
        rotate(queries, angles)
        .astype(jnp.bfloat16)
        .reshape(tok_rows, kv_local, group_size, head_dim)
    )
    keyval = jnp.dot(
        normed,
        w_keyval.reshape(model_width, kv_local * 2 * head_dim),
        preferred_element_type=jnp.float32,
    ).reshape(tok_rows, kv_local, 2 * head_dim)
    keys_new = rotate(keyval[..., :head_dim], angles).astype(jnp.bfloat16)
    values_new = keyval[..., head_dim:].astype(jnp.bfloat16)
    all_keys = jnp.concatenate([prefix[..., :head_dim], jnp.transpose(keys_new, (1, 0, 2))], axis=1)
    all_values = jnp.concatenate(
        [prefix[..., head_dim:], jnp.transpose(values_new, (1, 0, 2))], axis=1
    )
    admitted = admit(segment_row, carried, cached, pref_pages * page_len)
    context = attend(queries, all_keys, all_values, admitted).reshape(tok_rows, q_local * head_dim)
    attention = lax.psum(jnp.dot(context, w_out, preferred_element_type=jnp.float32), "tp")
    resid = (hidden_in.astype(jnp.float32) + attention).astype(jnp.bfloat16)
    moe_in = rms_scale(resid, moe_gain).astype(jnp.bfloat16)
    topk = expert_ids.shape[1]
    n_exp = n_req * w_gate_up.shape[0]
    cap_e = 4 * tok_rows * topk // (3 * n_exp)
    flat_ids = expert_ids.reshape(-1)
    onehot = (flat_ids[:, None] == jnp.arange(n_exp, dtype=jnp.int32)[None, :]).astype(jnp.int32)
    slot_rank = jnp.sum((jnp.cumsum(onehot, axis=0) - 1) * onehot, axis=1)
    assign_slot = flat_ids * cap_e + slot_rank
    slot_match = assign_slot[None, :] == jnp.arange(n_exp * cap_e, dtype=jnp.int32)[:, None]
    selector = jnp.any(slot_match.reshape(n_exp * cap_e, tok_rows, topk), axis=2).astype(
        jnp.bfloat16
    )
    outgoing = (
        jnp.dot(selector, moe_in, preferred_element_type=jnp.float32)
        .astype(jnp.bfloat16)
        .reshape(n_exp, cap_e, model_width)
    )
    expert_in = lax.all_to_all(outgoing, "req", split_axis=0, concat_axis=0, tiled=True)
    expert_rows = expert_in.reshape(-1, model_width)
    gate_part = jnp.dot(expert_rows, w_gate_up[0, 0], preferred_element_type=jnp.float32)
    up_part = jnp.dot(expert_rows, w_gate_up[0, 1], preferred_element_type=jnp.float32)
    hidden_act = (jax.nn.silu(gate_part) * up_part).astype(jnp.bfloat16)
    expert_share = lax.psum_scatter(
        jnp.dot(hidden_act, w_down[0], preferred_element_type=jnp.float32).astype(jnp.bfloat16),
        "tp",
        scatter_dimension=0,
        tiled=True,
    )
    whole_rows = lax.all_gather(expert_share, "tp", axis=0, tiled=True)
    results = lax.all_to_all(
        whole_rows.reshape(-1, cap_e, model_width), "req", split_axis=0, concat_axis=0, tiled=True
    )
    picked = results.reshape(-1, model_width)[assign_slot].reshape(tok_rows, topk, model_width)
    moe_out = jnp.sum(expert_weights[:, :, None] * picked.astype(jnp.float32), axis=1)
    return (resid.astype(jnp.float32) + moe_out).astype(jnp.bfloat16)


def solution(mesh):
    in_specs = (
        P("req", None),
        P(),
        P(None, "tp"),
        P(None, "tp", None),
        P("tp", None),
        P(),
        P("req", None, None, "tp"),
        P("req", "tp", None),
        P("req", None),
        P("req"),
        P("req", None),
        P("req", "tp", None, None),
        P("req", None),
        P("req", None),
    )
    out_specs = P("req", None)
    return jax.shard_map(shards, mesh=mesh, in_specs=in_specs, out_specs=out_specs, check_vma=False)
```

profile of v0, /device:TPU:1, one launch (start us, length us, event | category | flops | bytes accessed | tf_op | source)
XLA Modules:
  0.0 549.3 jit_solution(17424029415147350403)
XLA Ops:
  6.5 0.8 and_select_fusion.3
  7.4 0.7 fusion.63
  8.0 0.2 convert_reduce_fusion
  8.2 0.1 select_reduce_fusion
  8.3 0.1 copy.54
  8.4 22.6 %all_to_all.27 = s32[64,1,1]{2,1,0:T(1,128)S(1)} all-to-all(s32[64,1,1]{2,1,0:T(1,128)S(1)} %copy.54), channel_id=1, replica_groups=mesh['req'=64,'tp'=4] {'req'}, dimensions={0} | all-to-all | bytes 512 | tf_op jit(solution)/shard_map/all_to_all | solution.py:114
  31.0 1.2 reduce.3
  32.2 4.0 gather_fusion
  36.2 5.8 %all-to-all-start.1 = ((bf16[64,1,1,128,256]{4,3,2,1,0:T(8,128)(2,1)}), bf16[64,1,1,128,256]{4,3,2,1,0:T(8,128)(2,1)}, u32[]{:S(2)}, u32[]{:S(2)}) async-start(bf16[64,1,1,128,256]{4,3,2,1,0:T(8,128)(2,1)} %bitcast.127), calls=%async_computation.1 | async-start | bytes 8388608 | tf_op jit(solution)/shard_map/all_to_all | solution.py:118
  42.0 0.0 all-reduce.2.cloned.1.call-start
  42.7 0.1 compare_bitcast_fusion
  42.8 0.1 add_select_fusion
  42.9 0.1 copy.55
  43.0 0.2 reduce-window.18
  43.2 0.1 reduce.4
  43.3 0.2 fusion.22
  43.5 2.1 fusion.40
  45.6 0.1 reshape.641
  45.8 1.6 convolution_bitcast_fusion
  47.4 0.1 fusion.54
  47.5 0.3 multiply_cosine_fusion
  47.8 0.3 fusion.57
  48.1 0.2 fusion.70
  48.3 0.1 subtract_convert_fusion
  48.4 2.1 broadcast_and_fusion
  50.6 82.7 %all-to-all-done.1 = bf16[64,1,1,128,256]{4,3,2,1,0:T(8,128)(2,1)} async-done(((bf16[64,1,1,128,256]{4,3,2,1,0:T(8,128)(2,1)}), bf16[64,1,1,128,256]{4,3,2,1,0:T(8,128)(2,1)}, u32[]{:S(2)}, u32[]{:S(2)}) %all-to-all-start.1) | async-done | bytes 4194336 | tf_op jit(solution)/shard_map/all_to_all | solution.py:118
  133.3 4.2 gather_fusion.1
  137.5 1.7 fusion.69
  139.2 1.4 fusion.71
  140.6 1.1 fusion
  141.7 1.7 fusion.13
  143.4 1.5 fusion.72
  145.0 0.0 all-reduce.2.cloned.1.call-update
  145.0 0.2 reduce-scatter.2.cloned.1.call-start
  145.2 0.1 copy.61
  145.3 0.1 eq.129
  145.5 0.1 eq.125
  145.6 1.8 reduce-window.19
  147.4 0.3 slice_reduce_fusion
  147.7 0.1 fusion.38
  147.9 0.1 reduce_sum.75
  148.0 0.1 copy.65
  148.1 0.5 fusion.3
  148.6 49.2 %all-reduce.2.cloned.1.call-done = f32[128,2048]{1,0:T(8,128)} async-done(((f32[128,2048]{1,0:T(8,128)}), f32[128,2048]{1,0:T(8,128)}) %all-reduce.2.cloned.1.call-update) | async-done | bytes 1048592 | tf_op jit(solution)/shard_map/psum | solution.py:146
  197.8 1.5 fusion.26
  199.3 1.3 convolution_convert_fusion.1
  200.6 0.0 copy-start.9
  200.6 103.3 %all_to_all.28 = bf16[64,16,2048]{2,1,0:T(8,128)(2,1)S(1)} all-to-all(bf16[64,16,2048]{2,1,0:T(8,128)(2,1)S(1)} %bitcast.128), channel_id=1, replica_groups=mesh['req'=64,'tp'=4] {'req'}, dimensions={0} | all-to-all | bytes 8388608 | tf_op jit(solution)/shard_map/all_to_all | solution.py:165
  304.0 2.0 copy-done.3
  306.0 2.9 fusion.6
  308.9 9.0 %convolution_convert_fusion = bf16[1024,2048]{1,0:T(8,128)(2,1)} fusion(bf16[1,352,2048]{2,1,0:T(8,128)(2,1)S(1)} %copy-done.10, bf16[1024,2048]{1,0:T(8,128)(2,1)} %bitcast.133, bf16[1,2,2048,352]{2,3,1,0:T(8,128)(2,1)} %param.20, f32[1024,352]{0,1:T(8,128)} %fusion.6), kind=kOutput, calls=%fused_computation.10 | convolution fusion | flops 2957049856 | bytes 12713984 | tf_op jit(solution)/shard_map/dot_general | solution.py:171
  317.8 0.0 reduce-scatter.2.cloned.1.call-update
  317.8 0.0 all-gather.2.cloned.1.call-start
  317.9 56.0 %reduce-scatter.2.cloned.1.call-done = bf16[256,2048]{1,0:T(8,128)(2,1)} async-done(((bf16[1024,2048]{1,0:T(8,128)(2,1)}), bf16[256,2048]{1,0:T(8,128)(2,1)}) %reduce-scatter.2.cloned.1.call-update) | async-done | bytes 1048592 | tf_op jit(solution)/shard_map/reduce_scatter | solution.py:170
  373.9 0.0 all-gather.2.cloned.1.call-update
  373.9 42.9 %all-gather.2.cloned.1.call-done = bf16[1024,2048]{1,0:T(8,128)(2,1)} async-done(((bf16[256,2048]{1,0:T(8,128)(2,1)}), bf16[1024,2048]{1,0:T(8,128)(2,1)}) %all-gather.2.cloned.1.call-update) | async-done | bytes 4194320 | tf_op jit(solution)/shard_map/all_gather | solution.py:176
  416.8 10.8 %all-to-all-start.3 = ((bf16[64,16,2048]{2,1,0:T(8,128)(2,1)}), bf16[64,16,2048]{2,1,0:T(8,128)(2,1)}, u32[]{:S(2)}, u32[]{:S(2)}) async-start(bf16[64,16,2048]{2,1,0:T(8,128)(2,1)} %bitcast.131), calls=%async_computation.4 | async-start | bytes 8388608 | tf_op jit(solution)/shard_map/all_to_all | solution.py:177
  427.6 0.1 mul.199
  427.8 0.1 copy.60
  427.9 90.8 %all-to-all-done.3 = bf16[64,16,2048]{2,1,0:T(8,128)(2,1)} async-done(((bf16[64,16,2048]{2,1,0:T(8,128)(2,1)}), bf16[64,16,2048]{2,1,0:T(8,128)(2,1)}, u32[]{:S(2)}, u32[]{:S(2)}) %all-to-all-start.3) | async-done | bytes 4194336 | tf_op jit(solution)/shard_map/all_to_all | solution.py:177
  518.7 9.8 %gather_fusion.2 = bf16[768,2048]{1,0:T(8,128)(2,1)} fusion(bf16[1024,2048]{1,0:T(8,128)(2,1)} %bitcast.37, s32[1024]{0:T(1024)S(1)} %pad_clamp_fusion), kind=kCustom, calls=%fused_computation.2 | custom fusion | bytes 6294528 | tf_op jit(solution)/shard_map/gather | solution.py:180
  528.5 6.6 %reshape.649 = f32[128,6,2048]{2,1,0:T(8,128)} reshape(bf16[768,2048]{1,0:T(8,128)(2,1)} %gather_fusion.2) | data formatting | bytes 9437184 | tf_op jit(solution)/shard_map/convert_element_type | solution.py:181
  535.1 6.8 %multiply_reduce_fusion = f32[128,2048]{1,0:T(8,128)S(1)} fusion(f32[128,6,2048]{2,1,0:T(8,128)} %reshape.649, f32[128,6]{1,0:T(8,128)S(1)} %copy.60), kind=kLoop, calls=%fused_computation.6 | loop fusion | flops 2883584 | bytes 7343104 | tf_op jit(solution)/shard_map/reduce_sum | solution.py:181
  541.8 0.9 fusion.29
  (39 shorter events, 0.3 us)
Async XLA Ops:
  6.5 136.9 %copy-start = (bf16[512,2048]{1,0:T(8,128)(2,1)S(1)}, bf16[512,2048]{1,0:T(8,128)(2,1)}, u32[]{:S(2)}) copy-start(bf16[512,2048]{1,0:T(8,128)(2,1)} %param.18) | copy-start | bytes 6291460
  36.2 6.5 %copy-start.6 = (s32[1,128]{1,0:T(1,128)S(1)}, s32[1,128]{1,0:T(1,128)}, u32[]{:S(2)}) copy-start(s32[1,128]{1,0:T(1,128)} %param.22) | copy-start | bytes 1540
  36.2 7.1 %copy-start.2 = (bf16[128,2048]{1,0:T(8,128)(2,1)S(1)}, bf16[128,2048]{1,0:T(8,128)(2,1)}, u32[]{:S(2)}) copy-start(bf16[128,2048]{1,0:T(8,128)(2,1)} %param.14) | copy-start | bytes 1572868
  36.2 7.3 %copy-start.4 = (f32[2048]{0:T(1024)S(1)}, f32[2048]{0:T(1024)}, u32[]{:S(2)}) copy-start(f32[2048]{0:T(1024)} %param.15) | copy-start | bytes 24580
  36.2 97.1 %all-to-all-start.1 = ((bf16[64,1,1,128,256]{4,3,2,1,0:T(8,128)(2,1)}), bf16[64,1,1,128,256]{4,3,2,1,0:T(8,128)(2,1)}, u32[]{:S(2)}, u32[]{:S(2)}) async-start(bf16[64,1,1,128,256]{4,3,2,1,0:T(8,128)(2,1)} %bitcast.127), calls=%async_computation.1 | async-start | bytes 8388608 | tf_op jit(solution)/shard_map/all_to_all | solution.py:118
  42.0 3.7 copy-start.11
  42.0 155.8 %all-reduce.2.cloned.1.call-start = ((), (), s32[]{:S(2)}) async-start(), calls=%async_computation.5 | async-start | bytes 2097152 | tf_op jit(solution)/shard_map/psum | solution.py:146
  143.4 1.8 copy-start.7
  144.9 54.3 %copy-start.5 = (f32[2048]{0:T(1024)S(1)}, f32[2048]{0:T(1024)}, u32[]{:S(2)}) copy-start(f32[2048]{0:T(1024)} %param.19) | copy-start | bytes 24580
  145.0 228.9 %reduce-scatter.2.cloned.1.call-start = ((), (), s32[]{:S(2)}) async-start(), calls=%async_computation.6 | async-start | bytes 5242880 | tf_op jit(solution)/shard_map/reduce_scatter | solution.py:170
  200.6 105.3 %copy-start.9 = (bf16[1,2,2048,352]{2,3,1,0:T(8,128)(2,1)S(1)}, bf16[1,2,2048,352]{2,3,1,0:T(8,128)(2,1)}, u32[]{:S(2)}) copy-start(bf16[1,2,2048,352]{2,3,1,0:T(8,128)(2,1)} %param.20) | copy-start | bytes 8650756
  304.0 2.0 copy-start.3
  306.0 2.9 copy-start.10
  317.8 99.0 %all-gather.2.cloned.1.call-start = ((), (), s32[]{:S(2)}) async-start(), calls=%async_computation.7 | async-start | bytes 5242880 | tf_op jit(solution)/shard_map/all_gather | solution.py:176
  416.8 10.9 %copy-start.8 = (f32[128,6]{0,1:T(8,128)S(1)}, f32[128,6]{0,1:T(8,128)}, u32[]{:S(2)}) copy-start(f32[128,6]{0,1:T(8,128)} %param.27) | copy-start | bytes 9220
  416.8 101.9 %all-to-all-start.3 = ((bf16[64,16,2048]{2,1,0:T(8,128)(2,1)}), bf16[64,16,2048]{2,1,0:T(8,128)(2,1)}, u32[]{:S(2)}, u32[]{:S(2)}) async-start(bf16[64,16,2048]{2,1,0:T(8,128)(2,1)} %bitcast.131), calls=%async_computation.4 | async-start | bytes 8388608 | tf_op jit(solution)/shard_map/all_to_all | solution.py:177
  535.1 7.7 %copy-start.1 = (bf16[512,2048]{1,0:T(8,128)(2,1)S(1)}, bf16[512,2048]{1,0:T(8,128)(2,1)}, u32[]{:S(2)}) copy-start(bf16[512,2048]{1,0:T(8,128)(2,1)} %param.18) | copy-start | bytes 6291460
Sparse Core Ops, SparseCore 0:
  145.1 52.6 all-reduce.1
  318.0 55.8 reduce-scatter.1
  375.7 41.0 all-gather.1
where the time goes:
time: 554 us; the launch traced here: 549 us
  waiting for transfers between devices  322 us (58%)
  blocking collectives  126 us (23%)
  local copies, waits for them, and re-layouts  29.9 us (5%)
  matrix products  21.4 us (4%)
  other arithmetic  19.5 us (4%)
  starting transfers between devices  16.9 us (3%)
  between operations  14.1 us (3%)
    all_to_all x1, blocking collectives, shards(): lax.all_to_all(outgoing, 'req', split_axis=0, concat_axis=0, tiled=True)  103 us
    all_to_all x1, waiting for transfers between devices, shards(): lax.all_to_all(whole_rows.reshape(-1, cap_e, model_width), 'req', split_a...  90.8 us
    all_to_all x1, waiting for transfers between devices, shards(): lax.all_to_all(served, 'req', split_axis=0, concat_axis=0, tiled=True)  82.7 us
    reduce_scatter x1, waiting for transfers between devices, shards(): lax.psum_scatter(jnp.dot(hidden_act, w_down[0], preferred_element_type=jn...  56 us
    psum x1, waiting for transfers between devices, shards(): lax.psum(jnp.dot(context, w_out, preferred_element_type=jnp.float32), 'tp')  49.2 us
    all_gather x1, waiting for transfers between devices, shards(): whole_rows = lax.all_gather(expert_share, 'tp', axis=0, tiled=True)  42.9 us
    all_to_all x1, blocking collectives, shards(): lax.all_to_all(request, 'req', split_axis=0, concat_axis=0, tiled=True)  22.6 us
  transfers between devices with their start and end apart: 5, of which 5 were waited for; matrix products, arithmetic and copies ran while one was open for 2% of the time, Pallas kernels for 0%

commit v1 on v0

--- a/solution.py
+++ b/solution.py
@@ -157,26 +157,31 @@
     selector = jnp.any(slot_match.reshape(n_exp * cap_e, tok_rows, topk), axis=2).astype(
         jnp.bfloat16
     )
+    n_tp = lax.axis_size("tp")
+    tp_me = lax.axis_index("tp")
+    cap_q = cap_e // n_tp
+    sel_q = lax.dynamic_slice_in_dim(
+        selector.reshape(n_exp, cap_e, tok_rows), tp_me * cap_q, cap_q, axis=1
+    )
     outgoing = (
-        jnp.dot(selector, moe_in, preferred_element_type=jnp.float32)
+        jnp.einsum("ecs,sd->ecd", sel_q, moe_in, preferred_element_type=jnp.float32)
         .astype(jnp.bfloat16)
-        .reshape(n_exp, cap_e, model_width)
-    )
-    expert_in = lax.all_to_all(outgoing, "req", split_axis=0, concat_axis=0, tiled=True)
+        .reshape(n_exp, cap_q * model_width)
+    )
+    expert_q = lax.all_to_all(outgoing, "req", split_axis=0, concat_axis=0, tiled=True)
+    expert_in = lax.all_gather(expert_q, "tp", axis=1, tiled=True)
     expert_rows = expert_in.reshape(-1, model_width)
     gate_part = jnp.dot(expert_rows, w_gate_up[0, 0], preferred_element_type=jnp.float32)
     up_part = jnp.dot(expert_rows, w_gate_up[0, 1], preferred_element_type=jnp.float32)
     hidden_act = (jax.nn.silu(gate_part) * up_part).astype(jnp.bfloat16)
-    expert_share = lax.psum_scatter(
-        jnp.dot(hidden_act, w_down[0], preferred_element_type=jnp.float32).astype(jnp.bfloat16),
-        "tp",
-        scatter_dimension=0,
-        tiled=True,
-    )
-    whole_rows = lax.all_gather(expert_share, "tp", axis=0, tiled=True)
-    results = lax.all_to_all(
-        whole_rows.reshape(-1, cap_e, model_width), "req", split_axis=0, concat_axis=0, tiled=True
-    )
+    partial = (
+        jnp.dot(hidden_act, w_down[0], preferred_element_type=jnp.float32)
+        .astype(jnp.bfloat16)
+        .reshape(n_req, cap_e * model_width)
+    )
+    expert_share = lax.psum_scatter(partial, "tp", scatter_dimension=1, tiled=True)
+    results_q = lax.all_to_all(expert_share, "req", split_axis=0, concat_axis=0, tiled=True)
+    results = lax.all_gather(results_q, "tp", axis=1, tiled=True)
     picked = results.reshape(-1, model_width)[assign_slot].reshape(tok_rows, topk, model_width)
     moe_out = jnp.sum(expert_weights[:, :, None] * picked.astype(jnp.float32), axis=1)
     return (resid.astype(jnp.float32) + moe_out).astype(jnp.bfloat16)

time: 554 us -> 615 us (1.11)
  other arithmetic: 19.5 us -> 82.4 us
  local copies, waits for them, and re-layouts: 29.9 us -> 68.3 us
  blocking collectives: 126 us -> 96.4 us
  starting transfers between devices: 16.9 us -> 6.34 us
  waiting for transfers between devices: 322 us -> 314 us
    all_to_all x1 -> x0, waiting for transfers between devices: 90.8 us -> none  [shards(): lax.all_to_all(whole_rows.reshape(-1, cap_e, model_width), 'req', split_a...]
    all_gather x1 -> x2, waiting for transfers between devices: 42.9 us -> 127 us  [the longest x1 63.5 us: shards(): results = lax.all_gather(results_q, 'tp', axis=1, tiled=True)]
    all_to_all x1, blocking collectives: 103 us -> 36.8 us  [shards(): lax.all_to_all(outgoing, 'req', split_axis=0, concat_axis=0, tiled=True)]
    all_gather x0 -> x2, other arithmetic: none -> 52.1 us  [the longest x1 26.1 us: shards(): results = lax.all_gather(results_q, 'tp', axis=1, tiled=True)]
    all_to_all x0 -> x1, blocking collectives: none -> 36.9 us  [shards(): lax.all_to_all(expert_share, 'req', split_axis=0, concat_axis=0, tiled=True)]
    reshape x0 -> x3, local copies, waits for them, and re-layouts: none -> 22.2 us  [the longest x1 7.41 us: shards(): expert_rows = expert_in.reshape(-1, model_width)]
    all_to_all x0 -> x2, other arithmetic: none -> 10.8 us  [the longest x1 8.15 us: shards(): lax.all_to_all(outgoing, 'req', split_axis=0, concat_axis=0, tiled=True)]
    all_to_all x1 -> x0, starting transfers between devices: 10.8 us -> none  [shards(): lax.all_to_all(whole_rows.reshape(-1, cap_e, model_width), 'req', split_a...]
where the time goes in v1:
time: 615 us; the launch traced here: 606 us
  waiting for transfers between devices  314 us (51%)
  blocking collectives  96.4 us (16%)
  other arithmetic  82.4 us (13%)
  local copies, waits for them, and re-layouts  68.3 us (11%)
  matrix products  23.3 us (4%)
  between operations  14.6 us (2%)
  starting transfers between devices  6.34 us (1%)
    all_to_all x1, waiting for transfers between devices, shards(): lax.all_to_all(served, 'req', split_axis=0, concat_axis=0, tiled=True)  82.7 us
    all_gather x1, waiting for transfers between devices, shards(): results = lax.all_gather(results_q, 'tp', axis=1, tiled=True)  63.5 us
    all_gather x1, waiting for transfers between devices, shards(): expert_in = lax.all_gather(expert_q, 'tp', axis=1, tiled=True)  63.4 us
    reduce_scatter x1, waiting for transfers between devices, shards(): lax.psum_scatter(partial, 'tp', scatter_dimension=1, tiled=True)  55.6 us
    psum x1, waiting for transfers between devices, shards(): lax.psum(jnp.dot(context, w_out, preferred_element_type=jnp.float32), 'tp')  49.1 us
    all_to_all x1, blocking collectives, shards(): lax.all_to_all(expert_share, 'req', split_axis=0, concat_axis=0, tiled=True)  36.9 us
    all_to_all x1, blocking collectives, shards(): lax.all_to_all(outgoing, 'req', split_axis=0, concat_axis=0, tiled=True)  36.8 us
    all_gather x1, other arithmetic, shards(): results = lax.all_gather(results_q, 'tp', axis=1, tiled=True)  26.1 us
  transfers between devices with their start and end apart: 5, of which 5 were waited for; matrix products, arithmetic and copies ran while one was open for 2% of the time, Pallas kernels for 0%

profile of v1, /device:TPU:1, one launch (start us, length us, event | category | flops | bytes accessed | tf_op | source)
XLA Modules:
  0.0 605.7 jit_solution(16908138329106039818)
XLA Ops:
  6.5 0.8 fusion.65
  7.3 0.7 and_select_fusion.3
  8.0 0.2 convert_reduce_fusion
  8.4 22.6 %all_to_all.42 = s32[64,1,1]{2,1,0:T(1,128)S(1)} all-to-all(s32[64,1,1]{2,1,0:T(1,128)S(1)} %copy.63), channel_id=1, replica_groups=mesh['req'=64,'tp'=4] {'req'}, dimensions={0} | all-to-all | bytes 512 | tf_op jit(solution)/shard_map/all_to_all | solution.py:114
  31.0 1.2 reduce.3
  32.2 4.0 gather_fusion
  36.2 5.8 all-to-all-start.1
  42.9 0.1 copy.64
  43.0 0.2 reduce-window.18
  43.2 0.1 reduce.4
  43.3 0.2 fusion.22
  43.5 2.1 fusion.41
  45.8 1.6 convolution_bitcast_fusion
  47.5 0.3 fusion.59
  47.8 0.3 multiply_cosine_fusion
  48.1 0.2 fusion.72
  48.4 2.1 broadcast_and_fusion
  50.6 82.7 %all-to-all-done.1 = bf16[64,1,1,128,256]{4,3,2,1,0:T(8,128)(2,1)} async-done(((bf16[64,1,1,128,256]{4,3,2,1,0:T(8,128)(2,1)}), bf16[64,1,1,128,256]{4,3,2,1,0:T(8,128)(2,1)}, u32[]{:S(2)}, u32[]{:S(2)}) %all-to-all-start.1) | async-done | bytes 4194336 | tf_op jit(solution)/shard_map/all_to_all | solution.py:118
  133.3 4.2 gather_fusion.1
  137.5 1.7 fusion.71
  139.2 1.4 fusion.73
  140.6 1.1 fusion
  141.7 1.7 fusion.13
  143.4 1.5 fusion.74
  145.0 0.2 all-gather.5.cloned.1.call-start
  145.2 0.1 copy.70
  145.3 0.1 eq.129
  145.5 0.1 eq.125
  145.6 1.8 reduce-window.19
  147.4 0.3 slice_reduce_fusion
  147.7 0.1 fusion.39
  147.9 0.1 reduce_sum.75
  148.1 0.5 fusion.3
  148.7 49.1 %all-reduce.2.cloned.1.call-done = f32[128,2048]{1,0:T(8,128)} async-done(((f32[128,2048]{1,0:T(8,128)}), f32[128,2048]{1,0:T(8,128)}) %all-reduce.2.cloned.1.call-update) | async-done | bytes 1048592 | tf_op jit(solution)/shard_map/psum | solution.py:146
  197.8 1.5 fusion.26
  199.2 0.5 convolution_convert_fusion.1
  199.8 1.8 copy.76
  201.6 6.2 %all_to_all.37 = bf16[64,1,8192]{2,1,0:T(2,128)(2,1)S(1)} reshape(bf16[64,4,2048]{2,1,0:T(4,128)(2,1)} %copy.76) | data formatting | bytes 2097152 | tf_op jit(solution)/shard_map/all_to_all | solution.py:171
  207.7 0.5 broadcast.486
  208.2 8.1 %reduce.11 = bf16[64,8192]{1,0:T(8,128)(2,1)} reduce(bf16[64,1,8192]{2,1,0:T(2,128)(2,1)S(1)} %all_to_all.37, bf16[]{:T(256)} %broadcast.486), dimensions={1}, to_apply=%all_to_all.37.reduce_sub_computation | reduce | bytes 2097154 | tf_op jit(solution)/shard_map/all_to_all | solution.py:171
  216.4 1.8 reshape.700
  218.2 36.8 %all_to_all.43 = bf16[64,2,4096]{2,1,0:T(2,128)(2,1)S(1)} all-to-all(bf16[64,2,4096]{2,1,0:T(2,128)(2,1)S(1)} %reshape.700), channel_id=1, replica_groups=mesh['req'=64,'tp'=4] {'req'}, dimensions={0} | all-to-all | bytes 2097152 | tf_op jit(solution)/shard_map/all_to_all | solution.py:171
  255.1 3.5 reshape.701
  258.6 0.3 reduce-scatter.2.cloned.1.call-start
  258.9 63.4 %all-gather.5.cloned.1.call-done = bf16[64,1,32768]{2,1,0:T(2,128)(2,1)} async-done(((bf16[64,1,8192]{2,1,0:T(2,128)(2,1)}), bf16[64,1,32768]{2,1,0:T(2,128)(2,1)}) %all-gather.5.cloned.1.call-update) | async-done | bytes 4194320 | tf_op jit(solution)/shard_map/all_gather | solution.py:172
  322.2 26.1 %reduce.6 = bf16[64,32768]{1,0:T(8,128)(2,1)} reduce(bf16[64,1,32768]{2,1,0:T(2,128)(2,1)} %all-gather.5.cloned.1.call-done, bf16[]{:T(256)} %constant.92), dimensions={1}, to_apply=%all-gather.reduce_sub_computation | reduce | bytes 8388610 | tf_op jit(solution)/shard_map/all_gather | solution.py:172
  348.3 7.4 %reshape.652 = bf16[1024,2048]{1,0:T(8,128)(2,1)} reshape(bf16[64,32768]{1,0:T(8,128)(2,1)} %reduce.6) | data formatting | bytes 8388608 | tf_op jit(solution)/shard_map/reshape | solution.py:173
  355.7 5.6 fusion.6
  361.3 9.0 %convolution_convert_fusion = bf16[1024,2048]{1,0:T(8,128)(2,1)} fusion(bf16[1,352,2048]{2,1,0:T(8,128)(2,1)S(1)} %copy-done.8, bf16[1024,2048]{1,0:T(8,128)(2,1)} %reshape.652, bf16[1,2,2048,352]{2,3,1,0:T(8,128)(2,1)} %param.20, f32[1024,352]{0,1:T(8,128)} %fusion.6), kind=kOutput, calls=%fused_computation.10 | convolution fusion | flops 2957049856 | bytes 12713984 | tf_op jit(solution)/shard_map/dot_general | solution.py:178
  370.3 7.4 %reshape.653 = bf16[64,32768]{1,0:T(8,128)(2,1)} reshape(bf16[1024,2048]{1,0:T(8,128)(2,1)} %convolution_convert_fusion) | data formatting | bytes 8388608 | tf_op jit(solution)/shard_map/reshape | solution.py:180
  377.8 55.6 %reduce-scatter.2.cloned.1.call-done = bf16[64,8192]{1,0:T(8,128)(2,1)} async-done(((bf16[64,32768]{1,0:T(8,128)(2,1)}), bf16[64,8192]{1,0:T(8,128)(2,1)}) %reduce-scatter.2.cloned.1.call-update) | async-done | bytes 1048592 | tf_op jit(solution)/shard_map/reduce_scatter | solution.py:182
  433.4 2.7 reduce.12
  436.1 0.8 reshape.702
  436.9 36.9 %all_to_all.44 = bf16[64,2,4096]{2,1,0:T(2,128)(2,1)S(1)} all-to-all(bf16[64,2,4096]{2,1,0:T(2,128)(2,1)S(1)} %reshape.702), channel_id=1, replica_groups=mesh['req'=64,'tp'=4] {'req'}, dimensions={0} | all-to-all | bytes 2097152 | tf_op jit(solution)/shard_map/all_to_all | solution.py:183
  473.8 3.5 reshape.703
  477.4 0.1 copy.69
  477.5 0.1 mul.203
  477.7 63.5 %all-gather.7.cloned.1.call-done = bf16[64,1,32768]{2,1,0:T(2,128)(2,1)} async-done(((bf16[64,1,8192]{2,1,0:T(2,128)(2,1)}), bf16[64,1,32768]{2,1,0:T(2,128)(2,1)}) %all-gather.7.cloned.1.call-update) | async-done | bytes 4194320 | tf_op jit(solution)/shard_map/all_gather | solution.py:184
  541.2 26.1 %reduce.7 = bf16[64,32768]{1,0:T(8,128)(2,1)} reduce(bf16[64,1,32768]{2,1,0:T(2,128)(2,1)} %all-gather.7.cloned.1.call-done, bf16[]{:T(256)} %constant.92), dimensions={1}, to_apply=%all-gather.1.reduce_sub_computation | reduce | bytes 8388610 | tf_op jit(solution)/shard_map/all_gather | solution.py:184
  567.2 7.4 %reshape.654 = bf16[1024,2048]{1,0:T(8,128)(2,1)} reshape(bf16[64,32768]{1,0:T(8,128)(2,1)} %reduce.7) | data formatting | bytes 8388608 | tf_op jit(solution)/shard_map/reshape | solution.py:185
  574.6 9.8 %gather_fusion.2 = bf16[768,2048]{1,0:T(8,128)(2,1)} fusion(bf16[1024,2048]{1,0:T(8,128)(2,1)} %reshape.654, s32[1024]{0:T(1024)S(1)} %pad_clamp_fusion), kind=kCustom, calls=%fused_computation.2 | custom fusion | bytes 6294528 | tf_op jit(solution)/shard_map/gather | solution.py:185
  584.5 6.6 %reshape.655 = f32[128,6,2048]{2,1,0:T(8,128)} reshape(bf16[768,2048]{1,0:T(8,128)(2,1)} %gather_fusion.2) | data formatting | bytes 9437184 | tf_op jit(solution)/shard_map/convert_element_type | solution.py:186
  591.0 6.8 %multiply_reduce_fusion = f32[128,2048]{1,0:T(8,128)S(1)} fusion(f32[128,6,2048]{2,1,0:T(8,128)} %reshape.655, f32[128,6]{1,0:T(8,128)S(1)} %copy.69), kind=kLoop, calls=%fused_computation.6 | loop fusion | flops 2883584 | bytes 7343104 | tf_op jit(solution)/shard_map/reduce_sum | solution.py:186
  597.8 0.9 fusion.29
  (52 shorter events, 1.1 us)
Async XLA Ops:
  6.5 136.9 %copy-start = (bf16[512,2048]{1,0:T(8,128)(2,1)S(1)}, bf16[512,2048]{1,0:T(8,128)(2,1)}, u32[]{:S(2)}) copy-start(bf16[512,2048]{1,0:T(8,128)(2,1)} %param.18) | copy-start | bytes 6291460
  36.2 6.5 %copy-start.5 = (s32[1,128]{1,0:T(1,128)S(1)}, s32[1,128]{1,0:T(1,128)}, u32[]{:S(2)}) copy-start(s32[1,128]{1,0:T(1,128)} %param.22) | copy-start | bytes 1540
  36.2 7.1 %copy-start.2 = (bf16[128,2048]{1,0:T(8,128)(2,1)S(1)}, bf16[128,2048]{1,0:T(8,128)(2,1)}, u32[]{:S(2)}) copy-start(bf16[128,2048]{1,0:T(8,128)(2,1)} %param.14) | copy-start | bytes 1572868
  36.2 7.3 %copy-start.3 = (f32[2048]{0:T(1024)S(1)}, f32[2048]{0:T(1024)}, u32[]{:S(2)}) copy-start(f32[2048]{0:T(1024)} %param.15) | copy-start | bytes 24580
  36.2 97.1 %all-to-all-start.1 = ((bf16[64,1,1,128,256]{4,3,2,1,0:T(8,128)(2,1)}), bf16[64,1,1,128,256]{4,3,2,1,0:T(8,128)(2,1)}, u32[]{:S(2)}, u32[]{:S(2)}) async-start(bf16[64,1,1,128,256]{4,3,2,1,0:T(8,128)(2,1)} %bitcast.127), calls=%async_computation.1 | async-start | bytes 8388608 | tf_op jit(solution)/shard_map/all_to_all | solution.py:118
  42.0 3.7 copy-start.9
  42.0 155.7 %all-reduce.2.cloned.1.call-start = ((), (), s32[]{:S(2)}) async-start(), calls=%async_computation.5 | async-start | bytes 2097152 | tf_op jit(solution)/shard_map/psum | solution.py:146
  143.4 1.8 copy-start.6
  144.9 54.3 %copy-start.4 = (f32[2048]{0:T(1024)S(1)}, f32[2048]{0:T(1024)}, u32[]{:S(2)}) copy-start(f32[2048]{0:T(1024)} %param.19) | copy-start | bytes 24580
  145.0 177.3 %all-gather.5.cloned.1.call-start = ((), (), s32[]{:S(2)}) async-start(), calls=%async_computation.7 | async-start | bytes 10485760 | tf_op jit(solution)/shard_map/all_gather | solution.py:172
  258.6 174.8 %reduce-scatter.2.cloned.1.call-start = ((), (), s32[]{:S(2)}) async-start(), calls=%async_computation.6 | async-start | bytes 5242880 | tf_op jit(solution)/shard_map/reduce_scatter | solution.py:182
  355.7 5.6 copy-start.8
  377.8 163.4 %all-gather.7.cloned.1.call-start = ((), (), s32[]{:S(2)}) async-start(), calls=%async_computation.8 | async-start | bytes 10485760 | tf_op jit(solution)/shard_map/all_gather | solution.py:184
  473.8 3.5 copy-start.7
  591.0 7.7 %copy-start.1 = (bf16[512,2048]{1,0:T(8,128)(2,1)S(1)}, bf16[512,2048]{1,0:T(8,128)(2,1)}, u32[]{:S(2)}) copy-start(bf16[512,2048]{1,0:T(8,128)(2,1)} %param.18) | copy-start | bytes 6291460
Sparse Core Ops, SparseCore 0:
  145.1 52.6 all-reduce.1
  258.7 63.4 all-gather.4
  377.9 55.4 reduce-scatter.1
  477.5 63.6 all-gather.6

commit v2 on v0

--- a/solution.py
+++ b/solution.py
@@ -143,9 +143,22 @@
     )
     admitted = admit(segment_row, carried, cached, pref_pages * page_len)
     context = attend(queries, all_keys, all_values, admitted).reshape(tok_rows, q_local * head_dim)
-    attention = lax.psum(jnp.dot(context, w_out, preferred_element_type=jnp.float32), "tp")
-    resid = (hidden_in.astype(jnp.float32) + attention).astype(jnp.bfloat16)
-    moe_in = rms_scale(resid, moe_gain).astype(jnp.bfloat16)
+    n_tp = lax.axis_size("tp")
+    tp_me = lax.axis_index("tp")
+    quarter = model_width // n_tp
+    attn_part = jnp.einsum(
+        "tc,cqd->qtd",
+        context,
+        w_out.reshape(-1, n_tp, quarter),
+        preferred_element_type=jnp.float32,
+    )
+    attn_q = lax.psum_scatter(attn_part, "tp", scatter_dimension=0, tiled=True)[0]
+    hidden_q = lax.dynamic_slice_in_dim(hidden_in, tp_me * quarter, quarter, axis=1)
+    resid_q = (hidden_q.astype(jnp.float32) + attn_q).astype(jnp.bfloat16)
+    resid_wide = resid_q.astype(jnp.float32)
+    sq_sum = lax.psum(jnp.sum(resid_wide * resid_wide, axis=-1, keepdims=True), "tp")
+    gain_q = lax.dynamic_slice_in_dim(moe_gain, tp_me * quarter, quarter, axis=0)
+    moe_in = (resid_wide * lax.rsqrt(sq_sum / model_width + eps) * gain_q).astype(jnp.bfloat16)
     topk = expert_ids.shape[1]
     n_exp = n_req * w_gate_up.shape[0]
     cap_e = 4 * tok_rows * topk // (3 * n_exp)
@@ -160,26 +173,38 @@
     outgoing = (
         jnp.dot(selector, moe_in, preferred_element_type=jnp.float32)
         .astype(jnp.bfloat16)
-        .reshape(n_exp, cap_e, model_width)
-    )
-    expert_in = lax.all_to_all(outgoing, "req", split_axis=0, concat_axis=0, tiled=True)
-    expert_rows = expert_in.reshape(-1, model_width)
-    gate_part = jnp.dot(expert_rows, w_gate_up[0, 0], preferred_element_type=jnp.float32)
-    up_part = jnp.dot(expert_rows, w_gate_up[0, 1], preferred_element_type=jnp.float32)
+        .reshape(n_exp, cap_e, quarter)
+    )
+    expert_q = lax.all_to_all(outgoing, "req", split_axis=0, concat_axis=0, tiled=True)
+    expert_in = lax.all_gather(expert_q, "tp", axis=0, tiled=False).reshape(n_tp, -1, quarter)
+    hidden_units = w_gate_up.shape[3]
+    gate_part = jnp.einsum(
+        "qnd,qdh->nh",
+        expert_in,
+        w_gate_up[0, 0].reshape(n_tp, quarter, hidden_units),
+        preferred_element_type=jnp.float32,
+    )
+    up_part = jnp.einsum(
+        "qnd,qdh->nh",
+        expert_in,
+        w_gate_up[0, 1].reshape(n_tp, quarter, hidden_units),
+        preferred_element_type=jnp.float32,
+    )
     hidden_act = (jax.nn.silu(gate_part) * up_part).astype(jnp.bfloat16)
-    expert_share = lax.psum_scatter(
-        jnp.dot(hidden_act, w_down[0], preferred_element_type=jnp.float32).astype(jnp.bfloat16),
-        "tp",
-        scatter_dimension=0,
-        tiled=True,
-    )
-    whole_rows = lax.all_gather(expert_share, "tp", axis=0, tiled=True)
-    results = lax.all_to_all(
-        whole_rows.reshape(-1, cap_e, model_width), "req", split_axis=0, concat_axis=0, tiled=True
-    )
-    picked = results.reshape(-1, model_width)[assign_slot].reshape(tok_rows, topk, model_width)
-    moe_out = jnp.sum(expert_weights[:, :, None] * picked.astype(jnp.float32), axis=1)
-    return (resid.astype(jnp.float32) + moe_out).astype(jnp.bfloat16)
+    partial = jnp.einsum(
+        "nh,hqd->qnd",
+        hidden_act,
+        w_down[0].reshape(hidden_units, n_tp, quarter),
+        preferred_element_type=jnp.float32,
+    ).astype(jnp.bfloat16)
+    expert_share = lax.psum_scatter(partial, "tp", scatter_dimension=0, tiled=True).reshape(
+        n_req, cap_e, quarter
+    )
+    results = lax.all_to_all(expert_share, "req", split_axis=0, concat_axis=0, tiled=True)
+    picked = results.reshape(-1, quarter)[assign_slot].reshape(tok_rows, topk, quarter)
+    moe_q = jnp.sum(expert_weights[:, :, None] * picked.astype(jnp.float32), axis=1)
+    layer_q = (resid_wide + moe_q).astype(jnp.bfloat16)
+    return lax.all_gather(layer_q, "tp", axis=1, tiled=True)
 
 
 def solution(mesh):

time: 554 us -> 404 us (0.73)
  waiting for transfers between devices: 322 us -> 227 us
  blocking collectives: 126 us -> 76.8 us
    all_to_all x1, blocking collectives: 103 us -> 35.7 us  [shards(): lax.all_to_all(outgoing, 'req', split_axis=0, concat_axis=0, tiled=True)]
    all_to_all x1, waiting for transfers between devices: 90.8 us -> 26.4 us  [shards(): lax.all_to_all(expert_share, 'req', split_axis=0, concat_axis=0, tiled=True)]
    psum x1 -> x0, waiting for transfers between devices: 49.2 us -> none  [shards(): lax.psum(jnp.dot(context, w_out, preferred_element_type=jnp.float32), 'tp')]
    reduce_scatter x1 -> x2, waiting for transfers between devices: 56 us -> 89.4 us  [the longest x1 55.7 us: shards(): lax.psum_scatter(partial, 'tp', scatter_dimension=0, tiled=True)]
    all_gather x1, waiting for transfers between devices: 42.9 us -> 26.9 us  [shards(): lax.all_gather(expert_q, 'tp', axis=0, tiled=False)]
    all_gather x0 -> x1, blocking collectives: none -> 11.1 us  [shards(): return lax.all_gather(layer_q, 'tp', axis=1, tiled=True)]
    another operation x0 -> x3, local copies, waits for them, and re-layouts: none -> 10.9 us  [the longest x1 4.54 us: shards(): w_down[0].reshape(hidden_units, n_tp, quarter)]
    psum x0 -> x1, blocking collectives: none -> 7.37 us  [shards(): lax.psum(jnp.sum(resid_wide * resid_wide, axis=-1, keepdims=True), 'tp')]
  transfers between devices with their start and end apart: 5 -> 5, of which waited for: 5 -> 5; matrix products, arithmetic and copies ran while one was open for 2% -> 6% of each run, Pallas kernels for 0% -> 0%
where the time goes in v2:
time: 404 us; the launch traced here: 403 us
  waiting for transfers between devices  227 us (56%)
  blocking collectives  76.8 us (19%)
  local copies, waits for them, and re-layouts  33.1 us (8%)
  matrix products  21.6 us (5%)
  starting transfers between devices  16.5 us (4%)
  other arithmetic  14.3 us (4%)
  between operations  14.1 us (3%)
    all_to_all x1, waiting for transfers between devices, shards(): lax.all_to_all(served, 'req', split_axis=0, concat_axis=0, tiled=True)  84.3 us
    reduce_scatter x1, waiting for transfers between devices, shards(): lax.psum_scatter(partial, 'tp', scatter_dimension=0, tiled=True)  55.7 us
    all_to_all x1, blocking collectives, shards(): lax.all_to_all(outgoing, 'req', split_axis=0, concat_axis=0, tiled=True)  35.7 us
    reduce_scatter x1, waiting for transfers between devices, shards(): lax.psum_scatter(attn_part, 'tp', scatter_dimension=0, tiled=True)[0]  33.7 us
    all_gather x1, waiting for transfers between devices, shards(): lax.all_gather(expert_q, 'tp', axis=0, tiled=False)  26.9 us
    all_to_all x1, waiting for transfers between devices, shards(): lax.all_to_all(expert_share, 'req', split_axis=0, concat_axis=0, tiled=True)  26.4 us
    all_to_all x1, blocking collectives, shards(): lax.all_to_all(request, 'req', split_axis=0, concat_axis=0, tiled=True)  22.6 us
    all_gather x1, blocking collectives, shards(): return lax.all_gather(layer_q, 'tp', axis=1, tiled=True)  11.1 us
  transfers between devices with their start and end apart: 5, of which 5 were waited for; matrix products, arithmetic and copies ran while one was open for 6% of the time, Pallas kernels for 0%

profile of v2, /device:TPU:1, one launch (start us, length us, event | category | flops | bytes accessed | tf_op | source)
XLA Modules:
  0.0 403.5 jit_solution(13599505581170249118)
XLA Ops:
  6.5 0.8 and_select_fusion.3
  7.4 0.7 fusion.70
  8.0 0.2 convert_reduce_fusion
  8.2 0.1 select_reduce_fusion
  8.3 0.1 copy.70
  8.4 22.6 %all_to_all.27 = s32[64,1,1]{2,1,0:T(1,128)S(1)} all-to-all(s32[64,1,1]{2,1,0:T(1,128)S(1)} %copy.70), channel_id=1, replica_groups=mesh['req'=64,'tp'=4] {'req'}, dimensions={0} | all-to-all | bytes 512 | tf_op jit(solution)/shard_map/all_to_all | solution.py:114
  31.0 1.2 reduce.3
  32.2 4.0 gather_fusion
  36.2 5.8 %all-to-all-start.1 = ((bf16[64,1,1,128,256]{4,3,2,1,0:T(8,128)(2,1)}), bf16[64,1,1,128,256]{4,3,2,1,0:T(8,128)(2,1)}, u32[]{:S(2)}, u32[]{:S(2)}) async-start(bf16[64,1,1,128,256]{4,3,2,1,0:T(8,128)(2,1)} %bitcast.158), calls=%async_computation.1 | async-start | bytes 8388608 | tf_op jit(solution)/shard_map/all_to_all | solution.py:118
  42.7 0.1 compare_bitcast_fusion
  42.8 0.1 add_select_fusion
  42.9 0.1 copy.71
  43.0 0.2 reduce-window.18
  43.2 0.1 reduce.4
  43.3 0.2 fusion.29
  43.5 0.5 fusion.44
  44.0 0.1 reshape.636
  44.2 1.6 convolution_bitcast_fusion.2
  45.8 0.1 fusion.61
  45.9 0.3 multiply_cosine_fusion
  46.2 0.3 fusion.64
  46.5 0.2 fusion.78
  46.7 0.1 subtract_convert_fusion
  46.8 2.1 broadcast_and_fusion
  49.0 84.3 %all-to-all-done.1 = bf16[64,1,1,128,256]{4,3,2,1,0:T(8,128)(2,1)} async-done(((bf16[64,1,1,128,256]{4,3,2,1,0:T(8,128)(2,1)}), bf16[64,1,1,128,256]{4,3,2,1,0:T(8,128)(2,1)}, u32[]{:S(2)}, u32[]{:S(2)}) %all-to-all-start.1) | async-done | bytes 4194336 | tf_op jit(solution)/shard_map/all_to_all | solution.py:118
  133.3 4.2 %gather_fusion.1 = bf16[32,128,256]{2,1,0:T(8,128)(2,1)} fusion(bf16[64,128,256]{2,1,0:T(8,128)(2,1)} %bitcast.6, s32[1024]{0:T(1024)S(1)} %pad_clamp_fusion.1), kind=kCustom, calls=%fused_computation.1 | custom fusion | bytes 4194432 | tf_op jit(solution)/shard_map/gather | solution.py:119
  137.5 1.7 fusion.77
  139.2 1.4 fusion.79
  140.6 1.1 fusion
  141.7 1.7 fusion.20
  143.5 1.5 fusion.14
  144.9 0.2 all-gather.3.cloned.1.call-start
  145.2 0.1 copy.79
  145.3 0.1 eq.129
  145.4 0.1 eq.125
  145.6 1.8 reduce-window.19
  147.4 0.3 slice_reduce_fusion
  147.7 0.1 fusion.42
  147.9 0.1 reduce_sum.75
  148.0 0.6 broadcast_multiply_fusion
  148.7 0.8 dynamic_slice.7
  149.5 0.5 fusion.3
  150.0 33.7 %reduce-scatter.3.cloned.1.call-done = f32[1,128,512]{2,1,0:T(8,128)} async-done(((f32[4,128,512]{2,1,0:T(8,128)}), f32[1,128,512]{2,1,0:T(8,128)}) %reduce-scatter.3.cloned.1.call-update) | async-done | bytes 262160 | tf_op jit(solution)/shard_map/reduce_scatter | solution.py:155
  183.7 1.1 fusion.36
  184.8 7.4 %psum.7 = f32[128,1]{0,1:T(1,128)S(1)} all-reduce(f32[128,1]{0,1:T(1,128)S(1)} %bitcast.169), channel_id=1, replica_groups=mesh['req'=64,'tp'=4] {'tp'}, use_global_device_ids=true, to_apply=%region_12.13 | all-reduce | flops 128 | bytes 1024 | tf_op jit(solution)/shard_map/psum | solution.py:159
  192.1 0.5 convolution_convert_fusion
  192.7 35.7 %all_to_all.28 = bf16[64,16,512]{2,1,0:T(8,128)(2,1)} all-to-all(bf16[64,16,512]{2,1,0:T(8,128)(2,1)S(1)} %bitcast.161), channel_id=1, replica_groups=mesh['req'=64,'tp'=4] {'req'}, dimensions={0} | all-to-all | bytes 2097152 | tf_op jit(solution)/shard_map/all_to_all | solution.py:178
  228.5 3.2 fusion.76
  231.7 4.4 %reshape_squeeze.9 = bf16[4,512,352]{1,0,2:T(4,128)(2,1)} reshape(bf16[1,1,2048,352]{2,3,1,0:T(8,128)(2,1)} %get-tuple-element.9) | data formatting | bytes 2883584 | tf_op jit(solution)/shard_map/reshape;squeeze | solution.py:184
  236.1 2.0 reshape_squeeze.10
  238.1 4.5 %reshape_squeeze.11 = bf16[352,4,512]{2,1,0:T(4,128)(2,1)} reshape(bf16[1,352,2048]{2,1,0:T(8,128)(2,1)} %param.21) | data formatting | bytes 2883584 | tf_op jit(solution)/shard_map/reshape;squeeze | solution.py:197
  242.6 26.9 %all-gather.3.cloned.1.call-done = bf16[256,16,512]{2,1,0:T(8,128)(2,1)} async-done(((bf16[64,16,512]{2,1,0:T(8,128)(2,1)}), bf16[256,16,512]{2,1,0:T(8,128)(2,1)}) %all-gather.3.cloned.1.call-update) | async-done | bytes 4194320 | tf_op jit(solution)/shard_map/all_gather | solution.py:179
  269.5 5.0 %convolution_bitcast_fusion.1 = f32[1024,352]{0,1:T(8,128)} fusion(bf16[4,1024,512]{2,1,0:T(8,128)(2,1)} %bitcast.170, bf16[4,512,352]{1,0,2:T(4,128)(2,1)S(1)} %copy-done.3), kind=kOutput, calls=%fused_computation.20 | convolution fusion | flops 1476395008 | bytes 7077888 | tf_op jit(solution)/shard_map/qnd,qdh->nh/dot_general | solution.py:181
  274.5 9.4 %convert_bitcast_fusion = bf16[4,1024,512]{2,1,0:T(8,128)(2,1)} fusion(bf16[352,4,512]{2,1,0:T(4,128)(2,1)} %reshape_squeeze.11, bf16[4,1024,512]{2,1,0:T(8,128)(2,1)} %bitcast.171, bf16[4,512,352]{1,0,2:T(4,128)(2,1)} %reshape_squeeze.10, f32[1024,352]{0,1:T(8,128)} %convolution_bitcast_fusion.1), kind=kOutput, calls=%fused_computation.9 | convolution fusion | flops 2957049856 | bytes 12713984 | tf_op jit(solution)/shard_map/nh,hqd->qnd/dot_general | solution.py:194
  284.0 55.7 %reduce-scatter.5.cloned.1.call-done = bf16[1,1024,512]{2,1,0:T(8,128)(2,1)} async-done(((bf16[4,1024,512]{2,1,0:T(8,128)(2,1)}), bf16[1,1024,512]{2,1,0:T(8,128)(2,1)}) %reduce-scatter.5.cloned.1.call-update) | async-done | bytes 1048592 | tf_op jit(solution)/shard_map/reduce_scatter | solution.py:200
  339.7 10.4 %all-to-all-start.3 = ((bf16[64,16,512]{2,1,0:T(8,128)(2,1)}), bf16[64,16,512]{2,1,0:T(8,128)(2,1)S(1)}, u32[]{:S(2)}, u32[]{:S(2)}) async-start(bf16[64,16,512]{2,1,0:T(8,128)(2,1)} %bitcast.163), calls=%async_computation.5 | async-start | bytes 2097152 | tf_op jit(solution)/shard_map/all_to_all | solution.py:203
  350.1 0.1 mul.207
  350.2 0.1 copy.78
  350.4 26.4 %all-to-all-done.3 = bf16[64,16,512]{2,1,0:T(8,128)(2,1)S(1)} async-done(((bf16[64,16,512]{2,1,0:T(8,128)(2,1)}), bf16[64,16,512]{2,1,0:T(8,128)(2,1)S(1)}, u32[]{:S(2)}, u32[]{:S(2)}) %all-to-all-start.3) | async-done | bytes 1048608 | tf_op jit(solution)/shard_map/all_to_all | solution.py:203
  376.8 3.3 gather_fusion.2
  380.1 2.5 reshape.645
  382.6 2.3 multiply_reduce_fusion
  385.0 11.1 %all_gather.11 = bf16[128,2048]{1,0:T(8,128)(2,1)S(1)} all-gather(bf16[128,512]{1,0:T(8,128)(2,1)S(1)} %fusion.39), channel_id=1, replica_groups=mesh['req'=64,'tp'=4] {'tp'}, dimensions={1}, use_global_device_ids=true | all-gather | bytes 655360 | tf_op jit(solution)/shard_map/all_gather | solution.py:207
  396.1 0.8 copy.121
  (47 shorter events, 0.5 us)
Async XLA Ops:
  6.5 37.0 %copy-start = (bf16[2048,512]{1,0:T(8,128)(2,1)S(1)}, bf16[2048,512]{1,0:T(8,128)(2,1)}, u32[]{:S(2)}) copy-start(bf16[2048,512]{1,0:T(8,128)(2,1)} %param.16) | copy-start | bytes 6291460
  36.2 6.5 %copy-start.8 = (s32[1,128]{1,0:T(1,128)S(1)}, s32[1,128]{1,0:T(1,128)}, u32[]{:S(2)}) copy-start(s32[1,128]{1,0:T(1,128)} %param.22) | copy-start | bytes 1540
  36.2 7.1 %copy-start.1 = (bf16[128,2048]{1,0:T(8,128)(2,1)S(1)}, bf16[128,2048]{1,0:T(8,128)(2,1)}, u32[]{:S(2)}) copy-start(bf16[128,2048]{1,0:T(8,128)(2,1)} %param.14) | copy-start | bytes 1572868
  36.2 7.3 %copy-start.7 = (f32[2048]{0:T(1024)S(1)}, f32[2048]{0:T(1024)}, u32[]{:S(2)}) copy-start(f32[2048]{0:T(1024)} %param.15) | copy-start | bytes 24580
  36.2 97.1 %all-to-all-start.1 = ((bf16[64,1,1,128,256]{4,3,2,1,0:T(8,128)(2,1)}), bf16[64,1,1,128,256]{4,3,2,1,0:T(8,128)(2,1)}, u32[]{:S(2)}, u32[]{:S(2)}) async-start(bf16[64,1,1,128,256]{4,3,2,1,0:T(8,128)(2,1)} %bitcast.158), calls=%async_computation.1 | async-start | bytes 8388608 | tf_op jit(solution)/shard_map/all_to_all | solution.py:118
  42.0 141.7 %reduce-scatter.3.cloned.1.call-start = ((), (), s32[]{:S(2)}) async-start(), calls=%async_computation.6 | async-start | bytes 1310720 | tf_op jit(solution)/shard_map/reduce_scatter | solution.py:155
  42.9 1.2 copy-start.11
  141.7 1.7 copy-start.2
  143.4 1.7 copy-start.9
  144.9 124.6 %all-gather.3.cloned.1.call-start = ((), (), s32[]{:S(2)}) async-start(), calls=%async_computation.8 | async-start | bytes 5242880 | tf_op jit(solution)/shard_map/all_gather | solution.py:179
  184.8 43.7 %copy-start.4 = (bf16[128,512]{1,0:T(8,128)(2,1)}, bf16[128,512]{1,0:T(8,128)(2,1)S(1)}, u32[]{:S(2)}) copy-start(bf16[128,512]{1,0:T(8,128)(2,1)S(1)} %get-tuple-element.6) | copy-start | bytes 393220
  228.5 111.2 %reduce-scatter.5.cloned.1.call-start = ((), (), s32[]{:S(2)}) async-start(), calls=%async_computation.7 | async-start | bytes 5242880 | tf_op jit(solution)/shard_map/reduce_scatter | solution.py:200
  238.1 31.5 %copy-start.3 = (bf16[4,512,352]{1,0,2:T(4,128)(2,1)S(1)}, bf16[4,512,352]{1,0,2:T(4,128)(2,1)}, u32[]{:S(2)}) copy-start(bf16[4,512,352]{1,0,2:T(4,128)(2,1)} %reshape_squeeze.9) | copy-start | bytes 4325380
  284.0 66.1 %copy-start.6 = (s32[128,6]{1,0:T(8,128)S(1)}, s32[128,6]{1,0:T(8,128)}, u32[]{:S(2)}) copy-start(s32[128,6]{1,0:T(8,128)} %get-tuple-element.19) | copy-start | bytes 9220
  284.0 66.2 %copy-start.10 = (f32[128,6]{0,1:T(8,128)S(1)}, f32[128,6]{0,1:T(8,128)}, u32[]{:S(2)}) copy-start(f32[128,6]{0,1:T(8,128)} %param.27) | copy-start | bytes 9220
  339.7 37.1 %all-to-all-start.3 = ((bf16[64,16,512]{2,1,0:T(8,128)(2,1)}), bf16[64,16,512]{2,1,0:T(8,128)(2,1)S(1)}, u32[]{:S(2)}, u32[]{:S(2)}) async-start(bf16[64,16,512]{2,1,0:T(8,128)(2,1)} %bitcast.163), calls=%async_computation.5 | async-start | bytes 2097152 | tf_op jit(solution)/shard_map/all_to_all | solution.py:203
  380.1 4.8 %copy-start.5 = (bf16[128,512]{1,0:T(8,128)(2,1)S(1)}, bf16[128,512]{1,0:T(8,128)(2,1)}, u32[]{:S(2)}) copy-start(bf16[128,512]{1,0:T(8,128)(2,1)} %copy-done.4) | copy-start | bytes 393220
Sparse Core Ops, SparseCore 0:
  145.1 38.5 reduce-scatter.2
  228.6 40.8 all-gather.2
  284.1 55.5 reduce-scatter.4

commit v3 on v2

--- a/solution.py
+++ b/solution.py
@@ -66,6 +66,28 @@
     weights = (expo / totals).astype(jnp.bfloat16)
     context = jnp.einsum("kgtn,knd->tkgd", weights, all_values, preferred_element_type=jnp.float32)
     return context.astype(jnp.bfloat16)
+
+
+ON_CHIP = ((0, 1), (1, 0), (2, 3), (3, 2))
+CROSS_CHIP = ((0, 2), (2, 0), (1, 3), (3, 1))
+
+
+def tp_reduce_scatter(parts, wire_dtype):
+    tp_me = lax.axis_index("tp")
+    core, half = tp_me % 2, tp_me // 2
+    grid = parts.reshape((2, 2) + parts.shape[1:])
+    keep = lax.dynamic_index_in_dim(grid, core, axis=1, keepdims=False)
+    send = lax.dynamic_index_in_dim(grid, 1 - core, axis=1, keepdims=False)
+    got = lax.ppermute(send, "tp", ON_CHIP)
+    summed = keep.astype(jnp.float32) + got.astype(jnp.float32)
+    mine = lax.dynamic_index_in_dim(summed, half, axis=0, keepdims=False)
+    other = lax.dynamic_index_in_dim(summed, 1 - half, axis=0, keepdims=False)
+    return mine + lax.ppermute(other.astype(wire_dtype), "tp", CROSS_CHIP).astype(jnp.float32)
+
+
+def tp_sum(value):
+    value = value + lax.ppermute(value, "tp", ON_CHIP)
+    return value + lax.ppermute(value, "tp", CROSS_CHIP)
 
 
 def shards(
@@ -152,11 +174,11 @@
         w_out.reshape(-1, n_tp, quarter),
         preferred_element_type=jnp.float32,
     )
-    attn_q = lax.psum_scatter(attn_part, "tp", scatter_dimension=0, tiled=True)[0]
+    attn_q = tp_reduce_scatter(attn_part, jnp.float32)
     hidden_q = lax.dynamic_slice_in_dim(hidden_in, tp_me * quarter, quarter, axis=1)
     resid_q = (hidden_q.astype(jnp.float32) + attn_q).astype(jnp.bfloat16)
     resid_wide = resid_q.astype(jnp.float32)
-    sq_sum = lax.psum(jnp.sum(resid_wide * resid_wide, axis=-1, keepdims=True), "tp")
+    sq_sum = tp_sum(jnp.sum(resid_wide * resid_wide, axis=-1, keepdims=True))
     gain_q = lax.dynamic_slice_in_dim(moe_gain, tp_me * quarter, quarter, axis=0)
     moe_in = (resid_wide * lax.rsqrt(sq_sum / model_width + eps) * gain_q).astype(jnp.bfloat16)
     topk = expert_ids.shape[1]
@@ -176,20 +198,16 @@
         .reshape(n_exp, cap_e, quarter)
     )
     expert_q = lax.all_to_all(outgoing, "req", split_axis=0, concat_axis=0, tiled=True)
-    expert_in = lax.all_gather(expert_q, "tp", axis=0, tiled=False).reshape(n_tp, -1, quarter)
+    cross_q = lax.ppermute(expert_q, "tp", CROSS_CHIP)
+    chip_pair = jnp.stack([expert_q, cross_q])
+    partner_pair = lax.ppermute(chip_pair, "tp", ON_CHIP)
+    expert_in = jnp.concatenate([chip_pair, partner_pair]).reshape(n_tp, -1, quarter)
+    quarter_order = jnp.stack([tp_me, tp_me ^ 2, tp_me ^ 1, tp_me ^ 3])
     hidden_units = w_gate_up.shape[3]
-    gate_part = jnp.einsum(
-        "qnd,qdh->nh",
-        expert_in,
-        w_gate_up[0, 0].reshape(n_tp, quarter, hidden_units),
-        preferred_element_type=jnp.float32,
-    )
-    up_part = jnp.einsum(
-        "qnd,qdh->nh",
-        expert_in,
-        w_gate_up[0, 1].reshape(n_tp, quarter, hidden_units),
-        preferred_element_type=jnp.float32,
-    )
+    gate_w = w_gate_up[0, 0].reshape(n_tp, quarter, hidden_units)[quarter_order]
+    up_w = w_gate_up[0, 1].reshape(n_tp, quarter, hidden_units)[quarter_order]
+    gate_part = jnp.einsum("qnd,qdh->nh", expert_in, gate_w, preferred_element_type=jnp.float32)
+    up_part = jnp.einsum("qnd,qdh->nh", expert_in, up_w, preferred_element_type=jnp.float32)
     hidden_act = (jax.nn.silu(gate_part) * up_part).astype(jnp.bfloat16)
     partial = jnp.einsum(
         "nh,hqd->qnd",
@@ -197,8 +215,8 @@
         w_down[0].reshape(hidden_units, n_tp, quarter),
         preferred_element_type=jnp.float32,
     ).astype(jnp.bfloat16)
-    expert_share = lax.psum_scatter(partial, "tp", scatter_dimension=0, tiled=True).reshape(
-        n_req, cap_e, quarter
+    expert_share = (
+        tp_reduce_scatter(partial, jnp.bfloat16).astype(jnp.bfloat16).reshape(n_req, cap_e, quarter)
     )
     results = lax.all_to_all(expert_share, "req", split_axis=0, concat_axis=0, tiled=True)
     picked = results.reshape(-1, quarter)[assign_slot].reshape(tok_rows, topk, quarter)

time: 404 us -> 334 us (0.83)
  waiting for transfers between devices: 227 us -> 163 us
  starting transfers between devices: 16.5 us -> 36.4 us
  between operations: 14.1 us -> 1.23 us
  blocking collectives: 76.8 us -> 66 us
  matrix products: 21.6 us -> 15.3 us
    reduce_scatter x2 -> x0, waiting for transfers between devices: 89.4 us -> none  [the longest x1 55.7 us: shards(): lax.psum_scatter(partial, 'tp', scatter_dimension=0, tiled=True)]
    ppermute x0 -> x8, waiting for transfers between devices: none -> 52.7 us  [the longest x2 27.5 us: tp_reduce_scatter(): lax.ppermute(other.astype(wire_dtype), 'tp', CROSS_CHIP).astype(jnp.float32)]
    all_gather x1 -> x0, waiting for transfers between devices: 26.9 us -> none  [shards(): lax.all_gather(expert_q, 'tp', axis=0, tiled=False)]
    ppermute x0 -> x8, starting transfers between devices: none -> 22.5 us  [the longest x2 5.62 us: tp_reduce_scatter(): got = lax.ppermute(send, 'tp', ON_CHIP)]
    psum x1 -> x0, blocking collectives: 7.37 us -> none  [shards(): lax.psum(jnp.sum(resid_wide * resid_wide, axis=-1, keepdims=True), 'tp')]
    dot_general x1, matrix products: 9.44 us -> 2.54 us  [shards(): jnp.einsum('nh,hqd->qnd', hidden_act, w_down[0].reshape(hidden_units, n_t...]
    all_to_all x1, blocking collectives: 35.7 us -> 31.4 us  [shards(): lax.all_to_all(outgoing, 'req', split_axis=0, concat_axis=0, tiled=True)]
  transfers between devices with their start and end apart: 5 -> 10, of which waited for: 5 -> 8; matrix products, arithmetic and copies ran while one was open for 6% -> 9% of each run, Pallas kernels for 0% -> 0%
where the time goes in v3:
time: 334 us; the launch traced here: 333 us
  waiting for transfers between devices  163 us (49%)
  blocking collectives  66 us (20%)
  starting transfers between devices  36.4 us (11%)
  local copies, waits for them, and re-layouts  33.6 us (10%)
  other arithmetic  17.2 us (5%)
  matrix products  15.3 us (5%)
    all_to_all x1, waiting for transfers between devices, shards(): lax.all_to_all(served, 'req', split_axis=0, concat_axis=0, tiled=True)  84.3 us
    all_to_all x1, blocking collectives, shards(): lax.all_to_all(outgoing, 'req', split_axis=0, concat_axis=0, tiled=True)  31.4 us
    ppermute x2, waiting for transfers between devices, tp_reduce_scatter(): lax.ppermute(other.astype(wire_dtype), 'tp', CROSS_CHIP).astype(jnp.float32)  27.5 us
    all_to_all x1, waiting for transfers between devices, shards(): lax.all_to_all(expert_share, 'req', split_axis=0, concat_axis=0, tiled=True)  26.1 us
    all_to_all x1, blocking collectives, shards(): lax.all_to_all(request, 'req', split_axis=0, concat_axis=0, tiled=True)  22.6 us
    ppermute x1, waiting for transfers between devices, shards(): cross_q = lax.ppermute(expert_q, 'tp', CROSS_CHIP)  19.7 us
    all_gather x1, blocking collectives, shards(): return lax.all_gather(layer_q, 'tp', axis=1, tiled=True)  12 us
    all_to_all x1, starting transfers between devices, shards(): lax.all_to_all(expert_share, 'req', split_axis=0, concat_axis=0, tiled=True)  8.07 us
  transfers between devices with their start and end apart: 10, of which 8 were waited for; matrix products, arithmetic and copies ran while one was open for 9% of the time, Pallas kernels for 0%

profile of v3, /device:TPU:1, one launch (start us, length us, event | category | flops | bytes accessed | tf_op | source)
XLA Modules:
  0.0 332.9 jit_solution(2755132936718643748)
XLA Ops:
  0.0 0.8 and_select_fusion.3
  0.8 0.7 fusion.64
  1.5 0.2 convert_reduce_fusion
  1.9 22.6 %all_to_all.27 = s32[64,1,1]{2,1,0:T(1,128)S(1)} all-to-all(s32[64,1,1]{2,1,0:T(1,128)S(1)} %copy.85), channel_id=1, replica_groups=mesh['req'=64,'tp'=4] {'req'}, dimensions={0} | all-to-all | bytes 512 | tf_op jit(solution)/shard_map/all_to_all | solution.py:136
  24.4 1.2 reduce.3
  25.7 4.0 %gather_fusion = bf16[64,128,256]{2,1,0:T(8,128)(2,1)} fusion(bf16[16,128,256]{2,1,0:T(8,128)(2,1)} %bitcast.180, s32[1024]{0:T(1024)S(1)} %pad_clamp_fusion.3), kind=kCustom, calls=%fused_computation | custom fusion | bytes 8388864 | tf_op jit(solution)/shard_map/gather | solution.py:137
  29.7 5.8 %all-to-all-start.1 = ((bf16[64,1,1,128,256]{4,3,2,1,0:T(8,128)(2,1)}), bf16[64,1,1,128,256]{4,3,2,1,0:T(8,128)(2,1)}, u32[]{:S(2)}, u32[]{:S(2)}) async-start(bf16[64,1,1,128,256]{4,3,2,1,0:T(8,128)(2,1)} %bitcast.179), calls=%async_computation.1 | async-start | bytes 8388608 | tf_op jit(solution)/shard_map/all_to_all | solution.py:140
  36.4 0.2 reduce-window.18
  36.7 0.2 fusion.22
  36.9 0.5 fusion.37
  37.6 1.6 convolution_bitcast_fusion
  39.4 0.3 multiply_cosine_fusion
  39.7 0.3 fusion.57
  40.0 0.2 fusion.74
  40.3 2.1 broadcast_and_fusion
  42.5 84.3 %all-to-all-done.1 = bf16[64,1,1,128,256]{4,3,2,1,0:T(8,128)(2,1)} async-done(((bf16[64,1,1,128,256]{4,3,2,1,0:T(8,128)(2,1)}), bf16[64,1,1,128,256]{4,3,2,1,0:T(8,128)(2,1)}, u32[]{:S(2)}, u32[]{:S(2)}) %all-to-all-start.1) | async-done | bytes 4194336 | tf_op jit(solution)/shard_map/all_to_all | solution.py:140
  126.8 2.9 gather_fusion.1
  129.8 1.4 fusion.75
  131.2 1.1 fusion
  132.3 1.7 fusion.13
  134.1 0.5 fusion.4
  134.6 5.5 %collective-permute-start = (f32[2,128,512]{2,1,0:T(8,128)S(1)}, f32[2,128,512]{2,1,0:T(8,128)S(1)}, u32[]{:S(2)}, u32[]{:S(2)}) collective-permute-start(f32[2,128,512]{2,1,0:T(8,128)S(1)} %dynamic-slice_bitcast_fusion.1), channel_id=1, source_target_pairs={{0,1},{1,0},{2,3},{3,2},{4,5},{5,4},{6,7},{7,6},{8,9},{9,8},{10,11... | collective-permute-start | bytes 1572872 | tf_op jit(solution)/shard_map/ppermute | solution.py:81
  140.4 1.3 collective-permute-done
  141.8 2.9 collective-permute-start.1
  144.9 1.8 reduce-window.19
  146.7 0.3 slice_reduce_fusion
  147.2 3.8 %collective-permute-done.1 = f32[128,512]{1,0:T(8,128)S(1)} collective-permute-done((f32[128,512]{1,0:T(8,128)S(1)}, f32[128,512]{1,0:T(8,128)S(1)}, u32[]{:S(2)}, u32[]{:S(2)}) %collective-permute-start.1) | collective-permute-done | bytes 262176 | tf_op jit(solution)/shard_map/ppermute | solution.py:85
  151.2 1.3 collective-permute-start.2
  152.5 0.6 broadcast_multiply_fusion
  153.3 2.6 collective-permute-start.3
  156.0 0.5 fusion.3
  156.5 0.8 dynamic_slice.39
  157.3 0.5 convolution_convert_fusion.1
  157.8 31.4 %all_to_all.28 = bf16[64,16,512]{2,1,0:T(8,128)(2,1)S(1)} all-to-all(bf16[64,16,512]{2,1,0:T(8,128)(2,1)S(1)} %bitcast.184), channel_id=1, replica_groups=mesh['req'=64,'tp'=4] {'req'}, dimensions={0} | all-to-all | bytes 2097152 | tf_op jit(solution)/shard_map/all_to_all | solution.py:200
  189.2 2.6 collective-permute-start.4
  191.8 19.7 %collective-permute-done.4 = bf16[64,16,512]{2,1,0:T(8,128)(2,1)S(1)} collective-permute-done((bf16[64,16,512]{2,1,0:T(8,128)(2,1)S(1)}, bf16[64,16,512]{2,1,0:T(8,128)(2,1)S(1)}, u32[]{:S(2)}, u32[]{:S(2)}) %collective-permute-start.4) | collective-permute-done | bytes 1048608 | tf_op jit(solution)/shard_map/ppermute | solution.py:201
  211.5 1.6 pad_maximum_fusion.1
  213.2 4.9 %collective-permute-start.5 = (bf16[2,64,16,512]{3,2,1,0:T(8,128)(2,1)}, bf16[2,64,16,512]{3,2,1,0:T(8,128)(2,1)}, u32[]{:S(2)}, u32[]{:S(2)}) collective-permute-start(bf16[2,64,16,512]{3,2,1,0:T(8,128)(2,1)} %pad_maximum_fusion.1), channel_id=1, source_target_pairs={{0,1},{1,0},{2,3},{3,2},{4,5},{5,4},{6,7},{7,6},{8,9},{9,8},{10,11... | collective-permute-start | bytes 6291464 | tf_op jit(solution)/shard_map/ppermute | solution.py:203
  218.1 3.3 fusion.72
  221.4 1.1 reshape_squeeze.9
  222.5 0.3 copy.99
  222.8 4.4 %reshape_squeeze.10 = bf16[4,512,352]{1,0,2:T(4,128)(2,1)} reshape(bf16[1,1,2048,352]{2,3,1,0:T(8,128)(2,1)} %get-tuple-element.10) | data formatting | bytes 2883584 | tf_op jit(solution)/shard_map/reshape;squeeze | solution.py:208
  227.2 1.6 copy.100
  228.9 1.8 gather_fusion.2
  230.7 1.8 gather_fusion.3
  232.4 4.5 %reshape_squeeze.11 = bf16[352,4,512]{2,1,0:T(4,128)(2,1)} reshape(bf16[1,352,2048]{2,1,0:T(8,128)(2,1)} %param.21) | data formatting | bytes 2883584 | tf_op jit(solution)/shard_map/reshape;squeeze | solution.py:215
  237.0 3.3 fusion.10
  240.3 3.3 fusion.11
  243.6 2.5 convolution_convert_fusion
  246.2 0.1 dynamic-slice_bitcast_fusion
  246.4 4.1 %collective-permute-done.6 = bf16[2,1024,512]{2,1,0:T(8,128)(2,1)S(1)} collective-permute-done((bf16[2,1024,512]{2,1,0:T(8,128)(2,1)S(1)}, bf16[2,1024,512]{2,1,0:T(8,128)(2,1)S(1)}, u32[]{:S(2)}, u32[]{:S(2)}) %collective-permute-start.6) | collective-permute-done | bytes 2097184 | tf_op jit(solution)/shard_map/ppermute | solution.py:81
  250.6 0.7 convert_add_fusion
  251.2 0.1 fusion.25
  251.4 2.5 collective-permute-start.7
  253.9 23.6 %collective-permute-done.7 = bf16[1024,512]{1,0:T(8,128)(2,1)S(1)} collective-permute-done((bf16[1024,512]{1,0:T(8,128)(2,1)S(1)}, bf16[1024,512]{1,0:T(8,128)(2,1)S(1)}, u32[]{:S(2)}, u32[]{:S(2)}) %collective-permute-start.7) | collective-permute-done | bytes 1048608 | tf_op jit(solution)/shard_map/ppermute | solution.py:85
  277.6 1.3 fusion.7
  278.9 8.1 %all-to-all-start.3 = ((bf16[64,16,512]{2,1,0:T(8,128)(2,1)}), bf16[64,16,512]{2,1,0:T(8,128)(2,1)S(1)}, u32[]{:S(2)}, u32[]{:S(2)}) async-start(bf16[64,16,512]{2,1,0:T(8,128)(2,1)} %bitcast.62), calls=%async_computation.3 | async-start | bytes 2097152 | tf_op jit(solution)/shard_map/all_to_all | solution.py:221
  287.0 0.1 mul.207
  287.3 26.1 %all-to-all-done.3 = bf16[64,16,512]{2,1,0:T(8,128)(2,1)S(1)} async-done(((bf16[64,16,512]{2,1,0:T(8,128)(2,1)}), bf16[64,16,512]{2,1,0:T(8,128)(2,1)S(1)}, u32[]{:S(2)}, u32[]{:S(2)}) %all-to-all-start.3) | async-done | bytes 1048608 | tf_op jit(solution)/shard_map/all_to_all | solution.py:221
  313.4 2.7 gather_fusion.4
  316.1 1.5 reshape.820
  317.7 2.3 multiply_reduce_fusion
  320.0 12.0 %all_gather.3 = bf16[128,2048]{1,0:T(8,128)(2,1)S(1)} all-gather(bf16[128,512]{1,0:T(8,128)(2,1)S(1)} %fusion.31), channel_id=1, replica_groups=mesh['req'=64,'tp'=4] {'tp'}, dimensions={1}, use_global_device_ids=true | all-gather | bytes 655360 | tf_op jit(solution)/shard_map/all_gather | solution.py:225
  332.1 0.8 copy.124
  (83 shorter events, 2.7 us)
Async XLA Ops:
  0.0 36.9 %copy-start = (bf16[2048,512]{1,0:T(8,128)(2,1)S(1)}, bf16[2048,512]{1,0:T(8,128)(2,1)}, u32[]{:S(2)}) copy-start(bf16[2048,512]{1,0:T(8,128)(2,1)} %param.16) | copy-start | bytes 6291460
  29.7 6.5 %copy-start.15 = (s32[1,128]{1,0:T(1,128)S(1)}, s32[1,128]{1,0:T(1,128)}, u32[]{:S(2)}) copy-start(s32[1,128]{1,0:T(1,128)} %param.22) | copy-start | bytes 1540
  29.7 7.0 %copy-start.4 = (bf16[128,2048]{1,0:T(8,128)(2,1)S(1)}, bf16[128,2048]{1,0:T(8,128)(2,1)}, u32[]{:S(2)}) copy-start(bf16[128,2048]{1,0:T(8,128)(2,1)} %param.14) | copy-start | bytes 1572868
  29.7 7.2 %copy-start.14 = (f32[2048]{0:T(1024)S(1)}, f32[2048]{0:T(1024)}, u32[]{:S(2)}) copy-start(f32[2048]{0:T(1024)} %param.15) | copy-start | bytes 24580
  29.7 97.1 %all-to-all-start.1 = ((bf16[64,1,1,128,256]{4,3,2,1,0:T(8,128)(2,1)}), bf16[64,1,1,128,256]{4,3,2,1,0:T(8,128)(2,1)}, u32[]{:S(2)}, u32[]{:S(2)}) async-start(bf16[64,1,1,128,256]{4,3,2,1,0:T(8,128)(2,1)} %bitcast.179), calls=%async_computation.1 | async-start | bytes 8388608 | tf_op jit(solution)/shard_map/all_to_all | solution.py:140
  36.3 1.3 copy-start.18
  132.3 1.8 copy-start.5
  134.1 6.1 %copy-start.16 = (s32[128,6]{0,1:T(8,128)S(1)}, s32[128,6]{0,1:T(8,128)}, u32[]{:S(2)}) copy-start(s32[128,6]{0,1:T(8,128)} %param.26) | copy-start | bytes 9220
  134.6 7.1 %collective-permute-start = (f32[2,128,512]{2,1,0:T(8,128)S(1)}, f32[2,128,512]{2,1,0:T(8,128)S(1)}, u32[]{:S(2)}, u32[]{:S(2)}) collective-permute-start(f32[2,128,512]{2,1,0:T(8,128)S(1)} %dynamic-slice_bitcast_fusion.1), channel_id=1, source_target_pairs={{0,1},{1,0},{2,3},{3,2},{4,5},{5,4},{6,7},{7,6},{8,9},{9,8},{10,11... | collective-permute-start | bytes 1572872 | tf_op jit(solution)/shard_map/ppermute | solution.py:81
  141.8 9.3 %collective-permute-start.1 = (f32[128,512]{1,0:T(8,128)S(1)}, f32[128,512]{1,0:T(8,128)S(1)}, u32[]{:S(2)}, u32[]{:S(2)}) collective-permute-start(f32[128,512]{1,0:T(8,128)S(1)} %dynamic-slice_bitcast_fusion.2), channel_id=1, source_target_pairs={{0,2},{2,0},{1,3},{3,1},{4,6},{6,4},{5,7},{7,5},{8,10},{10,8},{9,1... | collective-permute-start | bytes 786440 | tf_op jit(solution)/shard_map/ppermute | solution.py:85
  151.2 6.6 %copy-start.9 = (bf16[128,512]{1,0:T(8,128)(2,1)}, bf16[128,512]{1,0:T(8,128)(2,1)S(1)}, u32[]{:S(2)}) copy-start(bf16[128,512]{1,0:T(8,128)(2,1)S(1)} %get-tuple-element.6) | copy-start | bytes 393220
  151.2 2.1 collective-permute-start.2
  153.3 3.9 %collective-permute-start.3 = (f32[128,1]{0,1:T(1,128)S(1)}, f32[128,1]{0,1:T(1,128)S(1)}, u32[]{:S(2)}, u32[]{:S(2)}) collective-permute-start(f32[128,1]{0,1:T(1,128)S(1)} %bitcast_add_fusion.4), channel_id=1, source_target_pairs={{0,2},{2,0},{1,3},{3,1},{4,6},{6,4},{5,7},{7,5},{8,10},{10,8},{9,1... | collective-permute-start | bytes 1544 | tf_op jit(solution)/shard_map/ppermute | solution.py:90
  189.2 23.9 %copy-start.2 = (bf16[64,16,512]{2,1,0:T(8,128)(2,1)}, bf16[64,16,512]{2,1,0:T(8,128)(2,1)S(1)}, u32[]{:S(2)}) copy-start(bf16[64,16,512]{2,1,0:T(8,128)(2,1)S(1)} %all_to_all.28) | copy-start | bytes 3145732
  189.2 22.3 %collective-permute-start.4 = (bf16[64,16,512]{2,1,0:T(8,128)(2,1)S(1)}, bf16[64,16,512]{2,1,0:T(8,128)(2,1)S(1)}, u32[]{:S(2)}, u32[]{:S(2)}) collective-permute-start(bf16[64,16,512]{2,1,0:T(8,128)(2,1)S(1)} %all_to_all.28), channel_id=1, source_target_pairs={{0,2},{2,0},{1,3},{3,1},{4,6},{6,4},{5,7},{7,5},{8,10},{10,8},{9,1... | collective-permute-start | bytes 3145736 | tf_op jit(solution)/shard_map/ppermute | solution.py:201
  211.5 1.6 copy-start.11
  213.2 23.8 %collective-permute-start.5 = (bf16[2,64,16,512]{3,2,1,0:T(8,128)(2,1)}, bf16[2,64,16,512]{3,2,1,0:T(8,128)(2,1)}, u32[]{:S(2)}, u32[]{:S(2)}) collective-permute-start(bf16[2,64,16,512]{3,2,1,0:T(8,128)(2,1)} %pad_maximum_fusion.1), channel_id=1, source_target_pairs={{0,1},{1,0},{2,3},{3,2},{4,5},{5,4},{6,7},{7,6},{8,9},{9,8},{10,11... | collective-permute-start | bytes 6291464 | tf_op jit(solution)/shard_map/ppermute | solution.py:203
  230.7 6.3 %copy-start.12 = (bf16[64,16,512]{2,1,0:T(8,128)(2,1)S(1)}, bf16[64,16,512]{2,1,0:T(8,128)(2,1)}, u32[]{:S(2)}) copy-start(bf16[64,16,512]{2,1,0:T(8,128)(2,1)} %copy-done.11) | copy-start | bytes 3145732
  232.4 4.5 %copy-start.3 = (bf16[64,16,512]{2,1,0:T(8,128)(2,1)S(1)}, bf16[64,16,512]{2,1,0:T(8,128)(2,1)}, u32[]{:S(2)}) copy-start(bf16[64,16,512]{2,1,0:T(8,128)(2,1)} %copy-done.2) | copy-start | bytes 3145732
  232.4 4.6 %copy-start.7 = (bf16[4,512,352]{1,2,0:T(8,128)(2,1)S(1)}, bf16[4,512,352]{1,2,0:T(8,128)(2,1)}, u32[]{:S(2)}) copy-start(bf16[4,512,352]{1,2,0:T(8,128)(2,1)} %gather_fusion.2) | copy-start | bytes 4325380
  237.0 3.3 copy-start.6
  240.3 3.3 copy-start.8
  246.3 4.2 %collective-permute-start.6 = (bf16[2,1024,512]{2,1,0:T(8,128)(2,1)S(1)}, bf16[2,1024,512]{2,1,0:T(8,128)(2,1)S(1)}, u32[]{:S(2)}, u32[]{:S(2)}) collective-permute-start(bf16[2,1024,512]{2,1,0:T(8,128)(2,1)S(1)} %dynamic-slice_bitcast_fusion), channel_id=1, source_target_pairs={{0,1},{1,0},{2,3},{3,2},{4,5},{5,4},{6,7},{7,6},{8,9},{9,8},{10,11... | collective-permute-start | bytes 6291464 | tf_op jit(solution)/shard_map/ppermute | solution.py:81
  251.4 26.2 %collective-permute-start.7 = (bf16[1024,512]{1,0:T(8,128)(2,1)S(1)}, bf16[1024,512]{1,0:T(8,128)(2,1)S(1)}, u32[]{:S(2)}, u32[]{:S(2)}) collective-permute-start(bf16[1024,512]{1,0:T(8,128)(2,1)S(1)} %fusion.25), channel_id=1, source_target_pairs={{0,2},{2,0},{1,3},{3,1},{4,6},{6,4},{5,7},{7,5},{8,10},{10,8},{9,1... | collective-permute-start | bytes 3145736 | tf_op jit(solution)/shard_map/ppermute | solution.py:85
  278.9 8.1 %copy-start.13 = (s32[128,6]{1,0:T(8,128)S(1)}, s32[128,6]{1,0:T(8,128)}, u32[]{:S(2)}) copy-start(s32[128,6]{1,0:T(8,128)} %get-tuple-element.19) | copy-start | bytes 9220
  278.9 8.2 %copy-start.17 = (f32[128,6]{0,1:T(8,128)S(1)}, f32[128,6]{0,1:T(8,128)}, u32[]{:S(2)}) copy-start(f32[128,6]{0,1:T(8,128)} %param.27) | copy-start | bytes 9220
  278.9 34.5 %all-to-all-start.3 = ((bf16[64,16,512]{2,1,0:T(8,128)(2,1)}), bf16[64,16,512]{2,1,0:T(8,128)(2,1)S(1)}, u32[]{:S(2)}, u32[]{:S(2)}) async-start(bf16[64,16,512]{2,1,0:T(8,128)(2,1)} %bitcast.62), calls=%async_computation.3 | async-start | bytes 2097152 | tf_op jit(solution)/shard_map/all_to_all | solution.py:221
  316.1 3.9 %copy-start.10 = (bf16[128,512]{1,0:T(8,128)(2,1)S(1)}, bf16[128,512]{1,0:T(8,128)(2,1)}, u32[]{:S(2)}) copy-start(bf16[128,512]{1,0:T(8,128)(2,1)} %copy-done.9) | copy-start | bytes 393220
  316.1 16.7 %copy-start.1 = (bf16[2048,512]{1,0:T(8,128)(2,1)S(1)}, bf16[2048,512]{1,0:T(8,128)(2,1)}, u32[]{:S(2)}) copy-start(bf16[2048,512]{1,0:T(8,128)(2,1)} %param.16) | copy-start | bytes 6291460

commit v4 on v3

--- a/solution.py
+++ b/solution.py
@@ -152,6 +152,15 @@
         .astype(jnp.bfloat16)
         .reshape(tok_rows, kv_local, group_size, head_dim)
     )
+    n_tp = lax.axis_size("tp")
+    tp_me = lax.axis_index("tp")
+    quarter = model_width // n_tp
+    quarter_order = jnp.stack([tp_me, tp_me ^ 2, tp_me ^ 1, tp_me ^ 3])
+    hidden_units = w_gate_up.shape[3]
+    gate_w = w_gate_up[0, 0].reshape(n_tp, quarter, hidden_units)[quarter_order]
+    up_w = w_gate_up[0, 1].reshape(n_tp, quarter, hidden_units)[quarter_order]
+    down_w = w_down[0].reshape(hidden_units, n_tp, quarter)
+    gate_w, up_w, down_w, queries = lax.optimization_barrier((gate_w, up_w, down_w, queries))
     keyval = jnp.dot(
         normed,
         w_keyval.reshape(model_width, kv_local * 2 * head_dim),
@@ -165,9 +174,6 @@
     )
     admitted = admit(segment_row, carried, cached, pref_pages * page_len)
     context = attend(queries, all_keys, all_values, admitted).reshape(tok_rows, q_local * head_dim)
-    n_tp = lax.axis_size("tp")
-    tp_me = lax.axis_index("tp")
-    quarter = model_width // n_tp
     attn_part = jnp.einsum(
         "tc,cqd->qtd",
         context,
@@ -202,17 +208,13 @@
     chip_pair = jnp.stack([expert_q, cross_q])
     partner_pair = lax.ppermute(chip_pair, "tp", ON_CHIP)
     expert_in = jnp.concatenate([chip_pair, partner_pair]).reshape(n_tp, -1, quarter)
-    quarter_order = jnp.stack([tp_me, tp_me ^ 2, tp_me ^ 1, tp_me ^ 3])
-    hidden_units = w_gate_up.shape[3]
-    gate_w = w_gate_up[0, 0].reshape(n_tp, quarter, hidden_units)[quarter_order]
-    up_w = w_gate_up[0, 1].reshape(n_tp, quarter, hidden_units)[quarter_order]
     gate_part = jnp.einsum("qnd,qdh->nh", expert_in, gate_w, preferred_element_type=jnp.float32)
     up_part = jnp.einsum("qnd,qdh->nh", expert_in, up_w, preferred_element_type=jnp.float32)
     hidden_act = (jax.nn.silu(gate_part) * up_part).astype(jnp.bfloat16)
     partial = jnp.einsum(
         "nh,hqd->qnd",
         hidden_act,
-        w_down[0].reshape(hidden_units, n_tp, quarter),
+        down_w,
         preferred_element_type=jnp.float32,
     ).astype(jnp.bfloat16)
     expert_share = (

time: 334 us -> 322 us (0.964)
  waiting for transfers between devices: 163 us -> 141 us
  local copies, waits for them, and re-layouts: 33.6 us -> 46.5 us
  matrix products: 15.3 us -> 11.3 us
    all_to_all x1, waiting for transfers between devices: 84.3 us -> 61.6 us  [shards(): lax.all_to_all(served, 'req', split_axis=0, concat_axis=0, tiled=True)]
    another operation x2, local copies, waits for them, and re-layouts: 1.38 us -> 7.13 us  [shards(): gate_w = w_gate_up[0, 0].reshape(n_tp, quarter, hidden_units)[quarter_order]]
    dynamic_slice x0 -> x2, local copies, waits for them, and re-layouts: none -> 5.72 us  [the longest x1 3.96 us: tp_reduce_scatter(): send = lax.dynamic_index_in_dim(grid, 1 - core, axis=1, keepdims=False)]
    ppermute x1, waiting for transfers between devices: 0.01 us -> 3.79 us  [shards(): partner_pair = lax.ppermute(chip_pair, 'tp', ON_CHIP)]
  transfers between devices with their start and end apart: 10 -> 10, of which waited for: 8 -> 9; matrix products, arithmetic and copies ran while one was open for 9% -> 11% of each run, Pallas kernels for 0% -> 0%
where the time goes in v4:
time: 322 us; the launch traced here: 321 us
  waiting for transfers between devices  141 us (44%)
  blocking collectives  66.4 us (21%)
  local copies, waits for them, and re-layouts  46.5 us (14%)
  starting transfers between devices  36.5 us (11%)
  other arithmetic  17.7 us (5%)
  matrix products  11.3 us (4%)
    all_to_all x1, waiting for transfers between devices, shards(): lax.all_to_all(served, 'req', split_axis=0, concat_axis=0, tiled=True)  61.6 us
    all_to_all x1, blocking collectives, shards(): lax.all_to_all(outgoing, 'req', split_axis=0, concat_axis=0, tiled=True)  31.4 us
    ppermute x2, waiting for transfers between devices, tp_reduce_scatter(): lax.ppermute(other.astype(wire_dtype), 'tp', CROSS_CHIP).astype(jnp.float32)  27.2 us
    all_to_all x1, waiting for transfers between devices, shards(): lax.all_to_all(expert_share, 'req', split_axis=0, concat_axis=0, tiled=True)  25.6 us
    all_to_all x1, blocking collectives, shards(): lax.all_to_all(request, 'req', split_axis=0, concat_axis=0, tiled=True)  22.6 us
    ppermute x1, waiting for transfers between devices, shards(): cross_q = lax.ppermute(expert_q, 'tp', CROSS_CHIP)  19.7 us
    all_gather x1, blocking collectives, shards(): return lax.all_gather(layer_q, 'tp', axis=1, tiled=True)  12.5 us
    all_to_all x1, starting transfers between devices, shards(): lax.all_to_all(expert_share, 'req', split_axis=0, concat_axis=0, tiled=True)  8.07 us
  transfers between devices with their start and end apart: 10, of which 9 were waited for; matrix products, arithmetic and copies ran while one was open for 11% of the time, Pallas kernels for 0%

profile of v4, /device:TPU:1, one launch (start us, length us, event | category | flops | bytes accessed | tf_op | source)
XLA Modules:
  0.0 321.0 jit_solution(15329428997846976949)
XLA Ops:
  0.0 0.8 and_select_fusion.3
  0.8 0.7 fusion.64
  1.9 22.6 %all_to_all.27 = s32[64,1,1]{2,1,0:T(1,128)S(1)} all-to-all(s32[64,1,1]{2,1,0:T(1,128)S(1)} %copy.94), channel_id=1, replica_groups=mesh['req'=64,'tp'=4] {'req'}, dimensions={0} | all-to-all | bytes 512 | tf_op jit(solution)/shard_map/all_to_all | solution.py:136
  24.4 1.2 reduce.3
  25.7 4.0 %gather_fusion = bf16[64,128,256]{2,1,0:T(8,128)(2,1)} fusion(bf16[16,128,256]{2,1,0:T(8,128)(2,1)} %bitcast.188, s32[1024]{0:T(1024)S(1)} %pad_clamp_fusion.3), kind=kCustom, calls=%fused_computation | custom fusion | bytes 8388864 | tf_op jit(solution)/shard_map/gather | solution.py:137
  29.7 5.7 %all-to-all-start.1 = ((bf16[64,1,1,128,256]{4,3,2,1,0:T(8,128)(2,1)}), bf16[64,1,1,128,256]{4,3,2,1,0:T(8,128)(2,1)}, u32[]{:S(2)}, u32[]{:S(2)}) async-start(bf16[64,1,1,128,256]{4,3,2,1,0:T(8,128)(2,1)} %bitcast.187), calls=%async_computation.1 | async-start | bytes 8388608 | tf_op jit(solution)/shard_map/all_to_all | solution.py:140
  35.4 3.3 %fusion.72 = (bf16[1,1,2048,352]{2,3,1,0:T(8,128)(2,1)S(1)}, bf16[1,1,2048,352]{2,3,1,0:T(8,128)(2,1)}) fusion(bf16[1,2,2048,352]{2,3,1,0:T(8,128)(2,1)} %param.20), kind=kLoop, calls=%fused_computation.153 | loop fusion | bytes 5767168 | tf_op jit(solution)/shard_map/slice | solution.py:161
  38.7 2.0 reshape_squeeze.10
  40.6 1.6 copy.97
  42.3 4.4 %reshape_squeeze.9 = bf16[4,512,352]{1,0,2:T(4,128)(2,1)} reshape(bf16[1,1,2048,352]{2,3,1,0:T(8,128)(2,1)} %get-tuple-element.20) | data formatting | bytes 2883584 | tf_op jit(solution)/shard_map/reshape;squeeze | solution.py:160
  46.7 2.7 copy.96
  49.5 1.8 gather_fusion.3
  51.3 3.2 gather_fusion.2
  55.7 0.2 fusion.22
  55.9 0.5 fusion.37
  56.6 4.5 %reshape_squeeze.11 = bf16[352,4,512]{2,1,0:T(4,128)(2,1)} reshape(bf16[1,352,2048]{2,1,0:T(8,128)(2,1)} %param.21) | data formatting | bytes 2883584 | tf_op jit(solution)/shard_map/reshape;squeeze | solution.py:162
  61.1 0.3 multiply_cosine_fusion
  61.4 0.2 fusion.74
  61.9 0.4 convolution_bitcast_fusion
  62.4 0.3 fusion.57
  62.7 2.3 broadcast_and_fusion
  65.1 61.6 %all-to-all-done.1 = bf16[64,1,1,128,256]{4,3,2,1,0:T(8,128)(2,1)} async-done(((bf16[64,1,1,128,256]{4,3,2,1,0:T(8,128)(2,1)}), bf16[64,1,1,128,256]{4,3,2,1,0:T(8,128)(2,1)}, u32[]{:S(2)}, u32[]{:S(2)}) %all-to-all-start.1) | async-done | bytes 4194336 | tf_op jit(solution)/shard_map/all_to_all | solution.py:140
  126.6 2.9 gather_fusion.1
  129.7 1.3 fusion.75
  130.9 1.1 fusion
  132.1 1.7 fusion.13
  133.9 0.5 fusion.4
  134.4 5.5 %collective-permute-start = (f32[2,128,512]{2,1,0:T(8,128)S(1)}, f32[2,128,512]{2,1,0:T(8,128)S(1)}, u32[]{:S(2)}, u32[]{:S(2)}) collective-permute-start(f32[2,128,512]{2,1,0:T(8,128)S(1)} %dynamic-slice_bitcast_fusion), channel_id=1, source_target_pairs={{0,1},{1,0},{2,3},{3,2},{4,5},{5,4},{6,7},{7,6},{8,9},{9,8},{10,11... | collective-permute-start | bytes 1572872 | tf_op jit(solution)/shard_map/ppermute | solution.py:81
  140.2 1.3 collective-permute-done
  141.6 2.7 collective-permute-start.1
  144.5 1.8 reduce-window.19
  146.3 0.3 slice_reduce_fusion
  146.9 3.8 %collective-permute-done.1 = f32[128,512]{1,0:T(8,128)S(1)} collective-permute-done((f32[128,512]{1,0:T(8,128)S(1)}, f32[128,512]{1,0:T(8,128)S(1)}, u32[]{:S(2)}, u32[]{:S(2)}) %collective-permute-start.1) | collective-permute-done | bytes 262176 | tf_op jit(solution)/shard_map/ppermute | solution.py:85
  150.8 1.3 collective-permute-start.2
  152.2 0.7 collective-permute-done.2
  152.9 2.6 collective-permute-start.3
  155.6 0.5 fusion.3
  156.1 0.8 dynamic_slice.39
  156.9 0.5 convolution_convert_fusion.1
  157.4 31.4 %all_to_all.28 = bf16[64,16,512]{2,1,0:T(8,128)(2,1)S(1)} all-to-all(bf16[64,16,512]{2,1,0:T(8,128)(2,1)S(1)} %bitcast.193), channel_id=1, replica_groups=mesh['req'=64,'tp'=4] {'req'}, dimensions={0} | all-to-all | bytes 2097152 | tf_op jit(solution)/shard_map/all_to_all | solution.py:206
  188.8 2.6 collective-permute-start.4
  191.4 19.7 %collective-permute-done.4 = bf16[64,16,512]{2,1,0:T(8,128)(2,1)S(1)} collective-permute-done((bf16[64,16,512]{2,1,0:T(8,128)(2,1)S(1)}, bf16[64,16,512]{2,1,0:T(8,128)(2,1)S(1)}, u32[]{:S(2)}, u32[]{:S(2)}) %collective-permute-start.4) | collective-permute-done | bytes 1048608 | tf_op jit(solution)/shard_map/ppermute | solution.py:207
  211.1 0.2 pad_maximum_fusion.1
  211.2 5.1 %collective-permute-start.5 = (bf16[2,64,16,512]{3,2,1,0:T(8,128)(2,1)S(1)}, bf16[2,64,16,512]{3,2,1,0:T(8,128)(2,1)S(1)}, u32[]{:S(2)}, u32[]{:S(2)}) collective-permute-start(bf16[2,64,16,512]{3,2,1,0:T(8,128)(2,1)S(1)} %pad_maximum_fusion.1), channel_id=1, source_target_pairs={{0,1},{1,0},{2,3},{3,2},{4,5},{5,4},{6,7},{7,6},{8,9},{9,8},{10,11... | collective-permute-start | bytes 6291464 | tf_op jit(solution)/shard_map/ppermute | solution.py:209
  216.3 3.8 %collective-permute-done.5 = bf16[2,64,16,512]{3,2,1,0:T(8,128)(2,1)S(1)} collective-permute-done((bf16[2,64,16,512]{3,2,1,0:T(8,128)(2,1)S(1)}, bf16[2,64,16,512]{3,2,1,0:T(8,128)(2,1)S(1)}, u32[]{:S(2)}, u32[]{:S(2)}) %collective-permute-start.5) | collective-permute-done | bytes 2097184 | tf_op jit(solution)/shard_map/ppermute | solution.py:209
  220.1 1.9 fusion.10
  222.1 2.0 fusion.11
  224.0 2.6 convolution_convert_fusion
  226.6 1.8 constant_dynamic-slice_fusion.1
  228.4 4.0 %copy.112 = bf16[2,1,1024,512]{3,2,0,1:T(8,128)(2,1)} copy(bf16[2,1,1024,512]{2,3,1,0:T(8,128)(2,1)} %get-tuple-element.18) | data formatting | bytes 4194304 | tf_op jit(solution)/shard_map/jit(dynamic_index_in_dim)/dynamic_slice | solution.py:80
  232.3 0.4 collective-permute-start.6
  232.7 2.6 copy.120
  235.3 1.6 collective-permute-done.6
  236.8 2.9 convert_add_fusion
  239.9 2.5 collective-permute-start.7
  242.4 23.4 %collective-permute-done.7 = bf16[1024,512]{1,0:T(8,128)(2,1)S(1)} collective-permute-done((bf16[1024,512]{1,0:T(8,128)(2,1)S(1)}, bf16[1024,512]{1,0:T(8,128)(2,1)S(1)}, u32[]{:S(2)}, u32[]{:S(2)}) %collective-permute-start.7) | collective-permute-done | bytes 1048608 | tf_op jit(solution)/shard_map/ppermute | solution.py:85
  265.8 1.3 fusion.7
  267.2 8.1 %all-to-all-start.3 = ((bf16[64,16,512]{2,1,0:T(8,128)(2,1)}), bf16[64,16,512]{2,1,0:T(8,128)(2,1)S(1)}, u32[]{:S(2)}, u32[]{:S(2)}) async-start(bf16[64,16,512]{2,1,0:T(8,128)(2,1)} %bitcast.65), calls=%async_computation.3 | async-start | bytes 2097152 | tf_op jit(solution)/shard_map/all_to_all | solution.py:223
  275.5 25.6 %all-to-all-done.3 = bf16[64,16,512]{2,1,0:T(8,128)(2,1)S(1)} async-done(((bf16[64,16,512]{2,1,0:T(8,128)(2,1)}), bf16[64,16,512]{2,1,0:T(8,128)(2,1)S(1)}, u32[]{:S(2)}, u32[]{:S(2)}) %all-to-all-start.3) | async-done | bytes 1048608 | tf_op jit(solution)/shard_map/all_to_all | solution.py:223
  301.1 2.7 gather_fusion.4
  303.8 1.5 reshape.848
  305.3 2.3 multiply_reduce_fusion
  307.7 12.5 %all_gather.3 = bf16[128,2048]{1,0:T(8,128)(2,1)S(1)} all-gather(bf16[128,512]{1,0:T(8,128)(2,1)S(1)} %fusion.31), channel_id=1, replica_groups=mesh['req'=64,'tp'=4] {'tp'}, dimensions={1}, use_global_device_ids=true | all-gather | bytes 655360 | tf_op jit(solution)/shard_map/all_gather | solution.py:227
  320.2 0.8 copy.144
  (74 shorter events, 3.3 us)
Async XLA Ops:
  0.0 55.9 %copy-start = (bf16[2048,512]{1,0:T(8,128)(2,1)S(1)}, bf16[2048,512]{1,0:T(8,128)(2,1)}, u32[]{:S(2)}) copy-start(bf16[2048,512]{1,0:T(8,128)(2,1)} %param.16) | copy-start | bytes 6291460
  29.7 96.9 %all-to-all-start.1 = ((bf16[64,1,1,128,256]{4,3,2,1,0:T(8,128)(2,1)}), bf16[64,1,1,128,256]{4,3,2,1,0:T(8,128)(2,1)}, u32[]{:S(2)}, u32[]{:S(2)}) async-start(bf16[64,1,1,128,256]{4,3,2,1,0:T(8,128)(2,1)} %bitcast.187), calls=%async_computation.1 | async-start | bytes 8388608 | tf_op jit(solution)/shard_map/all_to_all | solution.py:140
  51.3 3.8 %copy-start.8 = (s32[1,128]{1,0:T(1,128)S(1)}, s32[1,128]{1,0:T(1,128)}, u32[]{:S(2)}) copy-start(s32[1,128]{1,0:T(1,128)} %param.22) | copy-start | bytes 1540
  51.3 4.4 %copy-start.2 = (bf16[128,2048]{1,0:T(8,128)(2,1)S(1)}, bf16[128,2048]{1,0:T(8,128)(2,1)}, u32[]{:S(2)}) copy-start(bf16[128,2048]{1,0:T(8,128)(2,1)} %param.14) | copy-start | bytes 1572868
  51.3 4.6 %copy-start.7 = (f32[2048]{0:T(1024)S(1)}, f32[2048]{0:T(1024)}, u32[]{:S(2)}) copy-start(f32[2048]{0:T(1024)} %param.15) | copy-start | bytes 24580
  56.5 5.3 %copy-start.12 = (s32[1,32]{1,0:T(1,128)S(1)}, s32[1,32]{1,0:T(1,128)}, u32[]{:S(2)}) copy-start(s32[1,32]{1,0:T(1,128)} %param.24) | copy-start | bytes 388
  56.5 5.3 %copy-start.11 = (bf16[2048,1,256]{2,0,1:T(8,128)(2,1)S(1)}, bf16[2048,1,256]{2,0,1:T(8,128)(2,1)}, u32[]{:S(2)}) copy-start(bf16[2048,1,256]{2,0,1:T(8,128)(2,1)} %param.17) | copy-start | bytes 3145732
  132.1 1.8 copy-start.3
  133.9 6.1 %copy-start.9 = (s32[128,6]{0,1:T(8,128)S(1)}, s32[128,6]{0,1:T(8,128)}, u32[]{:S(2)}) copy-start(s32[128,6]{0,1:T(8,128)} %param.26) | copy-start | bytes 9220
  134.4 7.1 %collective-permute-start = (f32[2,128,512]{2,1,0:T(8,128)S(1)}, f32[2,128,512]{2,1,0:T(8,128)S(1)}, u32[]{:S(2)}, u32[]{:S(2)}) collective-permute-start(f32[2,128,512]{2,1,0:T(8,128)S(1)} %dynamic-slice_bitcast_fusion), channel_id=1, source_target_pairs={{0,1},{1,0},{2,3},{3,2},{4,5},{5,4},{6,7},{7,6},{8,9},{9,8},{10,11... | collective-permute-start | bytes 1572872 | tf_op jit(solution)/shard_map/ppermute | solution.py:81
  141.6 9.1 %collective-permute-start.1 = (f32[128,512]{1,0:T(8,128)S(1)}, f32[128,512]{1,0:T(8,128)S(1)}, u32[]{:S(2)}, u32[]{:S(2)}) collective-permute-start(f32[128,512]{1,0:T(8,128)S(1)} %dynamic-slice_bitcast_fusion.1), channel_id=1, source_target_pairs={{0,2},{2,0},{1,3},{3,1},{4,6},{6,4},{5,7},{7,5},{8,10},{10,8},{9,1... | collective-permute-start | bytes 786440 | tf_op jit(solution)/shard_map/ppermute | solution.py:85
  150.8 2.1 collective-permute-start.2
  152.9 3.9 %collective-permute-start.3 = (f32[128,1]{0,1:T(1,128)S(1)}, f32[128,1]{0,1:T(1,128)S(1)}, u32[]{:S(2)}, u32[]{:S(2)}) collective-permute-start(f32[128,1]{0,1:T(1,128)S(1)} %bitcast_add_fusion.4), channel_id=1, source_target_pairs={{0,2},{2,0},{1,3},{3,1},{4,6},{6,4},{5,7},{7,5},{8,10},{10,8},{9,1... | collective-permute-start | bytes 1544 | tf_op jit(solution)/shard_map/ppermute | solution.py:90
  188.8 22.3 %collective-permute-start.4 = (bf16[64,16,512]{2,1,0:T(8,128)(2,1)S(1)}, bf16[64,16,512]{2,1,0:T(8,128)(2,1)S(1)}, u32[]{:S(2)}, u32[]{:S(2)}) collective-permute-start(bf16[64,16,512]{2,1,0:T(8,128)(2,1)S(1)} %all_to_all.28), channel_id=1, source_target_pairs={{0,2},{2,0},{1,3},{3,1},{4,6},{6,4},{5,7},{7,5},{8,10},{10,8},{9,1... | collective-permute-start | bytes 3145736 | tf_op jit(solution)/shard_map/ppermute | solution.py:207
  211.1 9.0 %copy-start.5 = (bf16[4,512,352]{1,2,0:T(8,128)(2,1)S(1)}, bf16[4,512,352]{1,2,0:T(8,128)(2,1)}, u32[]{:S(2)}) copy-start(bf16[4,512,352]{1,2,0:T(8,128)(2,1)} %gather_fusion.2) | copy-start | bytes 4325380
  211.2 8.8 %collective-permute-start.5 = (bf16[2,64,16,512]{3,2,1,0:T(8,128)(2,1)S(1)}, bf16[2,64,16,512]{3,2,1,0:T(8,128)(2,1)S(1)}, u32[]{:S(2)}, u32[]{:S(2)}) collective-permute-start(bf16[2,64,16,512]{3,2,1,0:T(8,128)(2,1)S(1)} %pad_maximum_fusion.1), channel_id=1, source_target_pairs={{0,1},{1,0},{2,3},{3,2},{4,5},{5,4},{6,7},{7,6},{8,9},{9,8},{10,11... | collective-permute-start | bytes 6291464 | tf_op jit(solution)/shard_map/ppermute | solution.py:209
  220.1 2.0 copy-start.4
  222.1 2.0 copy-start.6
  232.3 4.5 %collective-permute-start.6 = (bf16[2,1024,512]{2,1,0:T(8,128)(2,1)}, bf16[2,1024,512]{2,1,0:T(8,128)(2,1)}, u32[]{:S(2)}, u32[]{:S(2)}) collective-permute-start(bf16[2,1024,512]{2,1,0:T(8,128)(2,1)} %bitcast.198), channel_id=1, source_target_pairs={{0,1},{1,0},{2,3},{3,2},{4,5},{5,4},{6,7},{7,6},{8,9},{9,8},{10,11... | collective-permute-start | bytes 6291464 | tf_op jit(solution)/shard_map/ppermute | solution.py:81
  239.9 25.9 %collective-permute-start.7 = (bf16[1024,512]{1,0:T(8,128)(2,1)S(1)}, bf16[1024,512]{1,0:T(8,128)(2,1)S(1)}, u32[]{:S(2)}, u32[]{:S(2)}) collective-permute-start(bf16[1024,512]{1,0:T(8,128)(2,1)S(1)} %fusion.25), channel_id=1, source_target_pairs={{0,2},{2,0},{1,3},{3,1},{4,6},{6,4},{5,7},{7,5},{8,10},{10,8},{9,1... | collective-permute-start | bytes 3145736 | tf_op jit(solution)/shard_map/ppermute | solution.py:85
  267.2 8.2 %copy-start.10 = (f32[128,6]{0,1:T(8,128)S(1)}, f32[128,6]{0,1:T(8,128)}, u32[]{:S(2)}) copy-start(f32[128,6]{0,1:T(8,128)} %param.27) | copy-start | bytes 9220
  267.2 33.9 %all-to-all-start.3 = ((bf16[64,16,512]{2,1,0:T(8,128)(2,1)}), bf16[64,16,512]{2,1,0:T(8,128)(2,1)S(1)}, u32[]{:S(2)}, u32[]{:S(2)}) async-start(bf16[64,16,512]{2,1,0:T(8,128)(2,1)} %bitcast.65), calls=%async_computation.3 | async-start | bytes 2097152 | tf_op jit(solution)/shard_map/all_to_all | solution.py:223
  303.8 17.2 %copy-start.1 = (bf16[2048,512]{1,0:T(8,128)(2,1)S(1)}, bf16[2048,512]{1,0:T(8,128)(2,1)}, u32[]{:S(2)}) copy-start(bf16[2048,512]{1,0:T(8,128)(2,1)} %param.16) | copy-start | bytes 6291460

commit v5 on v4

--- a/solution.py
+++ b/solution.py
@@ -73,21 +73,20 @@
 
 
 def tp_reduce_scatter(parts, wire_dtype):
-    tp_me = lax.axis_index("tp")
-    core, half = tp_me % 2, tp_me // 2
-    grid = parts.reshape((2, 2) + parts.shape[1:])
-    keep = lax.dynamic_index_in_dim(grid, core, axis=1, keepdims=False)
-    send = lax.dynamic_index_in_dim(grid, 1 - core, axis=1, keepdims=False)
-    got = lax.ppermute(send, "tp", ON_CHIP)
-    summed = keep.astype(jnp.float32) + got.astype(jnp.float32)
-    mine = lax.dynamic_index_in_dim(summed, half, axis=0, keepdims=False)
-    other = lax.dynamic_index_in_dim(summed, 1 - half, axis=0, keepdims=False)
-    return mine + lax.ppermute(other.astype(wire_dtype), "tp", CROSS_CHIP).astype(jnp.float32)
+    got = lax.ppermute(parts[:2], "tp", ON_CHIP)
+    summed = parts[2:].astype(jnp.float32) + got.astype(jnp.float32)
+    return summed[0] + lax.ppermute(summed[1].astype(wire_dtype), "tp", CROSS_CHIP).astype(
+        jnp.float32
+    )
+
+
+def tp_exchange(value):
+    return [lax.ppermute(value, "tp", tuple((t, t ^ flip) for t in range(4))) for flip in (1, 2, 3)]
 
 
 def tp_sum(value):
-    value = value + lax.ppermute(value, "tp", ON_CHIP)
-    return value + lax.ppermute(value, "tp", CROSS_CHIP)
+    near, across, diagonal = tp_exchange(value)
+    return (value + near) + (across + diagonal)
 
 
 def shards(
@@ -159,8 +158,12 @@
     hidden_units = w_gate_up.shape[3]
     gate_w = w_gate_up[0, 0].reshape(n_tp, quarter, hidden_units)[quarter_order]
     up_w = w_gate_up[0, 1].reshape(n_tp, quarter, hidden_units)[quarter_order]
-    down_w = w_down[0].reshape(hidden_units, n_tp, quarter)
-    gate_w, up_w, down_w, queries = lax.optimization_barrier((gate_w, up_w, down_w, queries))
+    scatter_order = jnp.stack([tp_me ^ 1, tp_me ^ 3, tp_me, tp_me ^ 2])
+    down_w = w_down[0].reshape(hidden_units, n_tp, quarter)[:, scatter_order]
+    out_w = w_out.reshape(-1, n_tp, quarter)[:, scatter_order]
+    gate_w, up_w, down_w, out_w, queries = lax.optimization_barrier(
+        (gate_w, up_w, down_w, out_w, queries)
+    )
     keyval = jnp.dot(
         normed,
         w_keyval.reshape(model_width, kv_local * 2 * head_dim),
@@ -177,7 +180,7 @@
     attn_part = jnp.einsum(
         "tc,cqd->qtd",
         context,
-        w_out.reshape(-1, n_tp, quarter),
+        out_w,
         preferred_element_type=jnp.float32,
     )
     attn_q = tp_reduce_scatter(attn_part, jnp.float32)

time: 322 us -> 322 us (level)
  starting transfers between devices: 36.5 us -> 32.9 us
    ppermute x6 -> x7, waiting for transfers between devices: 30.8 us -> 36.6 us  [the longest x2 30.2 us: tp_reduce_scatter(): lax.ppermute(summed[1].astype(wire_dtype), 'tp', CROSS_CHIP)]
    all_to_all x1, waiting for transfers between devices: 61.6 us -> 55.9 us  [shards(): lax.all_to_all(served, 'req', split_axis=0, concat_axis=0, tiled=True)]
    dynamic_slice x2 -> x1, local copies, waits for them, and re-layouts: 5.72 us -> 0.91 us  [shards(): lax.dynamic_slice_in_dim(hidden_in, tp_me * quarter, quarter, axis=1)]
    gather x0 -> x2, local copies, waits for them, and re-layouts: none -> 4.11 us  [the longest x1 2.27 us: shards(): out_w = w_out.reshape(-1, n_tp, quarter)[:, scatter_order]]
    ppermute x6 -> x7, starting transfers between devices: 15.1 us -> 14.1 us  [the longest x2 5.99 us: tp_reduce_scatter(): got = lax.ppermute(parts[:2], 'tp', ON_CHIP)]
  transfers between devices with their start and end apart: 10 -> 11, of which waited for: 9 -> 8; matrix products, arithmetic and copies ran while one was open for 11% -> 12% of each run, Pallas kernels for 0% -> 0%
where the time goes in v5:
time: 322 us; the launch traced here: 321 us
  waiting for transfers between devices  144 us (45%)
  blocking collectives  66.9 us (21%)
  local copies, waits for them, and re-layouts  48.1 us (15%)
  starting transfers between devices  32.9 us (10%)
  other arithmetic  16.5 us (5%)
  matrix products  11.5 us (4%)
    all_to_all x1, waiting for transfers between devices, shards(): lax.all_to_all(served, 'req', split_axis=0, concat_axis=0, tiled=True)  55.9 us
    all_to_all x1, blocking collectives, shards(): lax.all_to_all(outgoing, 'req', split_axis=0, concat_axis=0, tiled=True)  32.5 us
    ppermute x2, waiting for transfers between devices, tp_reduce_scatter(): lax.ppermute(summed[1].astype(wire_dtype), 'tp', CROSS_CHIP)  30.2 us
    all_to_all x1, waiting for transfers between devices, shards(): lax.all_to_all(expert_share, 'req', split_axis=0, concat_axis=0, tiled=True)  25.6 us
    all_to_all x1, blocking collectives, shards(): lax.all_to_all(request, 'req', split_axis=0, concat_axis=0, tiled=True)  22.6 us
    ppermute x1, waiting for transfers between devices, shards(): cross_q = lax.ppermute(expert_q, 'tp', CROSS_CHIP)  21.8 us
    all_gather x1, blocking collectives, shards(): return lax.all_gather(layer_q, 'tp', axis=1, tiled=True)  11.9 us
    all_to_all x1, starting transfers between devices, shards(): lax.all_to_all(expert_share, 'req', split_axis=0, concat_axis=0, tiled=True)  7.62 us
  transfers between devices with their start and end apart: 11, of which 8 were waited for; matrix products, arithmetic and copies ran while one was open for 12% of the time, Pallas kernels for 0%

profile of v5, /device:TPU:1, one launch (start us, length us, event | category | flops | bytes accessed | tf_op | source)
XLA Modules:
  0.0 320.8 jit_solution(6343040174411761128)
XLA Ops:
  0.0 0.8 and_select_fusion.3
  0.8 0.7 fusion.63
  2.3 22.6 %all_to_all.27 = s32[64,1,1]{2,1,0:T(1,128)S(1)} all-to-all(s32[64,1,1]{2,1,0:T(1,128)S(1)} %copy.114), channel_id=1, replica_groups=mesh['req'=64,'tp'=4] {'req'}, dimensions={0} | all-to-all | bytes 512 | tf_op jit(solution)/shard_map/all_to_all | solution.py:135
  24.8 1.2 reduce.4
  26.1 4.0 %gather_fusion.4 = bf16[64,128,256]{2,1,0:T(8,128)(2,1)} fusion(bf16[16,128,256]{2,1,0:T(8,128)(2,1)} %bitcast.185, s32[1024]{0:T(1024)S(1)} %pad_clamp_fusion.2), kind=kCustom, calls=%fused_computation.4 | custom fusion | bytes 8388864 | tf_op jit(solution)/shard_map/gather | solution.py:136
  30.1 5.8 %all-to-all-start.1 = ((bf16[64,1,1,128,256]{4,3,2,1,0:T(8,128)(2,1)}), bf16[64,1,1,128,256]{4,3,2,1,0:T(8,128)(2,1)}, u32[]{:S(2)}, u32[]{:S(2)}) async-start(bf16[64,1,1,128,256]{4,3,2,1,0:T(8,128)(2,1)} %bitcast.184), calls=%async_computation.1 | async-start | bytes 8388608 | tf_op jit(solution)/shard_map/all_to_all | solution.py:139
  37.0 0.7 reduce.3
  37.9 0.5 fusion.36
  38.4 0.8 reshape.983
  39.1 3.4 %fusion.71 = (bf16[1,1,2048,352]{2,3,1,0:T(8,128)(2,1)S(1)}, bf16[1,1,2048,352]{2,3,1,0:T(8,128)(2,1)}) fusion(bf16[1,2,2048,352]{2,3,1,0:T(8,128)(2,1)} %param.20), kind=kLoop, calls=%fused_computation.154 | loop fusion | bytes 5767168 | tf_op jit(solution)/shard_map/slice | solution.py:160
  42.5 1.1 reshape_squeeze.10
  43.9 4.4 %reshape_squeeze.9 = bf16[4,512,352]{1,0,2:T(4,128)(2,1)} reshape(bf16[1,1,2048,352]{2,3,1,0:T(8,128)(2,1)} %get-tuple-element.20) | data formatting | bytes 2883584 | tf_op jit(solution)/shard_map/reshape;squeeze | solution.py:159
  48.3 1.6 copy.106
  50.0 0.7 fusion.59
  50.6 1.8 gather_fusion.1
  52.4 1.8 gather_fusion
  54.2 2.9 copy.109
  57.1 2.4 copy.110
  59.5 1.1 reshape_squeeze.11
  61.3 2.3 gather_fusion.3
  63.6 1.8 gather_fusion.2
  65.4 0.8 add_convert_fusion.1
  66.5 1.2 fusion.73
  68.9 2.3 broadcast_and_fusion
  71.2 55.9 %all-to-all-done.1 = bf16[64,1,1,128,256]{4,3,2,1,0:T(8,128)(2,1)} async-done(((bf16[64,1,1,128,256]{4,3,2,1,0:T(8,128)(2,1)}), bf16[64,1,1,128,256]{4,3,2,1,0:T(8,128)(2,1)}, u32[]{:S(2)}, u32[]{:S(2)}) %all-to-all-start.1) | async-done | bytes 4194336 | tf_op jit(solution)/shard_map/all_to_all | solution.py:139
  127.2 4.2 %gather_fusion.5 = bf16[32,128,256]{2,1,0:T(8,128)(2,1)} fusion(bf16[64,128,256]{2,1,0:T(8,128)(2,1)} %bitcast.21, s32[1024]{0:T(1024)S(1)} %pad_clamp_fusion.1), kind=kCustom, calls=%fused_computation.5 | custom fusion | bytes 4194432 | tf_op jit(solution)/shard_map/gather | solution.py:140
  131.4 1.7 fusion.72
  133.0 1.3 fusion.74
  134.3 1.1 fusion
  135.5 1.7 fusion.10
  137.2 0.7 convolution_bitcast_fusion
  138.0 5.5 %collective-permute-start = (f32[2,128,512]{1,2,0:T(8,128)S(1)}, f32[2,128,512]{1,2,0:T(8,128)S(1)}, u32[]{:S(2)}, u32[]{:S(2)}) collective-permute-start(f32[2,128,512]{1,2,0:T(8,128)S(1)} %slice.118), channel_id=1, source_target_pairs={{0,1},{1,0},{2,3},{3,2},{4,5},{5,4},{6,7},{7,6},{8,9},{9,8},{10,11... | collective-permute-start | bytes 1572872 | tf_op jit(solution)/shard_map/ppermute | solution.py:76
  144.0 1.8 reduce-window.19
  146.3 2.7 collective-permute-start.1
  149.0 0.9 constant_dynamic-slice_fusion
  150.3 5.5 %collective-permute-done.1 = f32[128,512]{0,1:T(8,128)S(1)} collective-permute-done((f32[128,512]{0,1:T(8,128)S(1)}, f32[128,512]{0,1:T(8,128)S(1)}, u32[]{:S(2)}, u32[]{:S(2)}) %collective-permute-start.1) | collective-permute-done | bytes 262176 | tf_op jit(solution)/shard_map/ppermute | solution.py:78
  155.8 1.0 collective-permute-start.2
  156.8 2.6 collective-permute-start.3
  159.4 0.6 collective-permute-start.4
  160.0 0.5 fusion.3
  160.5 0.8 dynamic_slice.7
  161.3 2.6 collective-permute-done.4
  163.9 0.6 convolution_convert_fusion
  164.5 32.5 %all_to_all.28 = bf16[64,16,512]{2,1,0:T(8,128)(2,1)S(1)} all-to-all(bf16[64,16,512]{2,1,0:T(8,128)(2,1)S(1)} %bitcast.189), channel_id=1, replica_groups=mesh['req'=64,'tp'=4] {'req'}, dimensions={0} | all-to-all | bytes 2097152 | tf_op jit(solution)/shard_map/all_to_all | solution.py:209
  196.9 1.1 collective-permute-start.5
  198.1 21.8 %collective-permute-done.5 = bf16[64,16,512]{2,1,0:T(8,128)(2,1)S(1)} collective-permute-done((bf16[64,16,512]{2,1,0:T(8,128)(2,1)S(1)}, bf16[64,16,512]{2,1,0:T(8,128)(2,1)S(1)}, u32[]{:S(2)}, u32[]{:S(2)}) %collective-permute-start.5) | collective-permute-done | bytes 1048608 | tf_op jit(solution)/shard_map/ppermute | solution.py:210
  220.0 4.3 %collective-permute-start.6 = (bf16[2,64,16,512]{3,2,1,0:T(8,128)(2,1)S(1)}, bf16[2,64,16,512]{3,2,1,0:T(8,128)(2,1)S(1)}, u32[]{:S(2)}, u32[]{:S(2)}) collective-permute-start(bf16[2,64,16,512]{3,2,1,0:T(8,128)(2,1)S(1)} %pad_maximum_fusion.1), channel_id=1, source_target_pairs={{0,1},{1,0},{2,3},{3,2},{4,5},{5,4},{6,7},{7,6},{8,9},{9,8},{10,11... | collective-permute-start | bytes 6291464 | tf_op jit(solution)/shard_map/ppermute | solution.py:212
  224.3 3.8 %collective-permute-done.6 = bf16[2,64,16,512]{3,2,1,0:T(8,128)(2,1)S(1)} collective-permute-done((bf16[2,64,16,512]{3,2,1,0:T(8,128)(2,1)S(1)}, bf16[2,64,16,512]{3,2,1,0:T(8,128)(2,1)S(1)}, u32[]{:S(2)}, u32[]{:S(2)}) %collective-permute-start.6) | collective-permute-done | bytes 2097184 | tf_op jit(solution)/shard_map/ppermute | solution.py:212
  228.1 1.9 fusion.8
  230.1 2.0 fusion.9
  232.0 2.5 convert_bitcast_fusion
  234.7 0.5 collective-permute-start.7
  235.2 3.8 %collective-permute-done.7 = bf16[2,1024,512]{1,2,0:T(8,128)(2,1)S(1)} collective-permute-done((bf16[2,1024,512]{1,2,0:T(8,128)(2,1)S(1)}, bf16[2,1024,512]{1,2,0:T(8,128)(2,1)S(1)}, u32[]{:S(2)}, u32[]{:S(2)}) %collective-permute-start.7) | collective-permute-done | bytes 2097184 | tf_op jit(solution)/shard_map/ppermute | solution.py:76
  239.0 0.9 convert_add_fusion
  240.0 1.2 collective-permute-start.8
  241.3 24.7 %collective-permute-done.8 = bf16[1024,512]{0,1:T(8,128)(2,1)S(1)} collective-permute-done((bf16[1024,512]{0,1:T(8,128)(2,1)S(1)}, bf16[1024,512]{0,1:T(8,128)(2,1)S(1)}, u32[]{:S(2)}, u32[]{:S(2)}) %collective-permute-start.8) | collective-permute-done | bytes 1048608 | tf_op jit(solution)/shard_map/ppermute | solution.py:78
  266.3 1.3 copy.125
  267.7 7.6 %all-to-all-start.3 = ((bf16[64,16,512]{2,1,0:T(8,128)(2,1)}), bf16[64,16,512]{2,1,0:T(8,128)(2,1)S(1)}, u32[]{:S(2)}, u32[]{:S(2)}) async-start(bf16[64,16,512]{2,1,0:T(8,128)(2,1)} %bitcast.61), calls=%async_computation.3 | async-start | bytes 2097152 | tf_op jit(solution)/shard_map/all_to_all | solution.py:226
  275.6 25.6 %all-to-all-done.3 = bf16[64,16,512]{2,1,0:T(8,128)(2,1)S(1)} async-done(((bf16[64,16,512]{2,1,0:T(8,128)(2,1)}), bf16[64,16,512]{2,1,0:T(8,128)(2,1)S(1)}, u32[]{:S(2)}, u32[]{:S(2)}) %all-to-all-start.3) | async-done | bytes 1048608 | tf_op jit(solution)/shard_map/all_to_all | solution.py:226
  301.2 2.7 gather_fusion.6
  303.9 1.5 reshape.998
  305.4 2.3 multiply_reduce_fusion
  307.9 11.9 %all_gather.3 = bf16[128,2048]{0,1:T(8,128)(2,1)S(1)} all-gather(bf16[128,512]{0,1:T(8,128)(2,1)S(1)} %fusion.28), channel_id=1, replica_groups=mesh['req'=64,'tp'=4] {'tp'}, dimensions={1}, use_global_device_ids=true | all-gather | bytes 655360 | tf_op jit(solution)/shard_map/all_gather | solution.py:230
  319.8 1.0 copy.127
  (95 shorter events, 6.4 us)
Async XLA Ops:
  0.0 37.8 %copy-start = (bf16[2048,512]{1,0:T(8,128)(2,1)S(1)}, bf16[2048,512]{1,0:T(8,128)(2,1)}, u32[]{:S(2)}) copy-start(bf16[2048,512]{1,0:T(8,128)(2,1)} %param.16) | copy-start | bytes 6291460
  1.7 0.5 copy-start.17
  30.1 6.5 %copy-start.9 = (s32[1,128]{1,0:T(1,128)S(1)}, s32[1,128]{1,0:T(1,128)}, u32[]{:S(2)}) copy-start(s32[1,128]{1,0:T(1,128)} %param.22) | copy-start | bytes 1540
  30.1 7.6 %copy-start.2 = (bf16[128,2048]{1,0:T(8,128)(2,1)S(1)}, bf16[128,2048]{1,0:T(8,128)(2,1)}, u32[]{:S(2)}) copy-start(bf16[128,2048]{1,0:T(8,128)(2,1)} %param.14) | copy-start | bytes 1572868
  30.1 7.8 %copy-start.8 = (f32[2048]{0:T(1024)S(1)}, f32[2048]{0:T(1024)}, u32[]{:S(2)}) copy-start(f32[2048]{0:T(1024)} %param.15) | copy-start | bytes 24580
  30.1 97.1 %all-to-all-start.1 = ((bf16[64,1,1,128,256]{4,3,2,1,0:T(8,128)(2,1)}), bf16[64,1,1,128,256]{4,3,2,1,0:T(8,128)(2,1)}, u32[]{:S(2)}, u32[]{:S(2)}) async-start(bf16[64,1,1,128,256]{4,3,2,1,0:T(8,128)(2,1)} %bitcast.184), calls=%async_computation.1 | async-start | bytes 8388608 | tf_op jit(solution)/shard_map/all_to_all | solution.py:139
  37.9 4.7 %copy-start.13 = (f32[128]{0:T(128)}, f32[128]{0:T(128)S(1)}, u32[]{:S(2)}) copy-start(f32[128]{0:T(128)S(1)} %add_rsqrt_fusion) | copy-start | bytes 1540
  57.0 2.4 copy-start.6
  60.6 0.7 copy-start.12
  65.4 2.6 copy-start.16
  65.4 2.6 copy-start.18
  65.4 2.6 copy-start.3
  65.4 2.6 copy-start.14
  65.4 2.6 copy-start.15
  137.2 6.3 %copy-start.10 = (s32[128,6]{0,1:T(8,128)S(1)}, s32[128,6]{0,1:T(8,128)}, u32[]{:S(2)}) copy-start(s32[128,6]{0,1:T(8,128)} %param.26) | copy-start | bytes 9220
  138.0 8.2 %collective-permute-start = (f32[2,128,512]{1,2,0:T(8,128)S(1)}, f32[2,128,512]{1,2,0:T(8,128)S(1)}, u32[]{:S(2)}, u32[]{:S(2)}) collective-permute-start(f32[2,128,512]{1,2,0:T(8,128)S(1)} %slice.118), channel_id=1, source_target_pairs={{0,1},{1,0},{2,3},{3,2},{4,5},{5,4},{6,7},{7,6},{8,9},{9,8},{10,11... | collective-permute-start | bytes 1572872 | tf_op jit(solution)/shard_map/ppermute | solution.py:76
  146.3 9.4 %collective-permute-start.1 = (f32[128,512]{0,1:T(8,128)S(1)}, f32[128,512]{0,1:T(8,128)S(1)}, u32[]{:S(2)}, u32[]{:S(2)}) collective-permute-start(f32[128,512]{0,1:T(8,128)S(1)} %slice_bitcast_fusion.1), channel_id=1, source_target_pairs={{0,2},{2,0},{1,3},{3,1},{4,6},{6,4},{5,7},{7,5},{8,10},{10,8},{9,1... | collective-permute-start | bytes 786440 | tf_op jit(solution)/shard_map/ppermute | solution.py:78
  155.8 5.5 %collective-permute-start.2 = (f32[128,1]{0,1:T(1,128)S(1)}, f32[128,1]{0,1:T(1,128)S(1)}, u32[]{:S(2)}, u32[]{:S(2)}) collective-permute-start(f32[128,1]{0,1:T(1,128)S(1)} %bitcast.202), channel_id=1, source_target_pairs={{0,1},{1,0},{2,3},{3,2},{4,5},{5,4},{6,7},{7,6},{8,9},{9,8},{10,11... | collective-permute-start | bytes 1544 | tf_op jit(solution)/shard_map/ppermute | solution.py:84
  156.8 4.5 %collective-permute-start.3 = (f32[128,1]{0,1:T(1,128)S(1)}, f32[128,1]{0,1:T(1,128)S(1)}, u32[]{:S(2)}, u32[]{:S(2)}) collective-permute-start(f32[128,1]{0,1:T(1,128)S(1)} %bitcast.203), channel_id=1, source_target_pairs={{0,2},{1,3},{2,0},{3,1},{4,6},{5,7},{6,4},{7,5},{8,10},{9,11},{10,... | collective-permute-start | bytes 1544 | tf_op jit(solution)/shard_map/ppermute | solution.py:84
  159.4 4.5 %collective-permute-start.4 = (f32[128,1]{0,1:T(1,128)S(1)}, f32[128,1]{0,1:T(1,128)S(1)}, u32[]{:S(2)}, u32[]{:S(2)}) collective-permute-start(f32[128,1]{0,1:T(1,128)S(1)} %bitcast.204), channel_id=1, source_target_pairs={{0,3},{1,2},{2,1},{3,0},{4,7},{5,6},{6,5},{7,4},{8,11},{9,10},{10,... | collective-permute-start | bytes 1544 | tf_op jit(solution)/shard_map/ppermute | solution.py:84
  196.9 22.9 %collective-permute-start.5 = (bf16[64,16,512]{2,1,0:T(8,128)(2,1)S(1)}, bf16[64,16,512]{2,1,0:T(8,128)(2,1)S(1)}, u32[]{:S(2)}, u32[]{:S(2)}) collective-permute-start(bf16[64,16,512]{2,1,0:T(8,128)(2,1)S(1)} %all_to_all.28), channel_id=1, source_target_pairs={{0,2},{2,0},{1,3},{3,1},{4,6},{6,4},{5,7},{7,5},{8,10},{10,8},{9,1... | collective-permute-start | bytes 3145736 | tf_op jit(solution)/shard_map/ppermute | solution.py:210
  219.8 8.2 %copy-start.5 = (bf16[4,512,352]{1,2,0:T(8,128)(2,1)S(1)}, bf16[4,512,352]{1,2,0:T(8,128)(2,1)}, u32[]{:S(2)}) copy-start(bf16[4,512,352]{1,2,0:T(8,128)(2,1)} %gather_fusion) | copy-start | bytes 4325380
  220.0 8.0 %collective-permute-start.6 = (bf16[2,64,16,512]{3,2,1,0:T(8,128)(2,1)S(1)}, bf16[2,64,16,512]{3,2,1,0:T(8,128)(2,1)S(1)}, u32[]{:S(2)}, u32[]{:S(2)}) collective-permute-start(bf16[2,64,16,512]{3,2,1,0:T(8,128)(2,1)S(1)} %pad_maximum_fusion.1), channel_id=1, source_target_pairs={{0,1},{1,0},{2,3},{3,2},{4,5},{5,4},{6,7},{7,6},{8,9},{9,8},{10,11... | collective-permute-start | bytes 6291464 | tf_op jit(solution)/shard_map/ppermute | solution.py:212
  228.1 2.0 copy-start.4
  230.0 2.0 copy-start.7
  234.7 4.2 %collective-permute-start.7 = (bf16[2,1024,512]{1,2,0:T(8,128)(2,1)S(1)}, bf16[2,1024,512]{1,2,0:T(8,128)(2,1)S(1)}, u32[]{:S(2)}, u32[]{:S(2)}) collective-permute-start(bf16[2,1024,512]{1,2,0:T(8,128)(2,1)S(1)} %slice.123), channel_id=1, source_target_pairs={{0,1},{1,0},{2,3},{3,2},{4,5},{5,4},{6,7},{7,6},{8,9},{9,8},{10,11... | collective-permute-start | bytes 6291464 | tf_op jit(solution)/shard_map/ppermute | solution.py:76
  240.0 25.9 %collective-permute-start.8 = (bf16[1024,512]{0,1:T(8,128)(2,1)S(1)}, bf16[1024,512]{0,1:T(8,128)(2,1)S(1)}, u32[]{:S(2)}, u32[]{:S(2)}) collective-permute-start(bf16[1024,512]{0,1:T(8,128)(2,1)S(1)} %fusion.22), channel_id=1, source_target_pairs={{0,2},{2,0},{1,3},{3,1},{4,6},{6,4},{5,7},{7,5},{8,10},{10,8},{9,1... | collective-permute-start | bytes 3145736 | tf_op jit(solution)/shard_map/ppermute | solution.py:78
  266.3 9.1 %copy-start.11 = (f32[128,6]{0,1:T(8,128)S(1)}, f32[128,6]{0,1:T(8,128)}, u32[]{:S(2)}) copy-start(f32[128,6]{0,1:T(8,128)} %param.27) | copy-start | bytes 9220
  267.7 33.5 %all-to-all-start.3 = ((bf16[64,16,512]{2,1,0:T(8,128)(2,1)}), bf16[64,16,512]{2,1,0:T(8,128)(2,1)S(1)}, u32[]{:S(2)}, u32[]{:S(2)}) async-start(bf16[64,16,512]{2,1,0:T(8,128)(2,1)} %bitcast.61), calls=%async_computation.3 | async-start | bytes 2097152 | tf_op jit(solution)/shard_map/all_to_all | solution.py:226
  303.8 17.0 %copy-start.1 = (bf16[2048,512]{1,0:T(8,128)(2,1)S(1)}, bf16[2048,512]{1,0:T(8,128)(2,1)}, u32[]{:S(2)}) copy-start(bf16[2048,512]{1,0:T(8,128)(2,1)} %param.16) | copy-start | bytes 6291460

commit v6 on v5

--- a/solution.py
+++ b/solution.py
@@ -154,12 +154,14 @@
     n_tp = lax.axis_size("tp")
     tp_me = lax.axis_index("tp")
     quarter = model_width // n_tp
-    quarter_order = jnp.stack([tp_me, tp_me ^ 2, tp_me ^ 1, tp_me ^ 3])
+    core = tp_me % 2
+    quarter_order = jnp.stack([core, core + 2, 1 - core, 3 - core])
     hidden_units = w_gate_up.shape[3]
     gate_w = w_gate_up[0, 0].reshape(n_tp, quarter, hidden_units)[quarter_order]
     up_w = w_gate_up[0, 1].reshape(n_tp, quarter, hidden_units)[quarter_order]
     scatter_order = jnp.stack([tp_me ^ 1, tp_me ^ 3, tp_me, tp_me ^ 2])
-    down_w = w_down[0].reshape(hidden_units, n_tp, quarter)[:, scatter_order]
+    plane_order = jnp.stack([1 - core, 3 - core, core, core + 2])
+    down_w = w_down[0].reshape(hidden_units, n_tp, quarter)[:, plane_order]
     out_w = w_out.reshape(-1, n_tp, quarter)[:, scatter_order]
     gate_w, up_w, down_w, out_w, queries = lax.optimization_barrier(
         (gate_w, up_w, down_w, out_w, queries)
@@ -206,9 +208,19 @@
         .astype(jnp.bfloat16)
         .reshape(n_exp, cap_e, quarter)
     )
-    expert_q = lax.all_to_all(outgoing, "req", split_axis=0, concat_axis=0, tiled=True)
-    cross_q = lax.ppermute(expert_q, "tp", CROSS_CHIP)
-    chip_pair = jnp.stack([expert_q, cross_q])
+    same_core = [
+        [r * n_tp + half * 2 + c for half in range(n_tp // 2) for r in range(n_req)]
+        for c in range(2)
+    ]
+    expert_q = lax.all_to_all(
+        jnp.concatenate([outgoing, outgoing]),
+        ("req", "tp"),
+        0,
+        0,
+        axis_index_groups=same_core,
+        tiled=True,
+    )
+    chip_pair = expert_q.reshape(2, n_req, cap_e, quarter)
     partner_pair = lax.ppermute(chip_pair, "tp", ON_CHIP)
     expert_in = jnp.concatenate([chip_pair, partner_pair]).reshape(n_tp, -1, quarter)
     gate_part = jnp.einsum("qnd,qdh->nh", expert_in, gate_w, preferred_element_type=jnp.float32)
@@ -220,10 +232,19 @@
         down_w,
         preferred_element_type=jnp.float32,
     ).astype(jnp.bfloat16)
-    expert_share = (
-        tp_reduce_scatter(partial, jnp.bfloat16).astype(jnp.bfloat16).reshape(n_req, cap_e, quarter)
-    )
-    results = lax.all_to_all(expert_share, "req", split_axis=0, concat_axis=0, tiled=True)
+    got = lax.ppermute(partial[:2], "tp", ON_CHIP)
+    chip_sum = (partial[2:].astype(jnp.float32) + got.astype(jnp.float32)).astype(jnp.bfloat16)
+    both_planes = lax.all_to_all(
+        chip_sum.reshape(2 * n_req, cap_e, quarter),
+        ("req", "tp"),
+        0,
+        0,
+        axis_index_groups=same_core,
+        tiled=True,
+    ).reshape(2, n_req, cap_e, quarter)
+    results = (both_planes[0].astype(jnp.float32) + both_planes[1].astype(jnp.float32)).astype(
+        jnp.bfloat16
+    )
     picked = results.reshape(-1, quarter)[assign_slot].reshape(tok_rows, topk, quarter)
     moe_q = jnp.sum(expert_weights[:, :, None] * picked.astype(jnp.float32), axis=1)
     layer_q = (resid_wide + moe_q).astype(jnp.bfloat16)

time: 322 us -> 334 us (1.037)
  waiting for transfers between devices: 144 us -> 110 us
  blocking collectives: 66.9 us -> 92.9 us
  local copies, waits for them, and re-layouts: 48.1 us -> 60.6 us
  matrix products: 11.5 us -> 17.3 us
  other arithmetic: 16.5 us -> 21.6 us
  starting transfers between devices: 32.9 us -> 28.5 us
    all_to_all x1, blocking collectives: 32.5 us -> 60.2 us  [shards(): lax.all_to_all(jnp.concatenate([outgoing, outgoing]), ('req', 'tp'), 0, 0...]
    all_to_all x1, waiting for transfers between devices: 25.6 us -> 52.3 us  [shards(): lax.all_to_all(chip_sum.reshape(2 * n_req, cap_e, quarter), ('req', 'tp')...]
    ppermute x2 -> x1, waiting for transfers between devices: 30.2 us -> 4.84 us  [tp_reduce_scatter(): lax.ppermute(summed[1].astype(wire_dtype), 'tp', CROSS_CHIP)]
    ppermute x1, waiting for transfers between devices: 21.8 us -> 3.79 us  [shards(): got = lax.ppermute(partial[:2], 'tp', ON_CHIP)]
    all_to_all x1, waiting for transfers between devices: 55.9 us -> 43.1 us  [shards(): lax.all_to_all(served, 'req', split_axis=0, concat_axis=0, tiled=True)]
    dot_general x1, matrix products: 2.48 us -> 7.52 us  [shards(): jnp.einsum('nh,hqd->qnd', hidden_act, down_w, preferred_element_type=jnp....]
    ppermute x2 -> x1, waiting for transfers between devices: 3.79 us -> 0.01 us  [tp_reduce_scatter(): got = lax.ppermute(parts[:2], 'tp', ON_CHIP)]
  transfers between devices with their start and end apart: 11 -> 9, of which waited for: 8 -> 6; matrix products, arithmetic and copies ran while one was open for 12% -> 16% of each run, Pallas kernels for 0% -> 0%
where the time goes in v6:
time: 334 us; the launch traced here: 332 us
  waiting for transfers between devices  110 us (33%)
  blocking collectives  92.9 us (28%)
  local copies, waits for them, and re-layouts  60.6 us (18%)
  starting transfers between devices  28.5 us (9%)
  other arithmetic  21.6 us (6%)
  matrix products  17.3 us (5%)
    all_to_all x1, blocking collectives, shards(): lax.all_to_all(jnp.concatenate([outgoing, outgoing]), ('req', 'tp'), 0, 0...  60.2 us
    all_to_all x1, waiting for transfers between devices, shards(): lax.all_to_all(chip_sum.reshape(2 * n_req, cap_e, quarter), ('req', 'tp')...  52.3 us
    all_to_all x1, waiting for transfers between devices, shards(): lax.all_to_all(served, 'req', split_axis=0, concat_axis=0, tiled=True)  43.1 us
    all_to_all x1, blocking collectives, shards(): lax.all_to_all(request, 'req', split_axis=0, concat_axis=0, tiled=True)  22.6 us
    all_gather x1, blocking collectives, shards(): return lax.all_gather(layer_q, 'tp', axis=1, tiled=True)  10.2 us
    dot_general x1, matrix products, shards(): jnp.einsum('nh,hqd->qnd', hidden_act, down_w, preferred_element_type=jnp....  7.52 us
    all_to_all x1, starting transfers between devices, shards(): lax.all_to_all(chip_sum.reshape(2 * n_req, cap_e, quarter), ('req', 'tp')...  7.47 us
    another operation x2, local copies, waits for them, and re-layouts, shards(): gate_w = w_gate_up[0, 0].reshape(n_tp, quarter, hidden_units)[quarter_order]  7.23 us
  transfers between devices with their start and end apart: 9, of which 6 were waited for; matrix products, arithmetic and copies ran while one was open for 16% of the time, Pallas kernels for 0%

profile of v6, /device:TPU:1, one launch (start us, length us, event | category | flops | bytes accessed | tf_op | source)
XLA Modules:
  0.0 332.4 jit_solution(6222199033004711944)
XLA Ops:
  0.0 0.8 and_select_fusion.3
  0.8 0.7 fusion.61
  2.3 22.6 %all_to_all.27 = s32[64,1,1]{2,1,0:T(1,128)S(1)} all-to-all(s32[64,1,1]{2,1,0:T(1,128)S(1)} %copy.113), channel_id=1, replica_groups=mesh['req'=64,'tp'=4] {'req'}, dimensions={0} | all-to-all | bytes 512 | tf_op jit(solution)/shard_map/all_to_all | solution.py:135
  24.9 1.2 reduce.4
  26.1 4.0 %gather_fusion.4 = bf16[64,128,256]{2,1,0:T(8,128)(2,1)} fusion(bf16[16,128,256]{2,1,0:T(8,128)(2,1)} %bitcast.185, s32[1024]{0:T(1024)S(1)} %pad_clamp_fusion.2), kind=kCustom, calls=%fused_computation.4 | custom fusion | bytes 8388864 | tf_op jit(solution)/shard_map/gather | solution.py:136
  30.1 5.7 %all-to-all-start.1 = ((bf16[64,1,1,128,256]{4,3,2,1,0:T(8,128)(2,1)}), bf16[64,1,1,128,256]{4,3,2,1,0:T(8,128)(2,1)}, u32[]{:S(2)}, u32[]{:S(2)}) async-start(bf16[64,1,1,128,256]{4,3,2,1,0:T(8,128)(2,1)} %bitcast.184), calls=%async_computation.1 | async-start | bytes 8388608 | tf_op jit(solution)/shard_map/all_to_all | solution.py:139
  35.8 3.3 fusion.70
  39.1 2.0 reshape_squeeze.10
  41.1 1.6 copy.106
  42.7 4.4 %reshape_squeeze.9 = bf16[4,512,352]{1,0,2:T(4,128)(2,1)} reshape(bf16[1,1,2048,352]{2,3,1,0:T(8,128)(2,1)} %get-tuple-element.20) | data formatting | bytes 2883584 | tf_op jit(solution)/shard_map/reshape;squeeze | solution.py:160
  47.1 2.8 copy.105
  49.9 0.7 fusion.56
  50.6 1.8 gather_fusion.1
  52.3 3.3 gather_fusion
  55.6 2.0 reshape_squeeze.11
  57.6 1.6 copy.107
  60.1 0.7 copy.111
  60.8 1.6 reduce-window.18
  62.4 0.9 reduce.3
  63.4 1.2 fusion.17
  65.2 2.2 fusion.33
  67.5 1.8 reshape.1153
  69.2 2.9 copy.108
  72.1 2.4 copy.109
  74.5 0.7 pad_clamp_fusion.4
  75.2 1.7 gather_fusion.2
  77.0 2.3 gather_fusion.3
  81.6 2.3 broadcast_and_fusion
  84.0 43.1 %all-to-all-done.1 = bf16[64,1,1,128,256]{4,3,2,1,0:T(8,128)(2,1)} async-done(((bf16[64,1,1,128,256]{4,3,2,1,0:T(8,128)(2,1)}), bf16[64,1,1,128,256]{4,3,2,1,0:T(8,128)(2,1)}, u32[]{:S(2)}, u32[]{:S(2)}) %all-to-all-start.1) | async-done | bytes 4194336 | tf_op jit(solution)/shard_map/all_to_all | solution.py:139
  127.1 4.2 %gather_fusion.5 = bf16[32,128,256]{2,1,0:T(8,128)(2,1)} fusion(bf16[64,128,256]{2,1,0:T(8,128)(2,1)} %bitcast.26, s32[1024]{0:T(1024)S(1)} %pad_clamp_fusion.1), kind=kCustom, calls=%fused_computation.5 | custom fusion | bytes 4194432 | tf_op jit(solution)/shard_map/gather | solution.py:140
  131.3 1.7 fusion.71
  133.0 1.3 fusion.73
  134.3 1.1 fusion
  135.4 1.7 fusion.8
  137.1 0.7 convolution_bitcast_fusion
  137.9 5.5 %collective-permute-start = (f32[2,128,512]{1,2,0:T(8,128)S(1)}, f32[2,128,512]{1,2,0:T(8,128)S(1)}, u32[]{:S(2)}, u32[]{:S(2)}) collective-permute-start(f32[2,128,512]{1,2,0:T(8,128)S(1)} %slice.119), channel_id=1, source_target_pairs={{0,1},{1,0},{2,3},{3,2},{4,5},{5,4},{6,7},{7,6},{8,9},{9,8},{10,11... | collective-permute-start | bytes 1572872 | tf_op jit(solution)/shard_map/ppermute | solution.py:76
  143.9 1.8 reduce-window.19
  146.2 2.7 collective-permute-start.1
  148.9 0.9 constant_dynamic-slice_fusion
  150.1 0.6 broadcast_multiply_fusion
  150.8 4.8 %collective-permute-done.1 = f32[128,512]{0,1:T(8,128)S(1)} collective-permute-done((f32[128,512]{0,1:T(8,128)S(1)}, f32[128,512]{0,1:T(8,128)S(1)}, u32[]{:S(2)}, u32[]{:S(2)}) %collective-permute-start.1) | collective-permute-done | bytes 262176 | tf_op jit(solution)/shard_map/ppermute | solution.py:78
  155.7 1.0 collective-permute-start.2
  156.7 2.6 collective-permute-start.3
  159.3 0.6 collective-permute-start.4
  160.4 0.8 dynamic_slice.7
  161.2 2.6 collective-permute-done.4
  164.6 60.2 %all_to_all.28 = bf16[128,16,512]{2,1,0:T(8,128)(2,1)S(1)} all-to-all(bf16[128,16,512]{2,1,0:T(8,128)(2,1)S(1)} %pad_maximum_fusion.3), channel_id=1, replica_groups={{0,4,8,12,16,20,24,28,32,36,40,44,48,52,56,60,64,68,72,76,80,84,88,92,9..., dimensions={0} | all-to-all | bytes 4194304 | tf_op jit(solution)/shard_map/all_to_all | solution.py:215
  224.8 2.4 collective-permute-start.5
  227.2 3.8 %collective-permute-done.5 = bf16[2,64,16,512]{3,2,1,0:T(8,128)(2,1)S(1)} collective-permute-done((bf16[2,64,16,512]{3,2,1,0:T(8,128)(2,1)S(1)}, bf16[2,64,16,512]{3,2,1,0:T(8,128)(2,1)S(1)}, u32[]{:S(2)}, u32[]{:S(2)}) %collective-permute-start.5) | collective-permute-done | bytes 2097184 | tf_op jit(solution)/shard_map/ppermute | solution.py:224
  231.0 1.3 copy-done.19
  232.4 2.9 fusion.6
  235.2 7.5 %convert_bitcast_fusion = bf16[4,1024,512]{1,2,0:T(8,128)(2,1)} fusion(bf16[352,4,512]{2,0,1:T(8,128)(2,1)S(1)} %bitcast.194, f32[1024,352]{0,1:T(8,128)} %fusion.6, bf16[4,512,352]{1,2,0:T(8,128)(2,1)S(1)} %copy-done.6, bf16[2,1024,512]{2,1,0:T(8,128)(2,1)} %bitcast.204, bf16[2,1024,512]{2,1,0:T(8,128)(2,1)} %bitcast.193), kind=kOutput, calls=%fused_computation.15 | convolution fusion | flops 2959147008 | bytes 12713984 | tf_op jit(solution)/shard_map/nh,hqd->qnd/dot_general | solution.py:229
  242.7 1.9 slice.124
  245.1 3.8 %collective-permute-done.6 = bf16[2,1024,512]{1,2,0:T(8,128)(2,1)S(1)} collective-permute-done((bf16[2,1024,512]{1,2,0:T(8,128)(2,1)S(1)}, bf16[2,1024,512]{1,2,0:T(8,128)(2,1)S(1)}, u32[]{:S(2)}, u32[]{:S(2)}) %collective-permute-start.6) | collective-permute-done | bytes 2097184 | tf_op jit(solution)/shard_map/ppermute | solution.py:235
  248.9 1.0 add_convert_fusion
  249.9 2.6 copy.124
  252.5 7.5 %all-to-all-start.3 = ((bf16[128,16,512]{2,1,0:T(8,128)(2,1)}), bf16[128,16,512]{2,1,0:T(8,128)(2,1)}, u32[]{:S(2)}, u32[]{:S(2)}) async-start(bf16[128,16,512]{2,1,0:T(8,128)(2,1)} %bitcast.187), calls=%async_computation.3 | async-start | bytes 4194304 | tf_op jit(solution)/shard_map/all_to_all | solution.py:237
  260.3 52.3 %all-to-all-done.3 = bf16[128,16,512]{2,1,0:T(8,128)(2,1)} async-done(((bf16[128,16,512]{2,1,0:T(8,128)(2,1)}), bf16[128,16,512]{2,1,0:T(8,128)(2,1)}, u32[]{:S(2)}, u32[]{:S(2)}) %all-to-all-start.3) | async-done | bytes 2097184 | tf_op jit(solution)/shard_map/all_to_all | solution.py:237
  312.5 1.9 add_convert_fusion.1
  314.5 2.7 gather_fusion.6
  317.2 1.5 reshape.1168
  318.7 2.3 multiply_reduce_fusion
  321.2 10.2 %all_gather.3 = bf16[128,2048]{0,1:T(8,128)(2,1)S(1)} all-gather(bf16[128,512]{0,1:T(8,128)(2,1)S(1)} %fusion.25), channel_id=1, replica_groups=mesh['req'=64,'tp'=4] {'tp'}, dimensions={1}, use_global_device_ids=true | all-gather | bytes 655360 | tf_op jit(solution)/shard_map/all_gather | solution.py:251
  331.4 1.0 copy.126
  (101 shorter events, 7.3 us)
Async XLA Ops:
  0.0 65.2 %copy-start = (bf16[2048,512]{1,0:T(8,128)(2,1)S(1)}, bf16[2048,512]{1,0:T(8,128)(2,1)}, u32[]{:S(2)}) copy-start(bf16[2048,512]{1,0:T(8,128)(2,1)} %param.16) | copy-start | bytes 6291460
  1.7 0.6 copy-start.22
  30.1 96.9 %all-to-all-start.1 = ((bf16[64,1,1,128,256]{4,3,2,1,0:T(8,128)(2,1)}), bf16[64,1,1,128,256]{4,3,2,1,0:T(8,128)(2,1)}, u32[]{:S(2)}, u32[]{:S(2)}) async-start(bf16[64,1,1,128,256]{4,3,2,1,0:T(8,128)(2,1)} %bitcast.184), calls=%async_computation.1 | async-start | bytes 8388608 | tf_op jit(solution)/shard_map/all_to_all | solution.py:139
  52.3 3.3 copy-start.8
  57.6 2.3 copy-start.14
  57.6 7.6 %copy-start.13 = (f32[2048]{0:T(1024)S(1)}, f32[2048]{0:T(1024)}, u32[]{:S(2)}) copy-start(f32[2048]{0:T(1024)} %param.15) | copy-start | bytes 24580
  64.6 0.6 copy-start.17
  77.0 2.8 copy-start.4
  79.4 0.8 copy-start.21
  79.4 0.8 copy-start.23
  79.4 1.0 copy-start.3
  79.4 1.0 copy-start.18
  79.4 1.4 copy-start.20
  137.1 6.3 %copy-start.15 = (s32[128,6]{0,1:T(8,128)S(1)}, s32[128,6]{0,1:T(8,128)}, u32[]{:S(2)}) copy-start(s32[128,6]{0,1:T(8,128)} %param.26) | copy-start | bytes 9220
  137.9 8.2 %collective-permute-start = (f32[2,128,512]{1,2,0:T(8,128)S(1)}, f32[2,128,512]{1,2,0:T(8,128)S(1)}, u32[]{:S(2)}, u32[]{:S(2)}) collective-permute-start(f32[2,128,512]{1,2,0:T(8,128)S(1)} %slice.119), channel_id=1, source_target_pairs={{0,1},{1,0},{2,3},{3,2},{4,5},{5,4},{6,7},{7,6},{8,9},{9,8},{10,11... | collective-permute-start | bytes 1572872 | tf_op jit(solution)/shard_map/ppermute | solution.py:76
  146.2 9.4 %collective-permute-start.1 = (f32[128,512]{0,1:T(8,128)S(1)}, f32[128,512]{0,1:T(8,128)S(1)}, u32[]{:S(2)}, u32[]{:S(2)}) collective-permute-start(f32[128,512]{0,1:T(8,128)S(1)} %slice_bitcast_fusion), channel_id=1, source_target_pairs={{0,2},{2,0},{1,3},{3,1},{4,6},{6,4},{5,7},{7,5},{8,10},{10,8},{9,1... | collective-permute-start | bytes 786440 | tf_op jit(solution)/shard_map/ppermute | solution.py:78
  155.7 8.7 %copy-start.10 = (bf16[128,512]{0,1:T(8,128)(2,1)}, bf16[128,512]{0,1:T(8,128)(2,1)S(1)}, u32[]{:S(2)}) copy-start(bf16[128,512]{0,1:T(8,128)(2,1)S(1)} %get-tuple-element.16) | copy-start | bytes 393220
  155.7 5.5 %collective-permute-start.2 = (f32[128,1]{0,1:T(1,128)S(1)}, f32[128,1]{0,1:T(1,128)S(1)}, u32[]{:S(2)}, u32[]{:S(2)}) collective-permute-start(f32[128,1]{0,1:T(1,128)S(1)} %bitcast.200), channel_id=1, source_target_pairs={{0,1},{1,0},{2,3},{3,2},{4,5},{5,4},{6,7},{7,6},{8,9},{9,8},{10,11... | collective-permute-start | bytes 1544 | tf_op jit(solution)/shard_map/ppermute | solution.py:84
  156.7 4.5 %collective-permute-start.3 = (f32[128,1]{0,1:T(1,128)S(1)}, f32[128,1]{0,1:T(1,128)S(1)}, u32[]{:S(2)}, u32[]{:S(2)}) collective-permute-start(f32[128,1]{0,1:T(1,128)S(1)} %bitcast.201), channel_id=1, source_target_pairs={{0,2},{1,3},{2,0},{3,1},{4,6},{5,7},{6,4},{7,5},{8,10},{9,11},{10,... | collective-permute-start | bytes 1544 | tf_op jit(solution)/shard_map/ppermute | solution.py:84
  159.3 4.5 %collective-permute-start.4 = (f32[128,1]{0,1:T(1,128)S(1)}, f32[128,1]{0,1:T(1,128)S(1)}, u32[]{:S(2)}, u32[]{:S(2)}) collective-permute-start(f32[128,1]{0,1:T(1,128)S(1)} %bitcast.202), channel_id=1, source_target_pairs={{0,3},{1,2},{2,1},{3,0},{4,7},{5,6},{6,5},{7,4},{8,11},{9,10},{10,... | collective-permute-start | bytes 1544 | tf_op jit(solution)/shard_map/ppermute | solution.py:84
  164.6 67.8 %copy-start.7 = (bf16[4,512,352]{1,2,0:T(8,128)(2,1)S(1)}, bf16[4,512,352]{1,2,0:T(8,128)(2,1)}, u32[]{:S(2)}) copy-start(bf16[4,512,352]{1,2,0:T(8,128)(2,1)} %gather_fusion) | copy-start | bytes 4325380
  224.8 6.2 %copy-start.5 = (bf16[128,16,512]{2,1,0:T(8,128)(2,1)}, bf16[128,16,512]{2,1,0:T(8,128)(2,1)S(1)}, u32[]{:S(2)}) copy-start(bf16[128,16,512]{2,1,0:T(8,128)(2,1)S(1)} %all_to_all.28) | copy-start | bytes 6291460
  224.8 6.2 %collective-permute-start.5 = (bf16[2,64,16,512]{3,2,1,0:T(8,128)(2,1)S(1)}, bf16[2,64,16,512]{3,2,1,0:T(8,128)(2,1)S(1)}, u32[]{:S(2)}, u32[]{:S(2)}) collective-permute-start(bf16[2,64,16,512]{3,2,1,0:T(8,128)(2,1)S(1)} %bitcast.191), channel_id=1, source_target_pairs={{0,1},{1,0},{2,3},{3,2},{4,5},{5,4},{6,7},{7,6},{8,9},{9,8},{10,11... | collective-permute-start | bytes 6291464 | tf_op jit(solution)/shard_map/ppermute | solution.py:224
  231.0 1.3 copy-start.19
  232.4 2.9 copy-start.6
  232.4 2.9 copy-start.9
  242.7 6.2 %copy-start.2 = (bf16[4,1024,512]{1,2,0:T(8,128)(2,1)S(1)}, bf16[4,1024,512]{1,2,0:T(8,128)(2,1)}, u32[]{:S(2)}) copy-start(bf16[4,1024,512]{1,2,0:T(8,128)(2,1)} %convert_bitcast_fusion) | copy-start | bytes 12582916
  244.7 4.2 %collective-permute-start.6 = (bf16[2,1024,512]{1,2,0:T(8,128)(2,1)S(1)}, bf16[2,1024,512]{1,2,0:T(8,128)(2,1)S(1)}, u32[]{:S(2)}, u32[]{:S(2)}) collective-permute-start(bf16[2,1024,512]{1,2,0:T(8,128)(2,1)S(1)} %slice.124), channel_id=1, source_target_pairs={{0,1},{1,0},{2,3},{3,2},{4,5},{5,4},{6,7},{7,6},{8,9},{9,8},{10,11... | collective-permute-start | bytes 6291464 | tf_op jit(solution)/shard_map/ppermute | solution.py:235
  252.5 7.5 %copy-start.12 = (s32[128,6]{1,0:T(8,128)S(1)}, s32[128,6]{1,0:T(8,128)}, u32[]{:S(2)}) copy-start(s32[128,6]{1,0:T(8,128)} %get-tuple-element.29) | copy-start | bytes 9220
  252.5 7.6 %copy-start.16 = (f32[128,6]{0,1:T(8,128)S(1)}, f32[128,6]{0,1:T(8,128)}, u32[]{:S(2)}) copy-start(f32[128,6]{0,1:T(8,128)} %param.27) | copy-start | bytes 9220
  252.5 60.0 %all-to-all-start.3 = ((bf16[128,16,512]{2,1,0:T(8,128)(2,1)}), bf16[128,16,512]{2,1,0:T(8,128)(2,1)}, u32[]{:S(2)}, u32[]{:S(2)}) async-start(bf16[128,16,512]{2,1,0:T(8,128)(2,1)} %bitcast.187), calls=%async_computation.3 | async-start | bytes 4194304 | tf_op jit(solution)/shard_map/all_to_all | solution.py:237
  317.1 15.3 %copy-start.1 = (bf16[2048,512]{1,0:T(8,128)(2,1)S(1)}, bf16[2048,512]{1,0:T(8,128)(2,1)}, u32[]{:S(2)}) copy-start(bf16[2048,512]{1,0:T(8,128)(2,1)} %param.16) | copy-start | bytes 6291460
  318.7 2.5 copy-start.11

commit v7 on v5

--- a/solution.py
+++ b/solution.py
@@ -80,13 +80,9 @@
     )
 
 
-def tp_exchange(value):
-    return [lax.ppermute(value, "tp", tuple((t, t ^ flip) for t in range(4))) for flip in (1, 2, 3)]
-
-
 def tp_sum(value):
-    near, across, diagonal = tp_exchange(value)
-    return (value + near) + (across + diagonal)
+    value = value + lax.ppermute(value, "tp", ON_CHIP)
+    return value + lax.ppermute(value, "tp", CROSS_CHIP)
 
 
 def shards(
@@ -161,8 +157,19 @@
     scatter_order = jnp.stack([tp_me ^ 1, tp_me ^ 3, tp_me, tp_me ^ 2])
     down_w = w_down[0].reshape(hidden_units, n_tp, quarter)[:, scatter_order]
     out_w = w_out.reshape(-1, n_tp, quarter)[:, scatter_order]
-    gate_w, up_w, down_w, out_w, queries = lax.optimization_barrier(
-        (gate_w, up_w, down_w, out_w, queries)
+    topk = expert_ids.shape[1]
+    n_exp = n_req * w_gate_up.shape[0]
+    cap_e = 4 * tok_rows * topk // (3 * n_exp)
+    flat_ids = expert_ids.reshape(-1)
+    onehot = (flat_ids[:, None] == jnp.arange(n_exp, dtype=jnp.int32)[None, :]).astype(jnp.int32)
+    slot_rank = jnp.sum((jnp.cumsum(onehot, axis=0) - 1) * onehot, axis=1)
+    assign_slot = flat_ids * cap_e + slot_rank
+    slot_match = assign_slot[None, :] == jnp.arange(n_exp * cap_e, dtype=jnp.int32)[:, None]
+    selector = jnp.any(slot_match.reshape(n_exp * cap_e, tok_rows, topk), axis=2).astype(
+        jnp.bfloat16
+    )
+    gate_w, up_w, down_w, out_w, selector, assign_slot, queries = lax.optimization_barrier(
+        (gate_w, up_w, down_w, out_w, selector, assign_slot, queries)
     )
     keyval = jnp.dot(
         normed,
@@ -190,17 +197,6 @@
     sq_sum = tp_sum(jnp.sum(resid_wide * resid_wide, axis=-1, keepdims=True))
     gain_q = lax.dynamic_slice_in_dim(moe_gain, tp_me * quarter, quarter, axis=0)
     moe_in = (resid_wide * lax.rsqrt(sq_sum / model_width + eps) * gain_q).astype(jnp.bfloat16)
-    topk = expert_ids.shape[1]
-    n_exp = n_req * w_gate_up.shape[0]
-    cap_e = 4 * tok_rows * topk // (3 * n_exp)
-    flat_ids = expert_ids.reshape(-1)
-    onehot = (flat_ids[:, None] == jnp.arange(n_exp, dtype=jnp.int32)[None, :]).astype(jnp.int32)
-    slot_rank = jnp.sum((jnp.cumsum(onehot, axis=0) - 1) * onehot, axis=1)
-    assign_slot = flat_ids * cap_e + slot_rank
-    slot_match = assign_slot[None, :] == jnp.arange(n_exp * cap_e, dtype=jnp.int32)[:, None]
-    selector = jnp.any(slot_match.reshape(n_exp * cap_e, tok_rows, topk), axis=2).astype(
-        jnp.bfloat16
-    )
     outgoing = (
         jnp.dot(selector, moe_in, preferred_element_type=jnp.float32)
         .astype(jnp.bfloat16)

time: 322 us -> 318 us (0.988)
  waiting for transfers between devices: 144 us -> 137 us
  starting transfers between devices: 32.9 us -> 36.7 us
    all_to_all x1, waiting for transfers between devices: 55.9 us -> 51.9 us  [shards(): lax.all_to_all(served, 'req', split_axis=0, concat_axis=0, tiled=True)]
  transfers between devices with their start and end apart: 11 -> 10, of which waited for: 8 -> 10; matrix products, arithmetic and copies ran while one was open for 12% -> 12% of each run, Pallas kernels for 0% -> 0%
where the time goes in v7:
time: 318 us; the launch traced here: 317 us
  waiting for transfers between devices  137 us (43%)
  blocking collectives  66.4 us (21%)
  local copies, waits for them, and re-layouts  46.3 us (15%)
  starting transfers between devices  36.7 us (12%)
  other arithmetic  17.8 us (6%)
  matrix products  11.5 us (4%)
    all_to_all x1, waiting for transfers between devices, shards(): lax.all_to_all(served, 'req', split_axis=0, concat_axis=0, tiled=True)  51.9 us
    all_to_all x1, blocking collectives, shards(): lax.all_to_all(outgoing, 'req', split_axis=0, concat_axis=0, tiled=True)  31.4 us
    ppermute x2, waiting for transfers between devices, tp_reduce_scatter(): lax.ppermute(summed[1].astype(wire_dtype), 'tp', CROSS_CHIP)  29.7 us
    all_to_all x1, waiting for transfers between devices, shards(): lax.all_to_all(expert_share, 'req', split_axis=0, concat_axis=0, tiled=True)  25.7 us
    all_to_all x1, blocking collectives, shards(): lax.all_to_all(request, 'req', split_axis=0, concat_axis=0, tiled=True)  22.6 us
    ppermute x1, waiting for transfers between devices, shards(): cross_q = lax.ppermute(expert_q, 'tp', CROSS_CHIP)  19.7 us
    all_gather x1, blocking collectives, shards(): return lax.all_gather(layer_q, 'tp', axis=1, tiled=True)  12.5 us
    all_to_all x1, starting transfers between devices, shards(): lax.all_to_all(expert_share, 'req', split_axis=0, concat_axis=0, tiled=True)  7.94 us
  transfers between devices with their start and end apart: 10, of which 10 were waited for; matrix products, arithmetic and copies ran while one was open for 12% of the time, Pallas kernels for 0%

profile of v7, /device:TPU:1, one launch (start us, length us, event | category | flops | bytes accessed | tf_op | source)
XLA Modules:
  0.0 317.4 jit_solution(15675900048497555424)
XLA Ops:
  0.0 0.8 and_select_fusion.3
  0.8 0.7 fusion.62
  2.3 22.6 %all_to_all.27 = s32[64,1,1]{2,1,0:T(1,128)S(1)} all-to-all(s32[64,1,1]{2,1,0:T(1,128)S(1)} %copy.146), channel_id=1, replica_groups=mesh['req'=64,'tp'=4] {'req'}, dimensions={0} | all-to-all | bytes 512 | tf_op jit(solution)/shard_map/all_to_all | solution.py:131
  24.9 1.2 reduce.5
  26.1 4.0 %gather_fusion.4 = bf16[64,128,256]{2,1,0:T(8,128)(2,1)} fusion(bf16[16,128,256]{2,1,0:T(8,128)(2,1)} %bitcast.185, s32[1024]{0:T(1024)S(1)} %pad_clamp_fusion.2), kind=kCustom, calls=%fused_computation.4 | custom fusion | bytes 8388864 | tf_op jit(solution)/shard_map/gather | solution.py:132
  30.1 6.0 %all-to-all-start.1 = ((bf16[64,1,1,128,256]{4,3,2,1,0:T(8,128)(2,1)}), bf16[64,1,1,128,256]{4,3,2,1,0:T(8,128)(2,1)}, u32[]{:S(2)}, u32[]{:S(2)}) async-start(bf16[64,1,1,128,256]{4,3,2,1,0:T(8,128)(2,1)} %bitcast.184), calls=%async_computation.1 | async-start | bytes 8388608 | tf_op jit(solution)/shard_map/all_to_all | solution.py:135
  37.6 0.6 reduce.4
  38.5 0.5 fusion.36
  39.0 0.8 reshape.956
  39.8 3.4 %fusion.69 = (bf16[1,1,2048,352]{2,3,1,0:T(8,128)(2,1)S(1)}, bf16[1,1,2048,352]{2,3,1,0:T(8,128)(2,1)}) fusion(bf16[1,2,2048,352]{2,3,1,0:T(8,128)(2,1)} %param.20), kind=kLoop, calls=%fused_computation.154 | loop fusion | bytes 5767168 | tf_op jit(solution)/shard_map/slice | solution.py:156
  43.2 1.1 reshape_squeeze.10
  44.5 4.4 %reshape_squeeze.9 = bf16[4,512,352]{1,0,2:T(4,128)(2,1)} reshape(bf16[1,1,2048,352]{2,3,1,0:T(8,128)(2,1)} %get-tuple-element.24) | data formatting | bytes 2883584 | tf_op jit(solution)/shard_map/reshape;squeeze | solution.py:155
  49.0 1.6 copy.134
  50.6 0.6 fusion.58
  51.2 1.7 gather_fusion.1
  52.9 1.8 gather_fusion
  54.8 2.9 copy.137
  57.6 2.4 copy.138
  60.1 1.1 reshape_squeeze.11
  61.8 0.6 pad_clamp_fusion.3
  62.4 2.4 gather_fusion.3
  64.8 2.0 gather_fusion.2
  66.8 1.8 reduce-window.18
  69.2 0.5 fusion.3
  69.9 0.7 add_convert_fusion.1
  72.1 2.4 broadcast_and_fusion
  74.5 0.8 pad_add_fusion
  75.3 51.9 %all-to-all-done.1 = bf16[64,1,1,128,256]{4,3,2,1,0:T(8,128)(2,1)} async-done(((bf16[64,1,1,128,256]{4,3,2,1,0:T(8,128)(2,1)}), bf16[64,1,1,128,256]{4,3,2,1,0:T(8,128)(2,1)}, u32[]{:S(2)}, u32[]{:S(2)}) %all-to-all-start.1) | async-done | bytes 4194336 | tf_op jit(solution)/shard_map/all_to_all | solution.py:135
  127.2 4.2 %gather_fusion.5 = bf16[32,128,256]{2,1,0:T(8,128)(2,1)} fusion(bf16[64,128,256]{2,1,0:T(8,128)(2,1)} %bitcast.22, s32[1024]{0:T(1024)S(1)} %pad_clamp_fusion.1), kind=kCustom, calls=%fused_computation.5 | custom fusion | bytes 4194432 | tf_op jit(solution)/shard_map/gather | solution.py:136
  131.4 1.7 fusion.70
  133.2 1.3 fusion.72
  134.5 1.1 fusion
  135.6 1.7 fusion.10
  137.4 0.7 convolution_bitcast_fusion
  138.2 5.5 %collective-permute-start = (f32[2,128,512]{1,2,0:T(8,128)S(1)}, f32[2,128,512]{1,2,0:T(8,128)S(1)}, u32[]{:S(2)}, u32[]{:S(2)}) collective-permute-start(f32[2,128,512]{1,2,0:T(8,128)S(1)} %slice.119), channel_id=1, source_target_pairs={{0,1},{1,0},{2,3},{3,2},{4,5},{5,4},{6,7},{7,6},{8,9},{9,8},{10,11... | collective-permute-start | bytes 1572872 | tf_op jit(solution)/shard_map/ppermute | solution.py:76
  143.7 1.5 collective-permute-done
  145.3 2.7 collective-permute-start.1
  148.2 6.2 %collective-permute-done.1 = f32[128,512]{0,1:T(8,128)S(1)} collective-permute-done((f32[128,512]{0,1:T(8,128)S(1)}, f32[128,512]{0,1:T(8,128)S(1)}, u32[]{:S(2)}, u32[]{:S(2)}) %collective-permute-start.1) | collective-permute-done | bytes 262176 | tf_op jit(solution)/shard_map/ppermute | solution.py:78
  154.5 1.3 collective-permute-start.2
  155.8 0.8 collective-permute-done.2
  156.6 2.6 collective-permute-start.3
  159.2 0.8 dynamic_slice.7
  160.0 0.5 collective-permute-done.3
  160.5 0.5 convolution_convert_fusion
  161.1 31.4 %all_to_all.28 = bf16[64,16,512]{2,1,0:T(8,128)(2,1)S(1)} all-to-all(bf16[64,16,512]{2,1,0:T(8,128)(2,1)S(1)} %bitcast.189), channel_id=1, replica_groups=mesh['req'=64,'tp'=4] {'req'}, dimensions={0} | all-to-all | bytes 2097152 | tf_op jit(solution)/shard_map/all_to_all | solution.py:205
  192.5 2.6 collective-permute-start.4
  195.1 19.7 %collective-permute-done.4 = bf16[64,16,512]{2,1,0:T(8,128)(2,1)S(1)} collective-permute-done((bf16[64,16,512]{2,1,0:T(8,128)(2,1)S(1)}, bf16[64,16,512]{2,1,0:T(8,128)(2,1)S(1)}, u32[]{:S(2)}, u32[]{:S(2)}) %collective-permute-start.4) | collective-permute-done | bytes 1048608 | tf_op jit(solution)/shard_map/ppermute | solution.py:206
  215.0 5.0 %collective-permute-start.5 = (bf16[2,64,16,512]{3,2,1,0:T(8,128)(2,1)S(1)}, bf16[2,64,16,512]{3,2,1,0:T(8,128)(2,1)S(1)}, u32[]{:S(2)}, u32[]{:S(2)}) collective-permute-start(bf16[2,64,16,512]{3,2,1,0:T(8,128)(2,1)S(1)} %pad_maximum_fusion.1), channel_id=1, source_target_pairs={{0,1},{1,0},{2,3},{3,2},{4,5},{5,4},{6,7},{7,6},{8,9},{9,8},{10,11... | collective-permute-start | bytes 6291464 | tf_op jit(solution)/shard_map/ppermute | solution.py:208
  220.0 3.8 %collective-permute-done.5 = bf16[2,64,16,512]{3,2,1,0:T(8,128)(2,1)S(1)} collective-permute-done((bf16[2,64,16,512]{3,2,1,0:T(8,128)(2,1)S(1)}, bf16[2,64,16,512]{3,2,1,0:T(8,128)(2,1)S(1)}, u32[]{:S(2)}, u32[]{:S(2)}) %collective-permute-start.5) | collective-permute-done | bytes 2097184 | tf_op jit(solution)/shard_map/ppermute | solution.py:208
  223.8 1.9 fusion.8
  225.8 2.0 fusion.9
  227.8 2.5 convert_bitcast_fusion
  230.9 3.8 %collective-permute-done.6 = bf16[2,1024,512]{1,2,0:T(8,128)(2,1)S(1)} collective-permute-done((bf16[2,1024,512]{1,2,0:T(8,128)(2,1)S(1)}, bf16[2,1024,512]{1,2,0:T(8,128)(2,1)S(1)}, u32[]{:S(2)}, u32[]{:S(2)}) %collective-permute-start.6) | collective-permute-done | bytes 2097184 | tf_op jit(solution)/shard_map/ppermute | solution.py:76
  234.7 0.9 convert_add_fusion
  235.8 2.5 collective-permute-start.7
  238.3 23.4 %collective-permute-done.7 = bf16[1024,512]{0,1:T(8,128)(2,1)S(1)} collective-permute-done((bf16[1024,512]{0,1:T(8,128)(2,1)S(1)}, bf16[1024,512]{0,1:T(8,128)(2,1)S(1)}, u32[]{:S(2)}, u32[]{:S(2)}) %collective-permute-start.7) | collective-permute-done | bytes 1048608 | tf_op jit(solution)/shard_map/ppermute | solution.py:78
  262.1 1.3 copy.152
  263.4 7.9 %all-to-all-start.3 = ((bf16[64,16,512]{2,1,0:T(8,128)(2,1)}), bf16[64,16,512]{2,1,0:T(8,128)(2,1)S(1)}, u32[]{:S(2)}, u32[]{:S(2)}) async-start(bf16[64,16,512]{2,1,0:T(8,128)(2,1)} %bitcast.61), calls=%async_computation.3 | async-start | bytes 2097152 | tf_op jit(solution)/shard_map/all_to_all | solution.py:222
  271.5 25.7 %all-to-all-done.3 = bf16[64,16,512]{2,1,0:T(8,128)(2,1)S(1)} async-done(((bf16[64,16,512]{2,1,0:T(8,128)(2,1)}), bf16[64,16,512]{2,1,0:T(8,128)(2,1)S(1)}, u32[]{:S(2)}, u32[]{:S(2)}) %all-to-all-start.3) | async-done | bytes 1048608 | tf_op jit(solution)/shard_map/all_to_all | solution.py:222
  297.2 2.7 gather_fusion.6
  299.9 1.5 reshape.970
  301.5 2.3 multiply_reduce_fusion
  303.9 12.5 %all_gather.3 = bf16[128,2048]{0,1:T(8,128)(2,1)S(1)} all-gather(bf16[128,512]{0,1:T(8,128)(2,1)S(1)} %fusion.28), channel_id=1, replica_groups=mesh['req'=64,'tp'=4] {'tp'}, dimensions={1}, use_global_device_ids=true | all-gather | bytes 655360 | tf_op jit(solution)/shard_map/all_gather | solution.py:226
  316.4 1.0 copy.154
  (101 shorter events, 6.9 us)
Async XLA Ops:
  0.0 38.5 %copy-start = (bf16[2048,512]{1,0:T(8,128)(2,1)S(1)}, bf16[2048,512]{1,0:T(8,128)(2,1)}, u32[]{:S(2)}) copy-start(bf16[2048,512]{1,0:T(8,128)(2,1)} %param.16) | copy-start | bytes 6291460
  1.7 0.6 copy-start.20
  30.1 6.0 %copy-start.10 = (s32[128,6]{0,1:T(8,128)S(1)}, s32[128,6]{0,1:T(8,128)}, u32[]{:S(2)}) copy-start(s32[128,6]{0,1:T(8,128)} %param.26) | copy-start | bytes 9220
  30.1 7.1 %copy-start.13 = (s32[1,128]{1,0:T(1,128)S(1)}, s32[1,128]{1,0:T(1,128)}, u32[]{:S(2)}) copy-start(s32[1,128]{1,0:T(1,128)} %param.22) | copy-start | bytes 1540
  30.1 8.1 %copy-start.2 = (bf16[128,2048]{1,0:T(8,128)(2,1)S(1)}, bf16[128,2048]{1,0:T(8,128)(2,1)}, u32[]{:S(2)}) copy-start(bf16[128,2048]{1,0:T(8,128)(2,1)} %param.14) | copy-start | bytes 1572868
  30.1 8.4 %copy-start.11 = (f32[2048]{0:T(1024)S(1)}, f32[2048]{0:T(1024)}, u32[]{:S(2)}) copy-start(f32[2048]{0:T(1024)} %param.15) | copy-start | bytes 24580
  30.1 97.1 %all-to-all-start.1 = ((bf16[64,1,1,128,256]{4,3,2,1,0:T(8,128)(2,1)}), bf16[64,1,1,128,256]{4,3,2,1,0:T(8,128)(2,1)}, u32[]{:S(2)}, u32[]{:S(2)}) async-start(bf16[64,1,1,128,256]{4,3,2,1,0:T(8,128)(2,1)} %bitcast.184), calls=%async_computation.1 | async-start | bytes 8388608 | tf_op jit(solution)/shard_map/all_to_all | solution.py:135
  38.5 4.7 %copy-start.16 = (f32[128]{0:T(128)}, f32[128]{0:T(128)S(1)}, u32[]{:S(2)}) copy-start(f32[128]{0:T(128)S(1)} %add_rsqrt_fusion) | copy-start | bytes 1540
  57.6 2.4 copy-start.7
  61.2 0.6 copy-start.15
  66.7 4.1 %copy-start.4 = (f32[128,4,128]{2,1,0:T(4,128)S(1)}, f32[128,4,128]{2,1,0:T(4,128)}, u32[]{:S(2)}) copy-start(f32[128,4,128]{2,1,0:T(4,128)} %reshape.956) | copy-start | bytes 786436
  66.7 4.5 %copy-start.19 = (s32[1,32]{1,0:T(1,128)S(1)}, s32[1,32]{1,0:T(1,128)}, u32[]{:S(2)}) copy-start(s32[1,32]{1,0:T(1,128)} %param.24) | copy-start | bytes 388
  66.7 4.5 %copy-start.21 = (s32[32]{0:T(128)S(1)}, s32[32]{0:T(128)}, u32[]{:S(2)}) copy-start(s32[32]{0:T(128)} %copy-done.20) | copy-start | bytes 388
  66.7 4.6 %copy-start.3 = (bf16[128,2048]{1,0:T(8,128)(2,1)S(1)}, bf16[128,2048]{1,0:T(8,128)(2,1)}, u32[]{:S(2)}) copy-start(bf16[128,2048]{1,0:T(8,128)(2,1)} %param.14) | copy-start | bytes 1572868
  66.7 4.6 %copy-start.12 = (f32[2048]{0:T(1024)S(1)}, f32[2048]{0:T(1024)}, u32[]{:S(2)}) copy-start(f32[2048]{0:T(1024)} %param.15) | copy-start | bytes 24580
  66.8 4.6 %copy-start.17 = (f32[128]{0:T(128)S(1)}, f32[128]{0:T(128)}, u32[]{:S(2)}) copy-start(f32[128]{0:T(128)} %copy-done.16) | copy-start | bytes 1540
  69.2 2.1 copy-start.18
  131.4 1.7 copy-start.9
  138.2 7.1 %collective-permute-start = (f32[2,128,512]{1,2,0:T(8,128)S(1)}, f32[2,128,512]{1,2,0:T(8,128)S(1)}, u32[]{:S(2)}, u32[]{:S(2)}) collective-permute-start(f32[2,128,512]{1,2,0:T(8,128)S(1)} %slice.119), channel_id=1, source_target_pairs={{0,1},{1,0},{2,3},{3,2},{4,5},{5,4},{6,7},{7,6},{8,9},{9,8},{10,11... | collective-permute-start | bytes 1572872 | tf_op jit(solution)/shard_map/ppermute | solution.py:76
  145.3 9.1 %collective-permute-start.1 = (f32[128,512]{0,1:T(8,128)S(1)}, f32[128,512]{0,1:T(8,128)S(1)}, u32[]{:S(2)}, u32[]{:S(2)}) collective-permute-start(f32[128,512]{0,1:T(8,128)S(1)} %slice_bitcast_fusion.1), channel_id=1, source_target_pairs={{0,2},{2,0},{1,3},{3,1},{4,6},{6,4},{5,7},{7,5},{8,10},{10,8},{9,1... | collective-permute-start | bytes 786440 | tf_op jit(solution)/shard_map/ppermute | solution.py:78
  154.5 2.1 collective-permute-start.2
  156.6 3.9 %collective-permute-start.3 = (f32[128,1]{0,1:T(1,128)S(1)}, f32[128,1]{0,1:T(1,128)S(1)}, u32[]{:S(2)}, u32[]{:S(2)}) collective-permute-start(f32[128,1]{0,1:T(1,128)S(1)} %bitcast_add_fusion.1), channel_id=1, source_target_pairs={{0,2},{2,0},{1,3},{3,1},{4,6},{6,4},{5,7},{7,5},{8,10},{10,8},{9,1... | collective-permute-start | bytes 1544 | tf_op jit(solution)/shard_map/ppermute | solution.py:85
  192.5 22.3 %collective-permute-start.4 = (bf16[64,16,512]{2,1,0:T(8,128)(2,1)S(1)}, bf16[64,16,512]{2,1,0:T(8,128)(2,1)S(1)}, u32[]{:S(2)}, u32[]{:S(2)}) collective-permute-start(bf16[64,16,512]{2,1,0:T(8,128)(2,1)S(1)} %all_to_all.28), channel_id=1, source_target_pairs={{0,2},{2,0},{1,3},{3,1},{4,6},{6,4},{5,7},{7,5},{8,10},{10,8},{9,1... | collective-permute-start | bytes 3145736 | tf_op jit(solution)/shard_map/ppermute | solution.py:206
  214.8 9.0 %copy-start.6 = (bf16[4,512,352]{1,2,0:T(8,128)(2,1)S(1)}, bf16[4,512,352]{1,2,0:T(8,128)(2,1)}, u32[]{:S(2)}) copy-start(bf16[4,512,352]{1,2,0:T(8,128)(2,1)} %gather_fusion) | copy-start | bytes 4325380
  215.0 8.8 %collective-permute-start.5 = (bf16[2,64,16,512]{3,2,1,0:T(8,128)(2,1)S(1)}, bf16[2,64,16,512]{3,2,1,0:T(8,128)(2,1)S(1)}, u32[]{:S(2)}, u32[]{:S(2)}) collective-permute-start(bf16[2,64,16,512]{3,2,1,0:T(8,128)(2,1)S(1)} %pad_maximum_fusion.1), channel_id=1, source_target_pairs={{0,1},{1,0},{2,3},{3,2},{4,5},{5,4},{6,7},{7,6},{8,9},{9,8},{10,11... | collective-permute-start | bytes 6291464 | tf_op jit(solution)/shard_map/ppermute | solution.py:208
  223.8 2.0 copy-start.5
  225.8 2.0 copy-start.8
  230.5 4.2 %collective-permute-start.6 = (bf16[2,1024,512]{1,2,0:T(8,128)(2,1)S(1)}, bf16[2,1024,512]{1,2,0:T(8,128)(2,1)S(1)}, u32[]{:S(2)}, u32[]{:S(2)}) collective-permute-start(bf16[2,1024,512]{1,2,0:T(8,128)(2,1)S(1)} %slice.123), channel_id=1, source_target_pairs={{0,1},{1,0},{2,3},{3,2},{4,5},{5,4},{6,7},{7,6},{8,9},{9,8},{10,11... | collective-permute-start | bytes 6291464 | tf_op jit(solution)/shard_map/ppermute | solution.py:76
  235.8 25.9 %collective-permute-start.7 = (bf16[1024,512]{0,1:T(8,128)(2,1)S(1)}, bf16[1024,512]{0,1:T(8,128)(2,1)S(1)}, u32[]{:S(2)}, u32[]{:S(2)}) collective-permute-start(bf16[1024,512]{0,1:T(8,128)(2,1)S(1)} %fusion.22), channel_id=1, source_target_pairs={{0,2},{2,0},{1,3},{3,1},{4,6},{6,4},{5,7},{7,5},{8,10},{10,8},{9,1... | collective-permute-start | bytes 3145736 | tf_op jit(solution)/shard_map/ppermute | solution.py:78
  262.1 9.3 %copy-start.14 = (f32[128,6]{0,1:T(8,128)S(1)}, f32[128,6]{0,1:T(8,128)}, u32[]{:S(2)}) copy-start(f32[128,6]{0,1:T(8,128)} %param.27) | copy-start | bytes 9220
  263.4 33.8 %all-to-all-start.3 = ((bf16[64,16,512]{2,1,0:T(8,128)(2,1)}), bf16[64,16,512]{2,1,0:T(8,128)(2,1)S(1)}, u32[]{:S(2)}, u32[]{:S(2)}) async-start(bf16[64,16,512]{2,1,0:T(8,128)(2,1)} %bitcast.61), calls=%async_computation.3 | async-start | bytes 2097152 | tf_op jit(solution)/shard_map/all_to_all | solution.py:222
  299.9 17.5 %copy-start.1 = (bf16[2048,512]{1,0:T(8,128)(2,1)S(1)}, bf16[2048,512]{1,0:T(8,128)(2,1)}, u32[]{:S(2)}) copy-start(bf16[2048,512]{1,0:T(8,128)(2,1)} %param.16) | copy-start | bytes 6291460

commit v8 on v7

--- a/solution.py
+++ b/solution.py
@@ -150,7 +150,7 @@
     n_tp = lax.axis_size("tp")
     tp_me = lax.axis_index("tp")
     quarter = model_width // n_tp
-    quarter_order = jnp.stack([tp_me, tp_me ^ 2, tp_me ^ 1, tp_me ^ 3])
+    quarter_order = jnp.stack([tp_me, tp_me ^ 1, tp_me ^ 2, tp_me ^ 3])
     hidden_units = w_gate_up.shape[3]
     gate_w = w_gate_up[0, 0].reshape(n_tp, quarter, hidden_units)[quarter_order]
     up_w = w_gate_up[0, 1].reshape(n_tp, quarter, hidden_units)[quarter_order]
@@ -203,12 +203,21 @@
         .reshape(n_exp, cap_e, quarter)
     )
     expert_q = lax.all_to_all(outgoing, "req", split_axis=0, concat_axis=0, tiled=True)
+    near_q = lax.ppermute(expert_q, "tp", ON_CHIP)
     cross_q = lax.ppermute(expert_q, "tp", CROSS_CHIP)
-    chip_pair = jnp.stack([expert_q, cross_q])
-    partner_pair = lax.ppermute(chip_pair, "tp", ON_CHIP)
-    expert_in = jnp.concatenate([chip_pair, partner_pair]).reshape(n_tp, -1, quarter)
-    gate_part = jnp.einsum("qnd,qdh->nh", expert_in, gate_w, preferred_element_type=jnp.float32)
-    up_part = jnp.einsum("qnd,qdh->nh", expert_in, up_w, preferred_element_type=jnp.float32)
+    far_q = lax.ppermute(cross_q, "tp", ON_CHIP)
+    on_chip_in = jnp.stack([expert_q, near_q]).reshape(2, -1, quarter)
+    cross_in = jnp.stack([cross_q, far_q]).reshape(2, -1, quarter)
+
+    def contract(weights):
+        early = jnp.einsum(
+            "qnd,qdh->nh", on_chip_in, weights[:2], preferred_element_type=jnp.float32
+        )
+        late = jnp.einsum("qnd,qdh->nh", cross_in, weights[2:], preferred_element_type=jnp.float32)
+        return early + late
+
+    gate_part = contract(gate_w)
+    up_part = contract(up_w)
     hidden_act = (jax.nn.silu(gate_part) * up_part).astype(jnp.bfloat16)
     partial = jnp.einsum(
         "nh,hqd->qnd",

time: 318 us -> 325 us (1.022)
  matrix products: 11.5 us -> 19.4 us
  waiting for transfers between devices: 137 us -> 130 us
  starting transfers between devices: 36.7 us -> 40.9 us
    dot_general x1, matrix products: 2.48 us -> 8.01 us  [shards(): jnp.einsum('nh,hqd->qnd', hidden_act, down_w, preferred_element_type=jnp....]
    ppermute x1, waiting for transfers between devices: 19.7 us -> 15.1 us  [shards(): cross_q = lax.ppermute(expert_q, 'tp', CROSS_CHIP)]
    ppermute x1 -> x2, starting transfers between devices: 5.02 us -> 9.57 us  [the longest x1 4.94 us: shards(): far_q = lax.ppermute(cross_q, 'tp', ON_CHIP)]
    ppermute x1 -> x2, waiting for transfers between devices: 3.79 us -> 0.01 us  [the longest x1 0.01 us: shards(): near_q = lax.ppermute(expert_q, 'tp', ON_CHIP)]
  transfers between devices with their start and end apart: 10 -> 11, of which waited for: 10 -> 9; matrix products, arithmetic and copies ran while one was open for 12% -> 13% of each run, Pallas kernels for 0% -> 0%
where the time goes in v8:
time: 325 us; the launch traced here: 324 us
  waiting for transfers between devices  130 us (40%)
  blocking collectives  66 us (20%)
  local copies, waits for them, and re-layouts  48.9 us (15%)
  starting transfers between devices  40.9 us (13%)
  matrix products  19.4 us (6%)
  other arithmetic  17.6 us (5%)
    all_to_all x1, waiting for transfers between devices, shards(): lax.all_to_all(served, 'req', split_axis=0, concat_axis=0, tiled=True)  52 us
    all_to_all x1, blocking collectives, shards(): lax.all_to_all(outgoing, 'req', split_axis=0, concat_axis=0, tiled=True)  31.4 us
    ppermute x2, waiting for transfers between devices, tp_reduce_scatter(): lax.ppermute(summed[1].astype(wire_dtype), 'tp', CROSS_CHIP)  29.9 us
    all_to_all x1, waiting for transfers between devices, shards(): lax.all_to_all(expert_share, 'req', split_axis=0, concat_axis=0, tiled=True)  26.3 us
    all_to_all x1, blocking collectives, shards(): lax.all_to_all(request, 'req', split_axis=0, concat_axis=0, tiled=True)  22.6 us
    ppermute x1, waiting for transfers between devices, shards(): cross_q = lax.ppermute(expert_q, 'tp', CROSS_CHIP)  15.1 us
    all_gather x1, blocking collectives, shards(): return lax.all_gather(layer_q, 'tp', axis=1, tiled=True)  12 us
    dot_general x1, matrix products, shards(): jnp.einsum('nh,hqd->qnd', hidden_act, down_w, preferred_element_type=jnp....  8.01 us
  transfers between devices with their start and end apart: 11, of which 9 were waited for; matrix products, arithmetic and copies ran while one was open for 13% of the time, Pallas kernels for 0%

profile of v8, /device:TPU:1, one launch (start us, length us, event | category | flops | bytes accessed | tf_op | source)
XLA Modules:
  0.0 324.2 jit_solution(4502599243175559557)
XLA Ops:
  0.0 0.8 and_select_fusion.3
  0.8 0.7 fusion.64
  2.3 22.6 %all_to_all.27 = s32[64,1,1]{2,1,0:T(1,128)S(1)} all-to-all(s32[64,1,1]{2,1,0:T(1,128)S(1)} %copy.146), channel_id=1, replica_groups=mesh['req'=64,'tp'=4] {'req'}, dimensions={0} | all-to-all | bytes 512 | tf_op jit(solution)/shard_map/all_to_all | solution.py:131
  24.8 1.2 reduce.5
  26.1 4.0 %gather_fusion.4 = bf16[64,128,256]{2,1,0:T(8,128)(2,1)} fusion(bf16[16,128,256]{2,1,0:T(8,128)(2,1)} %bitcast.193, s32[1024]{0:T(1024)S(1)} %pad_clamp_fusion.2), kind=kCustom, calls=%fused_computation.4 | custom fusion | bytes 8388864 | tf_op jit(solution)/shard_map/gather | solution.py:132
  30.1 6.0 %all-to-all-start.1 = ((bf16[64,1,1,128,256]{4,3,2,1,0:T(8,128)(2,1)}), bf16[64,1,1,128,256]{4,3,2,1,0:T(8,128)(2,1)}, u32[]{:S(2)}, u32[]{:S(2)}) async-start(bf16[64,1,1,128,256]{4,3,2,1,0:T(8,128)(2,1)} %bitcast.192), calls=%async_computation.1 | async-start | bytes 8388608 | tf_op jit(solution)/shard_map/all_to_all | solution.py:135
  37.6 0.6 reduce.4
  39.0 0.8 reshape.960
  39.7 3.3 %fusion.74 = (bf16[1,1,2048,352]{2,3,1,0:T(8,128)(2,1)S(1)}, bf16[1,1,2048,352]{2,3,1,0:T(8,128)(2,1)}) fusion(bf16[1,2,2048,352]{2,3,1,0:T(8,128)(2,1)} %param.20), kind=kLoop, calls=%fused_computation.161 | loop fusion | bytes 5767168 | tf_op jit(solution)/shard_map/slice | solution.py:156
  43.1 1.1 reshape_squeeze.10
  44.5 4.4 %reshape_squeeze.9 = bf16[4,512,352]{1,0,2:T(4,128)(2,1)} reshape(bf16[1,1,2048,352]{2,3,1,0:T(8,128)(2,1)} %get-tuple-element.24) | data formatting | bytes 2883584 | tf_op jit(solution)/shard_map/reshape;squeeze | solution.py:155
  48.9 1.6 copy.134
  50.5 0.6 fusion.60
  51.1 1.8 gather_fusion.1
  52.9 1.8 gather_fusion
  54.7 2.9 copy.137
  57.6 2.4 copy.138
  60.0 1.1 reshape_squeeze.11
  61.7 0.6 pad_clamp_fusion.3
  62.3 2.4 gather_fusion.3
  64.7 1.9 gather_fusion.2
  66.7 1.8 reduce-window.18
  69.8 0.6 add_convert_fusion.1
  72.0 2.4 broadcast_and_fusion
  74.4 0.8 pad_add_fusion
  75.2 52.0 %all-to-all-done.1 = bf16[64,1,1,128,256]{4,3,2,1,0:T(8,128)(2,1)} async-done(((bf16[64,1,1,128,256]{4,3,2,1,0:T(8,128)(2,1)}), bf16[64,1,1,128,256]{4,3,2,1,0:T(8,128)(2,1)}, u32[]{:S(2)}, u32[]{:S(2)}) %all-to-all-start.1) | async-done | bytes 4194336 | tf_op jit(solution)/shard_map/all_to_all | solution.py:135
  127.2 4.2 %gather_fusion.5 = bf16[32,128,256]{2,1,0:T(8,128)(2,1)} fusion(bf16[64,128,256]{2,1,0:T(8,128)(2,1)} %bitcast.22, s32[1024]{0:T(1024)S(1)} %pad_clamp_fusion.1), kind=kCustom, calls=%fused_computation.5 | custom fusion | bytes 4194432 | tf_op jit(solution)/shard_map/gather | solution.py:136
  131.4 1.7 fusion.75
  133.1 1.3 fusion.77
  134.4 1.1 fusion
  135.6 1.7 fusion.7
  137.3 0.7 convolution_bitcast_fusion.4
  138.1 5.5 %collective-permute-start = (f32[2,128,512]{1,2,0:T(8,128)S(1)}, f32[2,128,512]{1,2,0:T(8,128)S(1)}, u32[]{:S(2)}, u32[]{:S(2)}) collective-permute-start(f32[2,128,512]{1,2,0:T(8,128)S(1)} %slice.135), channel_id=1, source_target_pairs={{0,1},{1,0},{2,3},{3,2},{4,5},{5,4},{6,7},{7,6},{8,9},{9,8},{10,11... | collective-permute-start | bytes 1572872 | tf_op jit(solution)/shard_map/ppermute | solution.py:76
  143.7 1.5 collective-permute-done
  145.3 2.7 collective-permute-start.1
  148.1 6.2 %collective-permute-done.1 = f32[128,512]{0,1:T(8,128)S(1)} collective-permute-done((f32[128,512]{0,1:T(8,128)S(1)}, f32[128,512]{0,1:T(8,128)S(1)}, u32[]{:S(2)}, u32[]{:S(2)}) %collective-permute-start.1) | collective-permute-done | bytes 262176 | tf_op jit(solution)/shard_map/ppermute | solution.py:78
  154.4 1.3 collective-permute-start.2
  155.8 0.8 collective-permute-done.2
  156.6 2.6 collective-permute-start.3
  159.2 0.8 dynamic_slice.7
  160.5 0.5 convolution_convert_fusion
  161.1 31.4 %all_to_all.28 = bf16[64,16,512]{2,1,0:T(8,128)(2,1)S(1)} all-to-all(bf16[64,16,512]{2,1,0:T(8,128)(2,1)S(1)} %bitcast.197), channel_id=1, replica_groups=mesh['req'=64,'tp'=4] {'req'}, dimensions={0} | all-to-all | bytes 2097152 | tf_op jit(solution)/shard_map/all_to_all | solution.py:205
  192.5 2.6 collective-permute-start.5
  195.1 4.6 %collective-permute-start.4 = (bf16[64,16,512]{2,1,0:T(8,128)(2,1)S(1)}, bf16[64,16,512]{2,1,0:T(8,128)(2,1)S(1)}, u32[]{:S(2)}, u32[]{:S(2)}) collective-permute-start(bf16[64,16,512]{2,1,0:T(8,128)(2,1)S(1)} %all_to_all.28), channel_id=1, source_target_pairs={{0,1},{1,0},{2,3},{3,2},{4,5},{5,4},{6,7},{7,6},{8,9},{9,8},{10,11... | collective-permute-start | bytes 3145736 | tf_op jit(solution)/shard_map/ppermute | solution.py:206
  199.7 15.1 %collective-permute-done.5 = bf16[64,16,512]{2,1,0:T(8,128)(2,1)S(1)} collective-permute-done((bf16[64,16,512]{2,1,0:T(8,128)(2,1)S(1)}, bf16[64,16,512]{2,1,0:T(8,128)(2,1)S(1)}, u32[]{:S(2)}, u32[]{:S(2)}) %collective-permute-start.5) | collective-permute-done | bytes 1048608 | tf_op jit(solution)/shard_map/ppermute | solution.py:207
  214.8 4.9 %collective-permute-start.6 = (bf16[64,16,512]{2,1,0:T(8,128)(2,1)S(1)}, bf16[64,16,512]{2,1,0:T(8,128)(2,1)S(1)}, u32[]{:S(2)}, u32[]{:S(2)}) collective-permute-start(bf16[64,16,512]{2,1,0:T(8,128)(2,1)S(1)} %collective-permute-done.5), channel_id=1, source_target_pairs={{0,1},{1,0},{2,3},{3,2},{4,5},{5,4},{6,7},{7,6},{8,9},{9,8},{10,11... | collective-permute-start | bytes 3145736 | tf_op jit(solution)/shard_map/ppermute | solution.py:208
  219.8 2.1 convolution_bitcast_fusion.3
  221.8 2.1 convolution_bitcast_fusion.1
  223.9 1.0 copy-done.23
  224.9 2.0 convolution_bitcast_fusion.2
  226.9 8.0 %convert_bitcast_fusion = bf16[4,1024,512]{1,2,0:T(8,128)(2,1)} fusion(bf16[352,4,512]{2,0,1:T(8,128)(2,1)S(1)} %bitcast.198, f32[1024,352]{0,1:T(8,128)} %convolution_bitcast_fusion.1, bf16[1,1024,512]{2,1,0:T(8,128)(2,1)} %bitcast.210, bf16[1,1024,512]{2,1,0:T(8,128)(2,1)} %bitcast.208, f32[1024,352]{0,1:T(8,128)} %convolution_bitcast_fusion.3, ...), kind=kOutput, calls=%fused_computation.14 | convolution fusion | flops 2220621824 | bytes 12779520 | tf_op jit(solution)/shard_map/nh,hqd->qnd/dot_general | solution.py:222
  234.9 1.9 slice.139
  237.0 4.1 %collective-permute-done.7 = bf16[2,1024,512]{1,2,0:T(8,128)(2,1)S(1)} collective-permute-done((bf16[2,1024,512]{1,2,0:T(8,128)(2,1)S(1)}, bf16[2,1024,512]{1,2,0:T(8,128)(2,1)S(1)}, u32[]{:S(2)}, u32[]{:S(2)}) %collective-permute-start.7) | collective-permute-done | bytes 2097184 | tf_op jit(solution)/shard_map/ppermute | solution.py:76
  241.1 0.9 convert_add_fusion
  242.2 2.5 collective-permute-start.8
  244.7 23.6 %collective-permute-done.8 = bf16[1024,512]{0,1:T(8,128)(2,1)S(1)} collective-permute-done((bf16[1024,512]{0,1:T(8,128)(2,1)S(1)}, bf16[1024,512]{0,1:T(8,128)(2,1)S(1)}, u32[]{:S(2)}, u32[]{:S(2)}) %collective-permute-start.8) | collective-permute-done | bytes 1048608 | tf_op jit(solution)/shard_map/ppermute | solution.py:78
  268.7 1.3 copy.152
  270.0 7.9 %all-to-all-start.3 = ((bf16[64,16,512]{2,1,0:T(8,128)(2,1)}), bf16[64,16,512]{2,1,0:T(8,128)(2,1)S(1)}, u32[]{:S(2)}, u32[]{:S(2)}) async-start(bf16[64,16,512]{2,1,0:T(8,128)(2,1)} %bitcast.62), calls=%async_computation.3 | async-start | bytes 2097152 | tf_op jit(solution)/shard_map/all_to_all | solution.py:231
  278.1 26.3 %all-to-all-done.3 = bf16[64,16,512]{2,1,0:T(8,128)(2,1)S(1)} async-done(((bf16[64,16,512]{2,1,0:T(8,128)(2,1)}), bf16[64,16,512]{2,1,0:T(8,128)(2,1)S(1)}, u32[]{:S(2)}, u32[]{:S(2)}) %all-to-all-start.3) | async-done | bytes 1048608 | tf_op jit(solution)/shard_map/all_to_all | solution.py:231
  304.4 2.7 gather_fusion.6
  307.1 1.5 reshape.974
  308.7 2.3 multiply_reduce_fusion
  311.2 12.0 %all_gather.3 = bf16[128,2048]{0,1:T(8,128)(2,1)S(1)} all-gather(bf16[128,512]{0,1:T(8,128)(2,1)S(1)} %fusion.30), channel_id=1, replica_groups=mesh['req'=64,'tp'=4] {'tp'}, dimensions={1}, use_global_device_ids=true | all-gather | bytes 655360 | tf_op jit(solution)/shard_map/all_gather | solution.py:235
  323.2 1.0 copy.154
  (113 shorter events, 7.7 us)
Async XLA Ops:
  0.0 38.4 %copy-start = (bf16[2048,512]{1,0:T(8,128)(2,1)S(1)}, bf16[2048,512]{1,0:T(8,128)(2,1)}, u32[]{:S(2)}) copy-start(bf16[2048,512]{1,0:T(8,128)(2,1)} %param.16) | copy-start | bytes 6291460
  1.7 0.5 copy-start.25
  30.1 6.0 %copy-start.13 = (s32[128,6]{0,1:T(8,128)S(1)}, s32[128,6]{0,1:T(8,128)}, u32[]{:S(2)}) copy-start(s32[128,6]{0,1:T(8,128)} %param.26) | copy-start | bytes 9220
  30.1 7.1 %copy-start.16 = (s32[1,128]{1,0:T(1,128)S(1)}, s32[1,128]{1,0:T(1,128)}, u32[]{:S(2)}) copy-start(s32[1,128]{1,0:T(1,128)} %param.22) | copy-start | bytes 1540
  30.1 8.1 %copy-start.3 = (bf16[128,2048]{1,0:T(8,128)(2,1)S(1)}, bf16[128,2048]{1,0:T(8,128)(2,1)}, u32[]{:S(2)}) copy-start(bf16[128,2048]{1,0:T(8,128)(2,1)} %param.14) | copy-start | bytes 1572868
  30.1 8.3 %copy-start.14 = (f32[2048]{0:T(1024)S(1)}, f32[2048]{0:T(1024)}, u32[]{:S(2)}) copy-start(f32[2048]{0:T(1024)} %param.15) | copy-start | bytes 24580
  30.1 97.1 %all-to-all-start.1 = ((bf16[64,1,1,128,256]{4,3,2,1,0:T(8,128)(2,1)}), bf16[64,1,1,128,256]{4,3,2,1,0:T(8,128)(2,1)}, u32[]{:S(2)}, u32[]{:S(2)}) async-start(bf16[64,1,1,128,256]{4,3,2,1,0:T(8,128)(2,1)} %bitcast.192), calls=%async_computation.1 | async-start | bytes 8388608 | tf_op jit(solution)/shard_map/all_to_all | solution.py:135
  38.4 4.6 %copy-start.19 = (f32[128]{0:T(128)}, f32[128]{0:T(128)S(1)}, u32[]{:S(2)}) copy-start(f32[128]{0:T(128)S(1)} %add_rsqrt_fusion) | copy-start | bytes 1540
  57.6 2.4 copy-start.8
  61.1 0.6 copy-start.18
  66.6 4.1 %copy-start.5 = (f32[128,4,128]{2,1,0:T(4,128)S(1)}, f32[128,4,128]{2,1,0:T(4,128)}, u32[]{:S(2)}) copy-start(f32[128,4,128]{2,1,0:T(4,128)} %reshape.960) | copy-start | bytes 786436
  66.6 4.5 %copy-start.24 = (s32[1,32]{1,0:T(1,128)S(1)}, s32[1,32]{1,0:T(1,128)}, u32[]{:S(2)}) copy-start(s32[1,32]{1,0:T(1,128)} %param.24) | copy-start | bytes 388
  66.6 4.5 %copy-start.26 = (s32[32]{0:T(128)S(1)}, s32[32]{0:T(128)}, u32[]{:S(2)}) copy-start(s32[32]{0:T(128)} %copy-done.25) | copy-start | bytes 388
  66.6 4.5 %copy-start.4 = (bf16[128,2048]{1,0:T(8,128)(2,1)S(1)}, bf16[128,2048]{1,0:T(8,128)(2,1)}, u32[]{:S(2)}) copy-start(bf16[128,2048]{1,0:T(8,128)(2,1)} %param.14) | copy-start | bytes 1572868
  66.7 4.6 %copy-start.15 = (f32[2048]{0:T(1024)S(1)}, f32[2048]{0:T(1024)}, u32[]{:S(2)}) copy-start(f32[2048]{0:T(1024)} %param.15) | copy-start | bytes 24580
  66.7 4.5 %copy-start.20 = (f32[128]{0:T(128)S(1)}, f32[128]{0:T(128)}, u32[]{:S(2)}) copy-start(f32[128]{0:T(128)} %copy-done.19) | copy-start | bytes 1540
  69.1 2.1 copy-start.21
  131.4 1.7 copy-start.12
  138.1 7.1 %collective-permute-start = (f32[2,128,512]{1,2,0:T(8,128)S(1)}, f32[2,128,512]{1,2,0:T(8,128)S(1)}, u32[]{:S(2)}, u32[]{:S(2)}) collective-permute-start(f32[2,128,512]{1,2,0:T(8,128)S(1)} %slice.135), channel_id=1, source_target_pairs={{0,1},{1,0},{2,3},{3,2},{4,5},{5,4},{6,7},{7,6},{8,9},{9,8},{10,11... | collective-permute-start | bytes 1572872 | tf_op jit(solution)/shard_map/ppermute | solution.py:76
  145.3 9.1 %collective-permute-start.1 = (f32[128,512]{0,1:T(8,128)S(1)}, f32[128,512]{0,1:T(8,128)S(1)}, u32[]{:S(2)}, u32[]{:S(2)}) collective-permute-start(f32[128,512]{0,1:T(8,128)S(1)} %slice_bitcast_fusion.1), channel_id=1, source_target_pairs={{0,2},{2,0},{1,3},{3,1},{4,6},{6,4},{5,7},{7,5},{8,10},{10,8},{9,1... | collective-permute-start | bytes 786440 | tf_op jit(solution)/shard_map/ppermute | solution.py:78
  148.1 71.6 %copy-start.7 = (bf16[4,512,352]{1,2,0:T(8,128)(2,1)S(1)}, bf16[4,512,352]{1,2,0:T(8,128)(2,1)}, u32[]{:S(2)}) copy-start(bf16[4,512,352]{1,2,0:T(8,128)(2,1)} %gather_fusion) | copy-start | bytes 4325380
  154.4 65.3 %copy-start.10 = (bf16[128,512]{0,1:T(8,128)(2,1)}, bf16[128,512]{0,1:T(8,128)(2,1)S(1)}, u32[]{:S(2)}) copy-start(bf16[128,512]{0,1:T(8,128)(2,1)S(1)} %get-tuple-element.20) | copy-start | bytes 393220
  154.4 2.1 collective-permute-start.2
  156.6 3.9 %collective-permute-start.3 = (f32[128,1]{0,1:T(1,128)S(1)}, f32[128,1]{0,1:T(1,128)S(1)}, u32[]{:S(2)}, u32[]{:S(2)}) collective-permute-start(f32[128,1]{0,1:T(1,128)S(1)} %bitcast_add_fusion.1), channel_id=1, source_target_pairs={{0,2},{2,0},{1,3},{3,1},{4,6},{6,4},{5,7},{7,5},{8,10},{10,8},{9,1... | collective-permute-start | bytes 1544 | tf_op jit(solution)/shard_map/ppermute | solution.py:85
  192.5 22.3 %collective-permute-start.5 = (bf16[64,16,512]{2,1,0:T(8,128)(2,1)S(1)}, bf16[64,16,512]{2,1,0:T(8,128)(2,1)S(1)}, u32[]{:S(2)}, u32[]{:S(2)}) collective-permute-start(bf16[64,16,512]{2,1,0:T(8,128)(2,1)S(1)} %all_to_all.28), channel_id=1, source_target_pairs={{0,2},{2,0},{1,3},{3,1},{4,6},{6,4},{5,7},{7,5},{8,10},{10,8},{9,1... | collective-permute-start | bytes 3145736 | tf_op jit(solution)/shard_map/ppermute | solution.py:207
  195.1 24.6 %collective-permute-start.4 = (bf16[64,16,512]{2,1,0:T(8,128)(2,1)S(1)}, bf16[64,16,512]{2,1,0:T(8,128)(2,1)S(1)}, u32[]{:S(2)}, u32[]{:S(2)}) collective-permute-start(bf16[64,16,512]{2,1,0:T(8,128)(2,1)S(1)} %all_to_all.28), channel_id=1, source_target_pairs={{0,1},{1,0},{2,3},{3,2},{4,5},{5,4},{6,7},{7,6},{8,9},{9,8},{10,11... | collective-permute-start | bytes 3145736 | tf_op jit(solution)/shard_map/ppermute | solution.py:206
  214.8 9.1 %copy-start.22 = (bf16[64,16,512]{2,1,0:T(8,128)(2,1)}, bf16[64,16,512]{2,1,0:T(8,128)(2,1)S(1)}, u32[]{:S(2)}) copy-start(bf16[64,16,512]{2,1,0:T(8,128)(2,1)S(1)} %collective-permute-done.5) | copy-start | bytes 3145732
  214.8 9.1 %collective-permute-start.6 = (bf16[64,16,512]{2,1,0:T(8,128)(2,1)S(1)}, bf16[64,16,512]{2,1,0:T(8,128)(2,1)S(1)}, u32[]{:S(2)}, u32[]{:S(2)}) collective-permute-start(bf16[64,16,512]{2,1,0:T(8,128)(2,1)S(1)} %collective-permute-done.5), channel_id=1, source_target_pairs={{0,1},{1,0},{2,3},{3,2},{4,5},{5,4},{6,7},{7,6},{8,9},{9,8},{10,11... | collective-permute-start | bytes 3145736 | tf_op jit(solution)/shard_map/ppermute | solution.py:208
  219.7 2.1 copy-start.6
  223.9 1.0 copy-start.23
  224.9 2.0 copy-start.9
  234.9 6.2 %copy-start.2 = (bf16[4,1024,512]{1,2,0:T(8,128)(2,1)S(1)}, bf16[4,1024,512]{1,2,0:T(8,128)(2,1)}, u32[]{:S(2)}) copy-start(bf16[4,1024,512]{1,2,0:T(8,128)(2,1)} %convert_bitcast_fusion) | copy-start | bytes 12582916
  236.8 4.2 %collective-permute-start.7 = (bf16[2,1024,512]{1,2,0:T(8,128)(2,1)S(1)}, bf16[2,1024,512]{1,2,0:T(8,128)(2,1)S(1)}, u32[]{:S(2)}, u32[]{:S(2)}) collective-permute-start(bf16[2,1024,512]{1,2,0:T(8,128)(2,1)S(1)} %slice.139), channel_id=1, source_target_pairs={{0,1},{1,0},{2,3},{3,2},{4,5},{5,4},{6,7},{7,6},{8,9},{9,8},{10,11... | collective-permute-start | bytes 6291464 | tf_op jit(solution)/shard_map/ppermute | solution.py:76
  242.2 26.2 %collective-permute-start.8 = (bf16[1024,512]{0,1:T(8,128)(2,1)S(1)}, bf16[1024,512]{0,1:T(8,128)(2,1)S(1)}, u32[]{:S(2)}, u32[]{:S(2)}) collective-permute-start(bf16[1024,512]{0,1:T(8,128)(2,1)S(1)} %fusion.19), channel_id=1, source_target_pairs={{0,2},{2,0},{1,3},{3,1},{4,6},{6,4},{5,7},{7,5},{8,10},{10,8},{9,1... | collective-permute-start | bytes 3145736 | tf_op jit(solution)/shard_map/ppermute | solution.py:78
  268.7 9.3 %copy-start.17 = (f32[128,6]{0,1:T(8,128)S(1)}, f32[128,6]{0,1:T(8,128)}, u32[]{:S(2)}) copy-start(f32[128,6]{0,1:T(8,128)} %param.27) | copy-start | bytes 9220
  270.0 34.4 %all-to-all-start.3 = ((bf16[64,16,512]{2,1,0:T(8,128)(2,1)}), bf16[64,16,512]{2,1,0:T(8,128)(2,1)S(1)}, u32[]{:S(2)}, u32[]{:S(2)}) async-start(bf16[64,16,512]{2,1,0:T(8,128)(2,1)} %bitcast.62), calls=%async_computation.3 | async-start | bytes 2097152 | tf_op jit(solution)/shard_map/all_to_all | solution.py:231
  307.1 17.1 %copy-start.1 = (bf16[2048,512]{1,0:T(8,128)(2,1)S(1)}, bf16[2048,512]{1,0:T(8,128)(2,1)}, u32[]{:S(2)}) copy-start(bf16[2048,512]{1,0:T(8,128)(2,1)} %param.16) | copy-start | bytes 6291460
  308.7 2.5 copy-start.11

commit v9 on v7

--- a/solution.py
+++ b/solution.py
@@ -220,8 +220,9 @@
         tp_reduce_scatter(partial, jnp.bfloat16).astype(jnp.bfloat16).reshape(n_req, cap_e, quarter)
     )
     results = lax.all_to_all(expert_share, "req", split_axis=0, concat_axis=0, tiled=True)
-    picked = results.reshape(-1, quarter)[assign_slot].reshape(tok_rows, topk, quarter)
-    moe_q = jnp.sum(expert_weights[:, :, None] * picked.astype(jnp.float32), axis=1)
+    slot_by_rank = assign_slot.reshape(tok_rows, topk).T.reshape(-1)
+    picked = results.reshape(-1, quarter)[slot_by_rank].reshape(topk, tok_rows, quarter)
+    moe_q = jnp.sum(expert_weights.T[:, :, None] * picked.astype(jnp.float32), axis=0)
     layer_q = (resid_wide + moe_q).astype(jnp.bfloat16)
     return lax.all_gather(layer_q, "tp", axis=1, tiled=True)
 

time: 318 us -> 316 us (level)
  no operation moved by 1% of the time
where the time goes in v9:
time: 316 us
  waiting for transfers between devices  137 us (43%)
  blocking collectives  66.4 us (21%)
  local copies, waits for them, and re-layouts  45.5 us (14%)
  starting transfers between devices  36.7 us (12%)
  other arithmetic  17 us (5%)
  matrix products  11.6 us (4%)
    all_to_all x1, waiting for transfers between devices, shards(): lax.all_to_all(served, 'req', split_axis=0, concat_axis=0, tiled=True)  51.7 us
    all_to_all x1, blocking collectives, shards(): lax.all_to_all(outgoing, 'req', split_axis=0, concat_axis=0, tiled=True)  31.4 us
    ppermute x2, waiting for transfers between devices, tp_reduce_scatter(): lax.ppermute(summed[1].astype(wire_dtype), 'tp', CROSS_CHIP)  29.6 us
    all_to_all x1, waiting for transfers between devices, shards(): lax.all_to_all(expert_share, 'req', split_axis=0, concat_axis=0, tiled=True)  25.6 us
    all_to_all x1, blocking collectives, shards(): lax.all_to_all(request, 'req', split_axis=0, concat_axis=0, tiled=True)  22.6 us
    ppermute x1, waiting for transfers between devices, shards(): cross_q = lax.ppermute(expert_q, 'tp', CROSS_CHIP)  19.7 us
    all_gather x1, blocking collectives, shards(): return lax.all_gather(layer_q, 'tp', axis=1, tiled=True)  12.5 us
    all_to_all x1, starting transfers between devices, shards(): lax.all_to_all(expert_share, 'req', split_axis=0, concat_axis=0, tiled=True)  7.94 us
  transfers between devices with their start and end apart: 10, of which 10 were waited for; matrix products, arithmetic and copies ran while one was open for 12% of the time, Pallas kernels for 0%

profile of v9, /device:TPU:1, one launch (start us, length us, event | category | flops | bytes accessed | tf_op | source)
XLA Modules:
  0.0 315.6 jit_solution(15022706037432842682)
XLA Ops:
  0.0 0.8 and_select_fusion.3
  0.8 0.7 fusion.64
  2.3 22.6 %all_to_all.27 = s32[64,1,1]{2,1,0:T(1,128)S(1)} all-to-all(s32[64,1,1]{2,1,0:T(1,128)S(1)} %copy.145), channel_id=1, replica_groups=mesh['req'=64,'tp'=4] {'req'}, dimensions={0} | all-to-all | bytes 512 | tf_op jit(solution)/shard_map/all_to_all | solution.py:131
  24.9 1.2 reduce.5
  26.1 4.0 %gather_fusion.4 = bf16[64,128,256]{2,1,0:T(8,128)(2,1)} fusion(bf16[16,128,256]{2,1,0:T(8,128)(2,1)} %bitcast.194, s32[1024]{0:T(1024)S(1)} %pad_clamp_fusion.2), kind=kCustom, calls=%fused_computation.4 | custom fusion | bytes 8388864 | tf_op jit(solution)/shard_map/gather | solution.py:132
  30.1 6.0 %all-to-all-start.1 = ((bf16[64,1,1,128,256]{4,3,2,1,0:T(8,128)(2,1)}), bf16[64,1,1,128,256]{4,3,2,1,0:T(8,128)(2,1)}, u32[]{:S(2)}, u32[]{:S(2)}) async-start(bf16[64,1,1,128,256]{4,3,2,1,0:T(8,128)(2,1)} %bitcast.193), calls=%async_computation.1 | async-start | bytes 8388608 | tf_op jit(solution)/shard_map/all_to_all | solution.py:135
  37.6 0.7 reduce.4
  38.6 0.5 fusion.37
  39.1 0.8 reshape.990
  39.9 3.4 %fusion.71 = (bf16[1,1,2048,352]{2,3,1,0:T(8,128)(2,1)S(1)}, bf16[1,1,2048,352]{2,3,1,0:T(8,128)(2,1)}) fusion(bf16[1,2,2048,352]{2,3,1,0:T(8,128)(2,1)} %param.20), kind=kLoop, calls=%fused_computation.156 | loop fusion | bytes 5767168 | tf_op jit(solution)/shard_map/slice | solution.py:156
  43.2 1.1 reshape_squeeze.10
  44.6 4.4 %reshape_squeeze.9 = bf16[4,512,352]{1,0,2:T(4,128)(2,1)} reshape(bf16[1,1,2048,352]{2,3,1,0:T(8,128)(2,1)} %get-tuple-element.24) | data formatting | bytes 2883584 | tf_op jit(solution)/shard_map/reshape;squeeze | solution.py:155
  49.0 1.6 copy.133
  50.7 0.7 fusion.60
  51.3 1.8 gather_fusion.1
  53.1 1.8 gather_fusion
  54.9 2.9 copy.136
  57.8 2.4 copy.137
  60.2 1.1 reshape_squeeze.11
  62.0 0.6 pad_clamp_fusion.3
  62.6 2.4 gather_fusion.3
  65.0 2.0 gather_fusion.2
  67.0 1.8 reduce-window.18
  69.4 0.5 fusion.3
  70.0 0.7 add_convert_fusion.1
  72.4 2.4 broadcast_and_fusion
  74.7 0.8 pad_add_fusion
  75.6 51.7 %all-to-all-done.1 = bf16[64,1,1,128,256]{4,3,2,1,0:T(8,128)(2,1)} async-done(((bf16[64,1,1,128,256]{4,3,2,1,0:T(8,128)(2,1)}), bf16[64,1,1,128,256]{4,3,2,1,0:T(8,128)(2,1)}, u32[]{:S(2)}, u32[]{:S(2)}) %all-to-all-start.1) | async-done | bytes 4194336 | tf_op jit(solution)/shard_map/all_to_all | solution.py:135
  127.2 4.2 %gather_fusion.5 = bf16[32,128,256]{2,1,0:T(8,128)(2,1)} fusion(bf16[64,128,256]{2,1,0:T(8,128)(2,1)} %bitcast.22, s32[1024]{0:T(1024)S(1)} %pad_clamp_fusion.1), kind=kCustom, calls=%fused_computation.5 | custom fusion | bytes 4194432 | tf_op jit(solution)/shard_map/gather | solution.py:136
  131.4 1.7 fusion.72
  133.2 1.3 fusion.74
  134.5 1.1 fusion
  135.6 1.7 fusion.11
  137.4 0.7 convolution_bitcast_fusion
  138.2 5.5 %collective-permute-start = (f32[2,128,512]{1,2,0:T(8,128)S(1)}, f32[2,128,512]{1,2,0:T(8,128)S(1)}, u32[]{:S(2)}, u32[]{:S(2)}) collective-permute-start(f32[2,128,512]{1,2,0:T(8,128)S(1)} %slice.119), channel_id=1, source_target_pairs={{0,1},{1,0},{2,3},{3,2},{4,5},{5,4},{6,7},{7,6},{8,9},{9,8},{10,11... | collective-permute-start | bytes 1572872 | tf_op jit(solution)/shard_map/ppermute | solution.py:76
  143.7 1.5 collective-permute-done
  145.3 2.7 collective-permute-start.1
  148.2 6.2 %collective-permute-done.1 = f32[128,512]{0,1:T(8,128)S(1)} collective-permute-done((f32[128,512]{0,1:T(8,128)S(1)}, f32[128,512]{0,1:T(8,128)S(1)}, u32[]{:S(2)}, u32[]{:S(2)}) %collective-permute-start.1) | collective-permute-done | bytes 262176 | tf_op jit(solution)/shard_map/ppermute | solution.py:78
  154.5 1.3 collective-permute-start.2
  155.8 0.8 collective-permute-done.2
  156.6 2.6 collective-permute-start.3
  159.2 0.8 dynamic_slice.7
  160.0 0.5 collective-permute-done.3
  160.6 0.5 convolution_convert_fusion
  161.1 31.4 %all_to_all.28 = bf16[64,16,512]{2,1,0:T(8,128)(2,1)S(1)} all-to-all(bf16[64,16,512]{2,1,0:T(8,128)(2,1)S(1)} %bitcast.198), channel_id=1, replica_groups=mesh['req'=64,'tp'=4] {'req'}, dimensions={0} | all-to-all | bytes 2097152 | tf_op jit(solution)/shard_map/all_to_all | solution.py:205
  192.5 2.6 collective-permute-start.4
  195.1 19.7 %collective-permute-done.4 = bf16[64,16,512]{2,1,0:T(8,128)(2,1)S(1)} collective-permute-done((bf16[64,16,512]{2,1,0:T(8,128)(2,1)S(1)}, bf16[64,16,512]{2,1,0:T(8,128)(2,1)S(1)}, u32[]{:S(2)}, u32[]{:S(2)}) %collective-permute-start.4) | collective-permute-done | bytes 1048608 | tf_op jit(solution)/shard_map/ppermute | solution.py:206
  215.0 5.0 %collective-permute-start.5 = (bf16[2,64,16,512]{3,2,1,0:T(8,128)(2,1)S(1)}, bf16[2,64,16,512]{3,2,1,0:T(8,128)(2,1)S(1)}, u32[]{:S(2)}, u32[]{:S(2)}) collective-permute-start(bf16[2,64,16,512]{3,2,1,0:T(8,128)(2,1)S(1)} %pad_maximum_fusion.1), channel_id=1, source_target_pairs={{0,1},{1,0},{2,3},{3,2},{4,5},{5,4},{6,7},{7,6},{8,9},{9,8},{10,11... | collective-permute-start | bytes 6291464 | tf_op jit(solution)/shard_map/ppermute | solution.py:208
  220.0 3.8 %collective-permute-done.5 = bf16[2,64,16,512]{3,2,1,0:T(8,128)(2,1)S(1)} collective-permute-done((bf16[2,64,16,512]{3,2,1,0:T(8,128)(2,1)S(1)}, bf16[2,64,16,512]{3,2,1,0:T(8,128)(2,1)S(1)}, u32[]{:S(2)}, u32[]{:S(2)}) %collective-permute-start.5) | collective-permute-done | bytes 2097184 | tf_op jit(solution)/shard_map/ppermute | solution.py:208
  223.8 1.9 fusion.9
  225.8 2.0 fusion.10
  227.8 2.5 convert_bitcast_fusion
  230.5 0.5 collective-permute-start.6
  230.9 3.8 %collective-permute-done.6 = bf16[2,1024,512]{1,2,0:T(8,128)(2,1)S(1)} collective-permute-done((bf16[2,1024,512]{1,2,0:T(8,128)(2,1)S(1)}, bf16[2,1024,512]{1,2,0:T(8,128)(2,1)S(1)}, u32[]{:S(2)}, u32[]{:S(2)}) %collective-permute-start.6) | collective-permute-done | bytes 2097184 | tf_op jit(solution)/shard_map/ppermute | solution.py:76
  234.7 0.9 convert_add_fusion
  235.8 2.5 collective-permute-start.7
  238.3 23.4 %collective-permute-done.7 = bf16[1024,512]{0,1:T(8,128)(2,1)S(1)} collective-permute-done((bf16[1024,512]{0,1:T(8,128)(2,1)S(1)}, bf16[1024,512]{0,1:T(8,128)(2,1)S(1)}, u32[]{:S(2)}, u32[]{:S(2)}) %collective-permute-start.7) | collective-permute-done | bytes 1048608 | tf_op jit(solution)/shard_map/ppermute | solution.py:78
  262.1 1.3 copy.150
  263.4 7.9 %all-to-all-start.3 = ((bf16[64,16,512]{2,1,0:T(8,128)(2,1)}), bf16[64,16,512]{2,1,0:T(8,128)(2,1)S(1)}, u32[]{:S(2)}, u32[]{:S(2)}) async-start(bf16[64,16,512]{2,1,0:T(8,128)(2,1)} %bitcast.62), calls=%async_computation.3 | async-start | bytes 2097152 | tf_op jit(solution)/shard_map/all_to_all | solution.py:222
  271.6 25.6 %all-to-all-done.3 = bf16[64,16,512]{2,1,0:T(8,128)(2,1)S(1)} async-done(((bf16[64,16,512]{2,1,0:T(8,128)(2,1)}), bf16[64,16,512]{2,1,0:T(8,128)(2,1)S(1)}, u32[]{:S(2)}, u32[]{:S(2)}) %all-to-all-start.3) | async-done | bytes 1048608 | tf_op jit(solution)/shard_map/all_to_all | solution.py:222
  297.2 3.3 %gather_fusion.6 = bf16[768,512]{1,0:T(8,128)(2,1)} fusion(bf16[1024,512]{1,0:T(8,128)(2,1)S(1)} %bitcast.192, s32[1024]{0:T(1024)S(1)} %pad_clamp_fusion), kind=kCustom, calls=%fused_computation.6 | custom fusion | bytes 1575936 | tf_op jit(solution)/shard_map/gather | solution.py:224
  300.5 1.4 fusion.8
  302.1 12.5 %all_gather.3 = bf16[128,2048]{0,1:T(8,128)(2,1)S(1)} all-gather(bf16[128,512]{0,1:T(8,128)(2,1)S(1)} %fusion.29), channel_id=1, replica_groups=mesh['req'=64,'tp'=4] {'tp'}, dimensions={1}, use_global_device_ids=true | all-gather | bytes 655360 | tf_op jit(solution)/shard_map/all_gather | solution.py:227
  314.6 1.0 copy.153
  (101 shorter events, 6.6 us)
Async XLA Ops:
  0.0 38.5 %copy-start = (bf16[2048,512]{1,0:T(8,128)(2,1)S(1)}, bf16[2048,512]{1,0:T(8,128)(2,1)}, u32[]{:S(2)}) copy-start(bf16[2048,512]{1,0:T(8,128)(2,1)} %param.16) | copy-start | bytes 6291460
  1.7 0.6 copy-start.20
  30.1 6.0 %copy-start.10 = (s32[128,6]{0,1:T(8,128)S(1)}, s32[128,6]{0,1:T(8,128)}, u32[]{:S(2)}) copy-start(s32[128,6]{0,1:T(8,128)} %param.26) | copy-start | bytes 9220
  30.1 7.1 %copy-start.13 = (s32[1,128]{1,0:T(1,128)S(1)}, s32[1,128]{1,0:T(1,128)}, u32[]{:S(2)}) copy-start(s32[1,128]{1,0:T(1,128)} %param.22) | copy-start | bytes 1540
  30.1 8.2 %copy-start.2 = (bf16[128,2048]{1,0:T(8,128)(2,1)S(1)}, bf16[128,2048]{1,0:T(8,128)(2,1)}, u32[]{:S(2)}) copy-start(bf16[128,2048]{1,0:T(8,128)(2,1)} %param.14) | copy-start | bytes 1572868
  30.1 8.4 %copy-start.11 = (f32[2048]{0:T(1024)S(1)}, f32[2048]{0:T(1024)}, u32[]{:S(2)}) copy-start(f32[2048]{0:T(1024)} %param.15) | copy-start | bytes 24580
  30.1 97.1 %all-to-all-start.1 = ((bf16[64,1,1,128,256]{4,3,2,1,0:T(8,128)(2,1)}), bf16[64,1,1,128,256]{4,3,2,1,0:T(8,128)(2,1)}, u32[]{:S(2)}, u32[]{:S(2)}) async-start(bf16[64,1,1,128,256]{4,3,2,1,0:T(8,128)(2,1)} %bitcast.193), calls=%async_computation.1 | async-start | bytes 8388608 | tf_op jit(solution)/shard_map/all_to_all | solution.py:135
  38.6 4.7 %copy-start.16 = (f32[128]{0:T(128)}, f32[128]{0:T(128)S(1)}, u32[]{:S(2)}) copy-start(f32[128]{0:T(128)S(1)} %add_rsqrt_fusion) | copy-start | bytes 1540
  57.7 2.4 copy-start.7
  61.3 0.7 copy-start.15
  66.9 4.1 %copy-start.4 = (f32[128,4,128]{2,1,0:T(4,128)S(1)}, f32[128,4,128]{2,1,0:T(4,128)}, u32[]{:S(2)}) copy-start(f32[128,4,128]{2,1,0:T(4,128)} %reshape.990) | copy-start | bytes 786436
  66.9 4.6 %copy-start.19 = (s32[1,32]{1,0:T(1,128)S(1)}, s32[1,32]{1,0:T(1,128)}, u32[]{:S(2)}) copy-start(s32[1,32]{1,0:T(1,128)} %param.24) | copy-start | bytes 388
  66.9 4.6 %copy-start.21 = (s32[32]{0:T(128)S(1)}, s32[32]{0:T(128)}, u32[]{:S(2)}) copy-start(s32[32]{0:T(128)} %copy-done.20) | copy-start | bytes 388
  66.9 4.6 %copy-start.3 = (bf16[128,2048]{1,0:T(8,128)(2,1)S(1)}, bf16[128,2048]{1,0:T(8,128)(2,1)}, u32[]{:S(2)}) copy-start(bf16[128,2048]{1,0:T(8,128)(2,1)} %param.14) | copy-start | bytes 1572868
  66.9 4.6 %copy-start.12 = (f32[2048]{0:T(1024)S(1)}, f32[2048]{0:T(1024)}, u32[]{:S(2)}) copy-start(f32[2048]{0:T(1024)} %param.15) | copy-start | bytes 24580
  66.9 4.6 %copy-start.17 = (f32[128]{0:T(128)S(1)}, f32[128]{0:T(128)}, u32[]{:S(2)}) copy-start(f32[128]{0:T(128)} %copy-done.16) | copy-start | bytes 1540
  69.4 2.2 copy-start.18
  131.4 1.7 copy-start.9
  138.2 7.1 %collective-permute-start = (f32[2,128,512]{1,2,0:T(8,128)S(1)}, f32[2,128,512]{1,2,0:T(8,128)S(1)}, u32[]{:S(2)}, u32[]{:S(2)}) collective-permute-start(f32[2,128,512]{1,2,0:T(8,128)S(1)} %slice.119), channel_id=1, source_target_pairs={{0,1},{1,0},{2,3},{3,2},{4,5},{5,4},{6,7},{7,6},{8,9},{9,8},{10,11... | collective-permute-start | bytes 1572872 | tf_op jit(solution)/shard_map/ppermute | solution.py:76
  145.3 9.1 %collective-permute-start.1 = (f32[128,512]{0,1:T(8,128)S(1)}, f32[128,512]{0,1:T(8,128)S(1)}, u32[]{:S(2)}, u32[]{:S(2)}) collective-permute-start(f32[128,512]{0,1:T(8,128)S(1)} %slice_bitcast_fusion.1), channel_id=1, source_target_pairs={{0,2},{2,0},{1,3},{3,1},{4,6},{6,4},{5,7},{7,5},{8,10},{10,8},{9,1... | collective-permute-start | bytes 786440 | tf_op jit(solution)/shard_map/ppermute | solution.py:78
  154.5 2.1 collective-permute-start.2
  156.6 3.9 %collective-permute-start.3 = (f32[128,1]{0,1:T(1,128)S(1)}, f32[128,1]{0,1:T(1,128)S(1)}, u32[]{:S(2)}, u32[]{:S(2)}) collective-permute-start(f32[128,1]{0,1:T(1,128)S(1)} %bitcast_add_fusion.1), channel_id=1, source_target_pairs={{0,2},{2,0},{1,3},{3,1},{4,6},{6,4},{5,7},{7,5},{8,10},{10,8},{9,1... | collective-permute-start | bytes 1544 | tf_op jit(solution)/shard_map/ppermute | solution.py:85
  192.5 22.3 %collective-permute-start.4 = (bf16[64,16,512]{2,1,0:T(8,128)(2,1)S(1)}, bf16[64,16,512]{2,1,0:T(8,128)(2,1)S(1)}, u32[]{:S(2)}, u32[]{:S(2)}) collective-permute-start(bf16[64,16,512]{2,1,0:T(8,128)(2,1)S(1)} %all_to_all.28), channel_id=1, source_target_pairs={{0,2},{2,0},{1,3},{3,1},{4,6},{6,4},{5,7},{7,5},{8,10},{10,8},{9,1... | collective-permute-start | bytes 3145736 | tf_op jit(solution)/shard_map/ppermute | solution.py:206
  214.8 9.0 %copy-start.6 = (bf16[4,512,352]{1,2,0:T(8,128)(2,1)S(1)}, bf16[4,512,352]{1,2,0:T(8,128)(2,1)}, u32[]{:S(2)}) copy-start(bf16[4,512,352]{1,2,0:T(8,128)(2,1)} %gather_fusion) | copy-start | bytes 4325380
  215.0 8.8 %collective-permute-start.5 = (bf16[2,64,16,512]{3,2,1,0:T(8,128)(2,1)S(1)}, bf16[2,64,16,512]{3,2,1,0:T(8,128)(2,1)S(1)}, u32[]{:S(2)}, u32[]{:S(2)}) collective-permute-start(bf16[2,64,16,512]{3,2,1,0:T(8,128)(2,1)S(1)} %pad_maximum_fusion.1), channel_id=1, source_target_pairs={{0,1},{1,0},{2,3},{3,2},{4,5},{5,4},{6,7},{7,6},{8,9},{9,8},{10,11... | collective-permute-start | bytes 6291464 | tf_op jit(solution)/shard_map/ppermute | solution.py:208
  223.8 2.0 copy-start.5
  225.8 2.0 copy-start.8
  230.5 4.2 %collective-permute-start.6 = (bf16[2,1024,512]{1,2,0:T(8,128)(2,1)S(1)}, bf16[2,1024,512]{1,2,0:T(8,128)(2,1)S(1)}, u32[]{:S(2)}, u32[]{:S(2)}) collective-permute-start(bf16[2,1024,512]{1,2,0:T(8,128)(2,1)S(1)} %slice.123), channel_id=1, source_target_pairs={{0,1},{1,0},{2,3},{3,2},{4,5},{5,4},{6,7},{7,6},{8,9},{9,8},{10,11... | collective-permute-start | bytes 6291464 | tf_op jit(solution)/shard_map/ppermute | solution.py:76
  235.8 25.9 %collective-permute-start.7 = (bf16[1024,512]{0,1:T(8,128)(2,1)S(1)}, bf16[1024,512]{0,1:T(8,128)(2,1)S(1)}, u32[]{:S(2)}, u32[]{:S(2)}) collective-permute-start(bf16[1024,512]{0,1:T(8,128)(2,1)S(1)} %fusion.23), channel_id=1, source_target_pairs={{0,2},{2,0},{1,3},{3,1},{4,6},{6,4},{5,7},{7,5},{8,10},{10,8},{9,1... | collective-permute-start | bytes 3145736 | tf_op jit(solution)/shard_map/ppermute | solution.py:78
  263.4 33.8 %all-to-all-start.3 = ((bf16[64,16,512]{2,1,0:T(8,128)(2,1)}), bf16[64,16,512]{2,1,0:T(8,128)(2,1)S(1)}, u32[]{:S(2)}, u32[]{:S(2)}) async-start(bf16[64,16,512]{2,1,0:T(8,128)(2,1)} %bitcast.62), calls=%async_computation.3 | async-start | bytes 2097152 | tf_op jit(solution)/shard_map/all_to_all | solution.py:222
  297.2 3.3 %copy-start.14 = (f32[128,6]{0,1:T(8,128)S(1)}, f32[128,6]{0,1:T(8,128)}, u32[]{:S(2)}) copy-start(f32[128,6]{0,1:T(8,128)} %param.27) | copy-start | bytes 9220
  297.2 18.4 %copy-start.1 = (bf16[2048,512]{1,0:T(8,128)(2,1)S(1)}, bf16[2048,512]{1,0:T(8,128)(2,1)}, u32[]{:S(2)}) copy-start(bf16[2048,512]{1,0:T(8,128)(2,1)} %param.16) | copy-start | bytes 6291460

commit v10 on v9

--- a/solution.py
+++ b/solution.py
@@ -211,13 +211,18 @@
     up_part = jnp.einsum("qnd,qdh->nh", expert_in, up_w, preferred_element_type=jnp.float32)
     hidden_act = (jax.nn.silu(gate_part) * up_part).astype(jnp.bfloat16)
     partial = jnp.einsum(
-        "nh,hqd->qnd",
+        "nh,hqd->nqd",
         hidden_act,
         down_w,
         preferred_element_type=jnp.float32,
     ).astype(jnp.bfloat16)
+    got = lax.ppermute(partial[:, :2], "tp", ON_CHIP)
+    chip_sum = partial[:, 2:].astype(jnp.float32) + got.astype(jnp.float32)
+    from_cross = lax.ppermute(chip_sum[:, 1].astype(jnp.bfloat16), "tp", CROSS_CHIP)
     expert_share = (
-        tp_reduce_scatter(partial, jnp.bfloat16).astype(jnp.bfloat16).reshape(n_req, cap_e, quarter)
+        (chip_sum[:, 0] + from_cross.astype(jnp.float32))
+        .astype(jnp.bfloat16)
+        .reshape(n_req, cap_e, quarter)
     )
     results = lax.all_to_all(expert_share, "req", split_axis=0, concat_axis=0, tiled=True)
     slot_by_rank = assign_slot.reshape(tok_rows, topk).T.reshape(-1)

time: 316 us -> 316 us (level)
    ppermute x0 -> x2, waiting for transfers between devices: none -> 27.2 us  [the longest x1 23.4 us: shards(): lax.ppermute(chip_sum[:, 1].astype(jnp.bfloat16), 'tp', CROSS_CHIP)]
    ppermute x2 -> x1, waiting for transfers between devices: 29.6 us -> 6.24 us  [tp_reduce_scatter(): lax.ppermute(summed[1].astype(wire_dtype), 'tp', CROSS_CHIP)]
    ppermute x2 -> x1, waiting for transfers between devices: 5.33 us -> 1.54 us  [tp_reduce_scatter(): got = lax.ppermute(parts[:2], 'tp', ON_CHIP)]
where the time goes in v10:
time: 316 us; the launch traced here: 315 us
  waiting for transfers between devices  137 us (43%)
  blocking collectives  66.4 us (21%)
  local copies, waits for them, and re-layouts  44.1 us (14%)
  starting transfers between devices  36.7 us (12%)
  other arithmetic  17.8 us (6%)
  matrix products  11.5 us (4%)
    all_to_all x1, waiting for transfers between devices, shards(): lax.all_to_all(served, 'req', split_axis=0, concat_axis=0, tiled=True)  51.7 us
    all_to_all x1, blocking collectives, shards(): lax.all_to_all(outgoing, 'req', split_axis=0, concat_axis=0, tiled=True)  31.4 us
    all_to_all x1, waiting for transfers between devices, shards(): lax.all_to_all(expert_share, 'req', split_axis=0, concat_axis=0, tiled=True)  25.6 us
    ppermute x1, waiting for transfers between devices, shards(): lax.ppermute(chip_sum[:, 1].astype(jnp.bfloat16), 'tp', CROSS_CHIP)  23.4 us
    all_to_all x1, blocking collectives, shards(): lax.all_to_all(request, 'req', split_axis=0, concat_axis=0, tiled=True)  22.6 us
    ppermute x1, waiting for transfers between devices, shards(): cross_q = lax.ppermute(expert_q, 'tp', CROSS_CHIP)  19.7 us
    all_gather x1, blocking collectives, shards(): return lax.all_gather(layer_q, 'tp', axis=1, tiled=True)  12.5 us
    all_to_all x1, starting transfers between devices, shards(): lax.all_to_all(expert_share, 'req', split_axis=0, concat_axis=0, tiled=True)  7.93 us
  transfers between devices with their start and end apart: 10, of which 10 were waited for; matrix products, arithmetic and copies ran while one was open for 12% of the time, Pallas kernels for 0%

profile of v10, /device:TPU:1, one launch (start us, length us, event | category | flops | bytes accessed | tf_op | source)
XLA Modules:
  0.0 314.9 jit_solution(16057489309633619217)
XLA Ops:
  0.0 0.8 and_select_fusion.3
  0.8 0.7 fusion.64
  1.8 0.5 copy-done.20
  2.3 22.6 %all_to_all.27 = s32[64,1,1]{2,1,0:T(1,128)S(1)} all-to-all(s32[64,1,1]{2,1,0:T(1,128)S(1)} %copy.139), channel_id=1, replica_groups=mesh['req'=64,'tp'=4] {'req'}, dimensions={0} | all-to-all | bytes 512 | tf_op jit(solution)/shard_map/all_to_all | solution.py:131
  24.9 1.2 reduce.5
  26.1 4.0 %gather_fusion.4 = bf16[64,128,256]{2,1,0:T(8,128)(2,1)} fusion(bf16[16,128,256]{2,1,0:T(8,128)(2,1)} %bitcast.192, s32[1024]{0:T(1024)S(1)} %pad_clamp_fusion.2), kind=kCustom, calls=%fused_computation.4 | custom fusion | bytes 8388864 | tf_op jit(solution)/shard_map/gather | solution.py:132
  30.1 6.0 %all-to-all-start.1 = ((bf16[64,1,1,128,256]{4,3,2,1,0:T(8,128)(2,1)}), bf16[64,1,1,128,256]{4,3,2,1,0:T(8,128)(2,1)}, u32[]{:S(2)}, u32[]{:S(2)}) async-start(bf16[64,1,1,128,256]{4,3,2,1,0:T(8,128)(2,1)} %bitcast.191), calls=%async_computation.1 | async-start | bytes 8388608 | tf_op jit(solution)/shard_map/all_to_all | solution.py:135
  37.6 0.7 reduce.4
  38.6 0.5 fusion.37
  39.1 0.8 reshape.990
  39.9 3.4 %fusion.71 = (bf16[1,1,2048,352]{2,3,1,0:T(8,128)(2,1)S(1)}, bf16[1,1,2048,352]{2,3,1,0:T(8,128)(2,1)}) fusion(bf16[1,2,2048,352]{2,3,1,0:T(8,128)(2,1)} %param.20), kind=kLoop, calls=%fused_computation.156 | loop fusion | bytes 5767168 | tf_op jit(solution)/shard_map/slice | solution.py:156
  43.2 1.1 reshape_squeeze.10
  44.6 4.4 %reshape_squeeze.9 = bf16[4,512,352]{1,0,2:T(4,128)(2,1)} reshape(bf16[1,1,2048,352]{2,3,1,0:T(8,128)(2,1)} %get-tuple-element.24) | data formatting | bytes 2883584 | tf_op jit(solution)/shard_map/reshape;squeeze | solution.py:155
  49.0 1.6 copy.127
  50.7 0.7 fusion.60
  51.3 1.8 gather_fusion.1
  53.1 1.8 gather_fusion
  54.9 2.9 copy.130
  57.8 2.4 copy.131
  60.2 1.1 reshape_squeeze.11
  62.0 0.6 pad_clamp_fusion.3
  62.6 2.4 gather_fusion.3
  65.0 2.0 gather_fusion.2
  67.0 1.8 reduce-window.18
  69.4 0.5 fusion.3
  70.0 0.7 add_convert_fusion.1
  72.4 2.4 broadcast_and_fusion
  74.7 0.8 pad_add_fusion
  75.6 51.7 %all-to-all-done.1 = bf16[64,1,1,128,256]{4,3,2,1,0:T(8,128)(2,1)} async-done(((bf16[64,1,1,128,256]{4,3,2,1,0:T(8,128)(2,1)}), bf16[64,1,1,128,256]{4,3,2,1,0:T(8,128)(2,1)}, u32[]{:S(2)}, u32[]{:S(2)}) %all-to-all-start.1) | async-done | bytes 4194336 | tf_op jit(solution)/shard_map/all_to_all | solution.py:135
  127.2 4.2 %gather_fusion.5 = bf16[32,128,256]{2,1,0:T(8,128)(2,1)} fusion(bf16[64,128,256]{2,1,0:T(8,128)(2,1)} %bitcast.22, s32[1024]{0:T(1024)S(1)} %pad_clamp_fusion.1), kind=kCustom, calls=%fused_computation.5 | custom fusion | bytes 4194432 | tf_op jit(solution)/shard_map/gather | solution.py:136
  131.4 1.7 fusion.72
  133.2 1.3 fusion.74
  134.5 1.1 fusion
  135.6 1.7 fusion.11
  137.4 0.7 convolution_bitcast_fusion
  138.2 5.5 %collective-permute-start = (f32[2,128,512]{1,2,0:T(8,128)S(1)}, f32[2,128,512]{1,2,0:T(8,128)S(1)}, u32[]{:S(2)}, u32[]{:S(2)}) collective-permute-start(f32[2,128,512]{1,2,0:T(8,128)S(1)} %slice.119), channel_id=1, source_target_pairs={{0,1},{1,0},{2,3},{3,2},{4,5},{5,4},{6,7},{7,6},{8,9},{9,8},{10,11... | collective-permute-start | bytes 1572872 | tf_op jit(solution)/shard_map/ppermute | solution.py:76
  143.7 1.5 collective-permute-done
  145.3 2.7 collective-permute-start.1
  148.2 6.2 %collective-permute-done.1 = f32[128,512]{0,1:T(8,128)S(1)} collective-permute-done((f32[128,512]{0,1:T(8,128)S(1)}, f32[128,512]{0,1:T(8,128)S(1)}, u32[]{:S(2)}, u32[]{:S(2)}) %collective-permute-start.1) | collective-permute-done | bytes 262176 | tf_op jit(solution)/shard_map/ppermute | solution.py:78
  154.5 1.3 collective-permute-start.2
  155.8 0.8 collective-permute-done.2
  156.6 2.6 collective-permute-start.3
  159.2 0.8 dynamic_slice.7
  160.0 0.5 collective-permute-done.3
  160.6 0.5 convolution_convert_fusion.1
  161.1 31.4 %all_to_all.28 = bf16[64,16,512]{2,1,0:T(8,128)(2,1)S(1)} all-to-all(bf16[64,16,512]{2,1,0:T(8,128)(2,1)S(1)} %bitcast.196), channel_id=1, replica_groups=mesh['req'=64,'tp'=4] {'req'}, dimensions={0} | all-to-all | bytes 2097152 | tf_op jit(solution)/shard_map/all_to_all | solution.py:205
  192.5 2.6 collective-permute-start.4
  195.1 19.7 %collective-permute-done.4 = bf16[64,16,512]{2,1,0:T(8,128)(2,1)S(1)} collective-permute-done((bf16[64,16,512]{2,1,0:T(8,128)(2,1)S(1)}, bf16[64,16,512]{2,1,0:T(8,128)(2,1)S(1)}, u32[]{:S(2)}, u32[]{:S(2)}) %collective-permute-start.4) | collective-permute-done | bytes 1048608 | tf_op jit(solution)/shard_map/ppermute | solution.py:206
  215.0 5.0 %collective-permute-start.5 = (bf16[2,64,16,512]{3,2,1,0:T(8,128)(2,1)S(1)}, bf16[2,64,16,512]{3,2,1,0:T(8,128)(2,1)S(1)}, u32[]{:S(2)}, u32[]{:S(2)}) collective-permute-start(bf16[2,64,16,512]{3,2,1,0:T(8,128)(2,1)S(1)} %pad_maximum_fusion.1), channel_id=1, source_target_pairs={{0,1},{1,0},{2,3},{3,2},{4,5},{5,4},{6,7},{7,6},{8,9},{9,8},{10,11... | collective-permute-start | bytes 6291464 | tf_op jit(solution)/shard_map/ppermute | solution.py:208
  220.0 3.8 %collective-permute-done.5 = bf16[2,64,16,512]{3,2,1,0:T(8,128)(2,1)S(1)} collective-permute-done((bf16[2,64,16,512]{3,2,1,0:T(8,128)(2,1)S(1)}, bf16[2,64,16,512]{3,2,1,0:T(8,128)(2,1)S(1)}, u32[]{:S(2)}, u32[]{:S(2)}) %collective-permute-start.5) | collective-permute-done | bytes 2097184 | tf_op jit(solution)/shard_map/ppermute | solution.py:208
  223.8 1.9 fusion.9
  225.8 2.0 fusion.10
  227.8 2.5 convolution_convert_fusion
  230.9 3.8 %collective-permute-done.6 = bf16[1024,2,512]{2,0,1:T(8,128)(2,1)S(1)} collective-permute-done((bf16[1024,2,512]{2,0,1:T(8,128)(2,1)S(1)}, bf16[1024,2,512]{2,0,1:T(8,128)(2,1)S(1)}, u32[]{:S(2)}, u32[]{:S(2)}) %collective-permute-start.6) | collective-permute-done | bytes 2097184 | tf_op jit(solution)/shard_map/ppermute | solution.py:219
  234.7 0.6 convert_add_fusion
  235.5 2.5 collective-permute-start.7
  238.0 23.4 %collective-permute-done.7 = bf16[1024,512]{1,0:T(8,128)(2,1)S(1)} collective-permute-done((bf16[1024,512]{1,0:T(8,128)(2,1)S(1)}, bf16[1024,512]{1,0:T(8,128)(2,1)S(1)}, u32[]{:S(2)}, u32[]{:S(2)}) %collective-permute-start.7) | collective-permute-done | bytes 1048608 | tf_op jit(solution)/shard_map/ppermute | solution.py:221
  261.4 1.3 fusion.5
  262.7 7.9 %all-to-all-start.3 = ((bf16[64,16,512]{2,1,0:T(8,128)(2,1)}), bf16[64,16,512]{2,1,0:T(8,128)(2,1)S(1)}, u32[]{:S(2)}, u32[]{:S(2)}) async-start(bf16[64,16,512]{2,1,0:T(8,128)(2,1)} %bitcast.61), calls=%async_computation.3 | async-start | bytes 2097152 | tf_op jit(solution)/shard_map/all_to_all | solution.py:227
  270.9 25.6 %all-to-all-done.3 = bf16[64,16,512]{2,1,0:T(8,128)(2,1)S(1)} async-done(((bf16[64,16,512]{2,1,0:T(8,128)(2,1)}), bf16[64,16,512]{2,1,0:T(8,128)(2,1)S(1)}, u32[]{:S(2)}, u32[]{:S(2)}) %all-to-all-start.3) | async-done | bytes 1048608 | tf_op jit(solution)/shard_map/all_to_all | solution.py:227
  296.5 3.3 %gather_fusion.6 = bf16[768,512]{1,0:T(8,128)(2,1)} fusion(bf16[1024,512]{1,0:T(8,128)(2,1)S(1)} %bitcast.190, s32[1024]{0:T(1024)S(1)} %pad_clamp_fusion), kind=kCustom, calls=%fused_computation.6 | custom fusion | bytes 1575936 | tf_op jit(solution)/shard_map/gather | solution.py:229
  299.8 1.4 fusion.8
  301.4 12.5 %all_gather.3 = bf16[128,2048]{0,1:T(8,128)(2,1)S(1)} all-gather(bf16[128,512]{0,1:T(8,128)(2,1)S(1)} %fusion.29), channel_id=1, replica_groups=mesh['req'=64,'tp'=4] {'tp'}, dimensions={1}, use_global_device_ids=true | all-gather | bytes 655360 | tf_op jit(solution)/shard_map/all_gather | solution.py:232
  313.9 1.0 copy.146
  (100 shorter events, 6.2 us)
Async XLA Ops:
  0.0 38.5 %copy-start = (bf16[2048,512]{1,0:T(8,128)(2,1)S(1)}, bf16[2048,512]{1,0:T(8,128)(2,1)}, u32[]{:S(2)}) copy-start(bf16[2048,512]{1,0:T(8,128)(2,1)} %param.16) | copy-start | bytes 6291460
  1.7 0.6 copy-start.20
  30.1 6.0 %copy-start.10 = (s32[128,6]{0,1:T(8,128)S(1)}, s32[128,6]{0,1:T(8,128)}, u32[]{:S(2)}) copy-start(s32[128,6]{0,1:T(8,128)} %param.26) | copy-start | bytes 9220
  30.1 7.1 %copy-start.13 = (s32[1,128]{1,0:T(1,128)S(1)}, s32[1,128]{1,0:T(1,128)}, u32[]{:S(2)}) copy-start(s32[1,128]{1,0:T(1,128)} %param.22) | copy-start | bytes 1540
  30.1 8.2 %copy-start.2 = (bf16[128,2048]{1,0:T(8,128)(2,1)S(1)}, bf16[128,2048]{1,0:T(8,128)(2,1)}, u32[]{:S(2)}) copy-start(bf16[128,2048]{1,0:T(8,128)(2,1)} %param.14) | copy-start | bytes 1572868
  30.1 8.4 %copy-start.11 = (f32[2048]{0:T(1024)S(1)}, f32[2048]{0:T(1024)}, u32[]{:S(2)}) copy-start(f32[2048]{0:T(1024)} %param.15) | copy-start | bytes 24580
  30.1 97.1 %all-to-all-start.1 = ((bf16[64,1,1,128,256]{4,3,2,1,0:T(8,128)(2,1)}), bf16[64,1,1,128,256]{4,3,2,1,0:T(8,128)(2,1)}, u32[]{:S(2)}, u32[]{:S(2)}) async-start(bf16[64,1,1,128,256]{4,3,2,1,0:T(8,128)(2,1)} %bitcast.191), calls=%async_computation.1 | async-start | bytes 8388608 | tf_op jit(solution)/shard_map/all_to_all | solution.py:135
  38.6 4.7 %copy-start.16 = (f32[128]{0:T(128)}, f32[128]{0:T(128)S(1)}, u32[]{:S(2)}) copy-start(f32[128]{0:T(128)S(1)} %add_rsqrt_fusion) | copy-start | bytes 1540
  57.7 2.4 copy-start.7
  61.3 0.7 copy-start.15
  66.9 4.1 %copy-start.4 = (f32[128,4,128]{2,1,0:T(4,128)S(1)}, f32[128,4,128]{2,1,0:T(4,128)}, u32[]{:S(2)}) copy-start(f32[128,4,128]{2,1,0:T(4,128)} %reshape.990) | copy-start | bytes 786436
  66.9 4.6 %copy-start.19 = (s32[1,32]{1,0:T(1,128)S(1)}, s32[1,32]{1,0:T(1,128)}, u32[]{:S(2)}) copy-start(s32[1,32]{1,0:T(1,128)} %param.24) | copy-start | bytes 388
  66.9 4.6 %copy-start.21 = (s32[32]{0:T(128)S(1)}, s32[32]{0:T(128)}, u32[]{:S(2)}) copy-start(s32[32]{0:T(128)} %copy-done.20) | copy-start | bytes 388
  66.9 4.6 %copy-start.3 = (bf16[128,2048]{1,0:T(8,128)(2,1)S(1)}, bf16[128,2048]{1,0:T(8,128)(2,1)}, u32[]{:S(2)}) copy-start(bf16[128,2048]{1,0:T(8,128)(2,1)} %param.14) | copy-start | bytes 1572868
  66.9 4.6 %copy-start.12 = (f32[2048]{0:T(1024)S(1)}, f32[2048]{0:T(1024)}, u32[]{:S(2)}) copy-start(f32[2048]{0:T(1024)} %param.15) | copy-start | bytes 24580
  66.9 4.6 %copy-start.17 = (f32[128]{0:T(128)S(1)}, f32[128]{0:T(128)}, u32[]{:S(2)}) copy-start(f32[128]{0:T(128)} %copy-done.16) | copy-start | bytes 1540
  69.4 2.2 copy-start.18
  131.4 1.7 copy-start.9
  138.2 7.1 %collective-permute-start = (f32[2,128,512]{1,2,0:T(8,128)S(1)}, f32[2,128,512]{1,2,0:T(8,128)S(1)}, u32[]{:S(2)}, u32[]{:S(2)}) collective-permute-start(f32[2,128,512]{1,2,0:T(8,128)S(1)} %slice.119), channel_id=1, source_target_pairs={{0,1},{1,0},{2,3},{3,2},{4,5},{5,4},{6,7},{7,6},{8,9},{9,8},{10,11... | collective-permute-start | bytes 1572872 | tf_op jit(solution)/shard_map/ppermute | solution.py:76
  145.3 9.1 %collective-permute-start.1 = (f32[128,512]{0,1:T(8,128)S(1)}, f32[128,512]{0,1:T(8,128)S(1)}, u32[]{:S(2)}, u32[]{:S(2)}) collective-permute-start(f32[128,512]{0,1:T(8,128)S(1)} %slice_bitcast_fusion.1), channel_id=1, source_target_pairs={{0,2},{2,0},{1,3},{3,1},{4,6},{6,4},{5,7},{7,5},{8,10},{10,8},{9,1... | collective-permute-start | bytes 786440 | tf_op jit(solution)/shard_map/ppermute | solution.py:78
  154.5 2.1 collective-permute-start.2
  156.6 3.9 %collective-permute-start.3 = (f32[128,1]{0,1:T(1,128)S(1)}, f32[128,1]{0,1:T(1,128)S(1)}, u32[]{:S(2)}, u32[]{:S(2)}) collective-permute-start(f32[128,1]{0,1:T(1,128)S(1)} %bitcast_add_fusion.1), channel_id=1, source_target_pairs={{0,2},{2,0},{1,3},{3,1},{4,6},{6,4},{5,7},{7,5},{8,10},{10,8},{9,1... | collective-permute-start | bytes 1544 | tf_op jit(solution)/shard_map/ppermute | solution.py:85
  192.5 22.3 %collective-permute-start.4 = (bf16[64,16,512]{2,1,0:T(8,128)(2,1)S(1)}, bf16[64,16,512]{2,1,0:T(8,128)(2,1)S(1)}, u32[]{:S(2)}, u32[]{:S(2)}) collective-permute-start(bf16[64,16,512]{2,1,0:T(8,128)(2,1)S(1)} %all_to_all.28), channel_id=1, source_target_pairs={{0,2},{2,0},{1,3},{3,1},{4,6},{6,4},{5,7},{7,5},{8,10},{10,8},{9,1... | collective-permute-start | bytes 3145736 | tf_op jit(solution)/shard_map/ppermute | solution.py:206
  214.8 9.0 %copy-start.6 = (bf16[4,512,352]{1,2,0:T(8,128)(2,1)S(1)}, bf16[4,512,352]{1,2,0:T(8,128)(2,1)}, u32[]{:S(2)}) copy-start(bf16[4,512,352]{1,2,0:T(8,128)(2,1)} %gather_fusion) | copy-start | bytes 4325380
  215.0 8.8 %collective-permute-start.5 = (bf16[2,64,16,512]{3,2,1,0:T(8,128)(2,1)S(1)}, bf16[2,64,16,512]{3,2,1,0:T(8,128)(2,1)S(1)}, u32[]{:S(2)}, u32[]{:S(2)}) collective-permute-start(bf16[2,64,16,512]{3,2,1,0:T(8,128)(2,1)S(1)} %pad_maximum_fusion.1), channel_id=1, source_target_pairs={{0,1},{1,0},{2,3},{3,2},{4,5},{5,4},{6,7},{7,6},{8,9},{9,8},{10,11... | collective-permute-start | bytes 6291464 | tf_op jit(solution)/shard_map/ppermute | solution.py:208
  223.8 2.0 copy-start.5
  225.8 2.0 copy-start.8
  230.4 4.2 %collective-permute-start.6 = (bf16[1024,2,512]{2,0,1:T(8,128)(2,1)S(1)}, bf16[1024,2,512]{2,0,1:T(8,128)(2,1)S(1)}, u32[]{:S(2)}, u32[]{:S(2)}) collective-permute-start(bf16[1024,2,512]{2,0,1:T(8,128)(2,1)S(1)} %slice.123), channel_id=1, source_target_pairs={{0,1},{1,0},{2,3},{3,2},{4,5},{5,4},{6,7},{7,6},{8,9},{9,8},{10,11... | collective-permute-start | bytes 6291464 | tf_op jit(solution)/shard_map/ppermute | solution.py:219
  235.5 25.9 %collective-permute-start.7 = (bf16[1024,512]{1,0:T(8,128)(2,1)S(1)}, bf16[1024,512]{1,0:T(8,128)(2,1)S(1)}, u32[]{:S(2)}, u32[]{:S(2)}) collective-permute-start(bf16[1024,512]{1,0:T(8,128)(2,1)S(1)} %fusion.23), channel_id=1, source_target_pairs={{0,2},{2,0},{1,3},{3,1},{4,6},{6,4},{5,7},{7,5},{8,10},{10,8},{9,1... | collective-permute-start | bytes 3145736 | tf_op jit(solution)/shard_map/ppermute | solution.py:221
  262.7 33.8 %all-to-all-start.3 = ((bf16[64,16,512]{2,1,0:T(8,128)(2,1)}), bf16[64,16,512]{2,1,0:T(8,128)(2,1)S(1)}, u32[]{:S(2)}, u32[]{:S(2)}) async-start(bf16[64,16,512]{2,1,0:T(8,128)(2,1)} %bitcast.61), calls=%async_computation.3 | async-start | bytes 2097152 | tf_op jit(solution)/shard_map/all_to_all | solution.py:227
  296.5 3.3 %copy-start.14 = (f32[128,6]{0,1:T(8,128)S(1)}, f32[128,6]{0,1:T(8,128)}, u32[]{:S(2)}) copy-start(f32[128,6]{0,1:T(8,128)} %param.27) | copy-start | bytes 9220
  296.5 18.4 %copy-start.1 = (bf16[2048,512]{1,0:T(8,128)(2,1)S(1)}, bf16[2048,512]{1,0:T(8,128)(2,1)}, u32[]{:S(2)}) copy-start(bf16[2048,512]{1,0:T(8,128)(2,1)} %param.16) | copy-start | bytes 6291460

commit v11 on v10

--- a/solution.py
+++ b/solution.py
@@ -203,10 +203,10 @@
         .reshape(n_exp, cap_e, quarter)
     )
     expert_q = lax.all_to_all(outgoing, "req", split_axis=0, concat_axis=0, tiled=True)
+    near_q = lax.ppermute(expert_q, "tp", ON_CHIP)
     cross_q = lax.ppermute(expert_q, "tp", CROSS_CHIP)
-    chip_pair = jnp.stack([expert_q, cross_q])
-    partner_pair = lax.ppermute(chip_pair, "tp", ON_CHIP)
-    expert_in = jnp.concatenate([chip_pair, partner_pair]).reshape(n_tp, -1, quarter)
+    far_q = lax.ppermute(cross_q, "tp", ON_CHIP)
+    expert_in = jnp.stack([expert_q, cross_q, near_q, far_q]).reshape(n_tp, -1, quarter)
     gate_part = jnp.einsum("qnd,qdh->nh", expert_in, gate_w, preferred_element_type=jnp.float32)
     up_part = jnp.einsum("qnd,qdh->nh", expert_in, up_w, preferred_element_type=jnp.float32)
     hidden_act = (jax.nn.silu(gate_part) * up_part).astype(jnp.bfloat16)

time: 316 us -> 321 us (1.016)
  waiting for transfers between devices: 137 us -> 131 us
  starting transfers between devices: 36.7 us -> 41.3 us
  matrix products: 11.5 us -> 15.9 us
    dot_general x1, matrix products: 2.46 us -> 7.64 us  [shards(): jnp.einsum('nh,hqd->nqd', hidden_act, down_w, preferred_element_type=jnp....]
    ppermute x1, waiting for transfers between devices: 19.7 us -> 15.1 us  [shards(): cross_q = lax.ppermute(expert_q, 'tp', CROSS_CHIP)]
    ppermute x1 -> x2, starting transfers between devices: 5.02 us -> 9.58 us  [the longest x1 4.94 us: shards(): far_q = lax.ppermute(cross_q, 'tp', ON_CHIP)]
  transfers between devices with their start and end apart: 10 -> 11, of which waited for: 10 -> 10; matrix products, arithmetic and copies ran while one was open for 12% -> 12% of each run, Pallas kernels for 0% -> 0%
where the time goes in v11:
time: 321 us; the launch traced here: 320 us
  waiting for transfers between devices  131 us (41%)
  blocking collectives  66.4 us (21%)
  local copies, waits for them, and re-layouts  46.6 us (15%)
  starting transfers between devices  41.3 us (13%)
  other arithmetic  17.6 us (5%)
  matrix products  15.9 us (5%)
    all_to_all x1, waiting for transfers between devices, shards(): lax.all_to_all(served, 'req', split_axis=0, concat_axis=0, tiled=True)  51.9 us
    all_to_all x1, blocking collectives, shards(): lax.all_to_all(outgoing, 'req', split_axis=0, concat_axis=0, tiled=True)  31.4 us
    all_to_all x1, waiting for transfers between devices, shards(): lax.all_to_all(expert_share, 'req', split_axis=0, concat_axis=0, tiled=True)  25.6 us
    ppermute x1, waiting for transfers between devices, shards(): lax.ppermute(chip_sum[:, 1].astype(jnp.bfloat16), 'tp', CROSS_CHIP)  23.4 us
    all_to_all x1, blocking collectives, shards(): lax.all_to_all(request, 'req', split_axis=0, concat_axis=0, tiled=True)  22.6 us
    ppermute x1, waiting for transfers between devices, shards(): cross_q = lax.ppermute(expert_q, 'tp', CROSS_CHIP)  15.1 us
    all_gather x1, blocking collectives, shards(): return lax.all_gather(layer_q, 'tp', axis=1, tiled=True)  12.5 us
    all_to_all x1, starting transfers between devices, shards(): lax.all_to_all(expert_share, 'req', split_axis=0, concat_axis=0, tiled=True)  7.96 us
  transfers between devices with their start and end apart: 11, of which 10 were waited for; matrix products, arithmetic and copies ran while one was open for 12% of the time, Pallas kernels for 0%

profile of v11, /device:TPU:1, one launch (start us, length us, event | category | flops | bytes accessed | tf_op | source)
XLA Modules:
  0.0 320.1 jit_solution(8782915096321656047)
XLA Ops:
  0.0 0.8 and_select_fusion.3
  0.8 0.7 fusion.60
  2.3 22.6 %all_to_all.27 = s32[64,1,1]{2,1,0:T(1,128)S(1)} all-to-all(s32[64,1,1]{2,1,0:T(1,128)S(1)} %copy.139), channel_id=1, replica_groups=mesh['req'=64,'tp'=4] {'req'}, dimensions={0} | all-to-all | bytes 512 | tf_op jit(solution)/shard_map/all_to_all | solution.py:131
  24.8 1.2 reduce.5
  26.1 4.0 %gather_fusion.4 = bf16[64,128,256]{2,1,0:T(8,128)(2,1)} fusion(bf16[16,128,256]{2,1,0:T(8,128)(2,1)} %bitcast.195, s32[1024]{0:T(1024)S(1)} %pad_clamp_fusion.2), kind=kCustom, calls=%fused_computation.4 | custom fusion | bytes 8388864 | tf_op jit(solution)/shard_map/gather | solution.py:132
  30.1 6.0 %all-to-all-start.1 = ((bf16[64,1,1,128,256]{4,3,2,1,0:T(8,128)(2,1)}), bf16[64,1,1,128,256]{4,3,2,1,0:T(8,128)(2,1)}, u32[]{:S(2)}, u32[]{:S(2)}) async-start(bf16[64,1,1,128,256]{4,3,2,1,0:T(8,128)(2,1)} %bitcast.194), calls=%async_computation.1 | async-start | bytes 8388608 | tf_op jit(solution)/shard_map/all_to_all | solution.py:135
  37.6 0.7 reduce.4
  39.0 0.8 reshape.993
  39.8 3.3 %fusion.68 = (bf16[1,1,2048,352]{2,3,1,0:T(8,128)(2,1)S(1)}, bf16[1,1,2048,352]{2,3,1,0:T(8,128)(2,1)}) fusion(bf16[1,2,2048,352]{2,3,1,0:T(8,128)(2,1)} %param.20), kind=kLoop, calls=%fused_computation.153 | loop fusion | bytes 5767168 | tf_op jit(solution)/shard_map/slice | solution.py:156
  43.1 1.1 reshape_squeeze.10
  44.5 4.4 %reshape_squeeze.9 = bf16[4,512,352]{1,0,2:T(4,128)(2,1)} reshape(bf16[1,1,2048,352]{2,3,1,0:T(8,128)(2,1)} %get-tuple-element.24) | data formatting | bytes 2883584 | tf_op jit(solution)/shard_map/reshape;squeeze | solution.py:155
  48.9 1.6 copy.127
  50.5 0.6 fusion.56
  51.2 1.7 gather_fusion.1
  52.9 1.8 gather_fusion
  54.7 2.9 copy.130
  57.6 2.4 copy.131
  60.0 1.1 reshape_squeeze.11
  61.8 0.6 pad_clamp_fusion.3
  62.4 2.4 gather_fusion.3
  64.8 1.9 gather_fusion.2
  66.7 1.8 reduce-window.18
  69.2 0.5 fusion.3
  69.8 0.7 add_convert_fusion.1
  72.1 2.4 broadcast_and_fusion
  74.5 0.9 pad_add_fusion
  75.4 51.9 %all-to-all-done.1 = bf16[64,1,1,128,256]{4,3,2,1,0:T(8,128)(2,1)} async-done(((bf16[64,1,1,128,256]{4,3,2,1,0:T(8,128)(2,1)}), bf16[64,1,1,128,256]{4,3,2,1,0:T(8,128)(2,1)}, u32[]{:S(2)}, u32[]{:S(2)}) %all-to-all-start.1) | async-done | bytes 4194336 | tf_op jit(solution)/shard_map/all_to_all | solution.py:135
  127.2 4.2 %gather_fusion.5 = bf16[32,128,256]{2,1,0:T(8,128)(2,1)} fusion(bf16[64,128,256]{2,1,0:T(8,128)(2,1)} %bitcast.22, s32[1024]{0:T(1024)S(1)} %pad_clamp_fusion.1), kind=kCustom, calls=%fused_computation.5 | custom fusion | bytes 4194432 | tf_op jit(solution)/shard_map/gather | solution.py:136
  131.4 1.7 fusion.69
  133.1 1.3 fusion.71
  134.4 1.1 fusion
  135.6 1.7 fusion.7
  137.3 0.7 convolution_bitcast_fusion.2
  138.1 5.5 %collective-permute-start = (f32[2,128,512]{1,2,0:T(8,128)S(1)}, f32[2,128,512]{1,2,0:T(8,128)S(1)}, u32[]{:S(2)}, u32[]{:S(2)}) collective-permute-start(f32[2,128,512]{1,2,0:T(8,128)S(1)} %slice.119), channel_id=1, source_target_pairs={{0,1},{1,0},{2,3},{3,2},{4,5},{5,4},{6,7},{7,6},{8,9},{9,8},{10,11... | collective-permute-start | bytes 1572872 | tf_op jit(solution)/shard_map/ppermute | solution.py:76
  143.7 1.5 collective-permute-done
  145.3 2.7 collective-permute-start.1
  148.1 6.2 %collective-permute-done.1 = f32[128,512]{0,1:T(8,128)S(1)} collective-permute-done((f32[128,512]{0,1:T(8,128)S(1)}, f32[128,512]{0,1:T(8,128)S(1)}, u32[]{:S(2)}, u32[]{:S(2)}) %collective-permute-start.1) | collective-permute-done | bytes 262176 | tf_op jit(solution)/shard_map/ppermute | solution.py:78
  154.5 1.3 collective-permute-start.2
  155.8 0.8 collective-permute-done.2
  156.6 2.6 collective-permute-start.3
  159.2 0.8 dynamic_slice.7
  160.0 0.5 collective-permute-done.3
  160.5 0.5 convolution_convert_fusion.1
  161.1 31.4 %all_to_all.28 = bf16[64,16,512]{2,1,0:T(8,128)(2,1)S(1)} all-to-all(bf16[64,16,512]{2,1,0:T(8,128)(2,1)S(1)} %bitcast.199), channel_id=1, replica_groups=mesh['req'=64,'tp'=4] {'req'}, dimensions={0} | all-to-all | bytes 2097152 | tf_op jit(solution)/shard_map/all_to_all | solution.py:205
  192.5 2.6 collective-permute-start.4
  195.1 4.6 %collective-permute-start.5 = (bf16[64,16,512]{2,1,0:T(8,128)(2,1)S(1)}, bf16[64,16,512]{2,1,0:T(8,128)(2,1)S(1)}, u32[]{:S(2)}, u32[]{:S(2)}) collective-permute-start(bf16[64,16,512]{2,1,0:T(8,128)(2,1)S(1)} %all_to_all.28), channel_id=1, source_target_pairs={{0,1},{1,0},{2,3},{3,2},{4,5},{5,4},{6,7},{7,6},{8,9},{9,8},{10,11... | collective-permute-start | bytes 3145736 | tf_op jit(solution)/shard_map/ppermute | solution.py:206
  199.7 15.1 %collective-permute-done.4 = bf16[64,16,512]{2,1,0:T(8,128)(2,1)S(1)} collective-permute-done((bf16[64,16,512]{2,1,0:T(8,128)(2,1)S(1)}, bf16[64,16,512]{2,1,0:T(8,128)(2,1)S(1)}, u32[]{:S(2)}, u32[]{:S(2)}) %collective-permute-start.4) | collective-permute-done | bytes 1048608 | tf_op jit(solution)/shard_map/ppermute | solution.py:207
  214.8 4.9 %collective-permute-start.6 = (bf16[64,16,512]{2,1,0:T(8,128)(2,1)S(1)}, bf16[64,16,512]{2,1,0:T(8,128)(2,1)S(1)}, u32[]{:S(2)}, u32[]{:S(2)}) collective-permute-start(bf16[64,16,512]{2,1,0:T(8,128)(2,1)S(1)} %collective-permute-done.4), channel_id=1, source_target_pairs={{0,1},{1,0},{2,3},{3,2},{4,5},{5,4},{6,7},{7,6},{8,9},{9,8},{10,11... | collective-permute-start | bytes 3145736 | tf_op jit(solution)/shard_map/ppermute | solution.py:208
  219.7 2.3 collective-permute-done.6
  222.1 1.0 copy-done.25
  223.0 3.1 convolution_bitcast_fusion
  226.1 7.6 %convolution_convert_fusion = bf16[1024,4,512]{2,0,1:T(8,128)(2,1)} fusion(bf16[352,4,512]{2,0,1:T(8,128)(2,1)S(1)} %bitcast.201, f32[1024,352]{0,1:T(8,128)} %convolution_bitcast_fusion, bf16[4,512,352]{1,2,0:T(8,128)(2,1)S(1)} %copy-done.7, bf16[1,1024,512]{2,1,0:T(8,128)(2,1)} %bitcast.218, bf16[1,1024,512]{2,1,0:T(8,128)(2,1)} %bitcast.216, ...), kind=kOutput, calls=%fused_computation.17 | convolution fusion | flops 2963341312 | bytes 12713984 | tf_op jit(solution)/shard_map/nh,hqd->nqd/dot_general | solution.py:213
  233.7 1.9 slice.123
  236.1 3.8 %collective-permute-done.7 = bf16[1024,2,512]{2,0,1:T(8,128)(2,1)S(1)} collective-permute-done((bf16[1024,2,512]{2,0,1:T(8,128)(2,1)S(1)}, bf16[1024,2,512]{2,0,1:T(8,128)(2,1)S(1)}, u32[]{:S(2)}, u32[]{:S(2)}) %collective-permute-start.7) | collective-permute-done | bytes 2097184 | tf_op jit(solution)/shard_map/ppermute | solution.py:219
  239.9 0.6 convert_add_fusion
  240.7 2.5 collective-permute-start.8
  243.2 23.4 %collective-permute-done.8 = bf16[1024,512]{1,0:T(8,128)(2,1)S(1)} collective-permute-done((bf16[1024,512]{1,0:T(8,128)(2,1)S(1)}, bf16[1024,512]{1,0:T(8,128)(2,1)S(1)}, u32[]{:S(2)}, u32[]{:S(2)}) %collective-permute-start.8) | collective-permute-done | bytes 1048608 | tf_op jit(solution)/shard_map/ppermute | solution.py:221
  266.6 1.3 fusion.5
  267.9 8.0 %all-to-all-start.3 = ((bf16[64,16,512]{2,1,0:T(8,128)(2,1)}), bf16[64,16,512]{2,1,0:T(8,128)(2,1)S(1)}, u32[]{:S(2)}, u32[]{:S(2)}) async-start(bf16[64,16,512]{2,1,0:T(8,128)(2,1)} %bitcast.60), calls=%async_computation.3 | async-start | bytes 2097152 | tf_op jit(solution)/shard_map/all_to_all | solution.py:227
  276.1 25.6 %all-to-all-done.3 = bf16[64,16,512]{2,1,0:T(8,128)(2,1)S(1)} async-done(((bf16[64,16,512]{2,1,0:T(8,128)(2,1)}), bf16[64,16,512]{2,1,0:T(8,128)(2,1)S(1)}, u32[]{:S(2)}, u32[]{:S(2)}) %all-to-all-start.3) | async-done | bytes 1048608 | tf_op jit(solution)/shard_map/all_to_all | solution.py:227
  301.8 3.3 %gather_fusion.6 = bf16[768,512]{1,0:T(8,128)(2,1)} fusion(bf16[1024,512]{1,0:T(8,128)(2,1)S(1)} %bitcast.193, s32[1024]{0:T(1024)S(1)} %pad_clamp_fusion), kind=kCustom, calls=%fused_computation.6 | custom fusion | bytes 1575936 | tf_op jit(solution)/shard_map/gather | solution.py:229
  305.1 1.4 fusion.6
  306.6 12.5 %all_gather.3 = bf16[128,2048]{0,1:T(8,128)(2,1)S(1)} all-gather(bf16[128,512]{0,1:T(8,128)(2,1)S(1)} %fusion.25), channel_id=1, replica_groups=mesh['req'=64,'tp'=4] {'tp'}, dimensions={1}, use_global_device_ids=true | all-gather | bytes 655360 | tf_op jit(solution)/shard_map/all_gather | solution.py:232
  319.1 1.0 copy.146
  (114 shorter events, 6.8 us)
Async XLA Ops:
  0.0 38.5 %copy-start = (bf16[2048,512]{1,0:T(8,128)(2,1)S(1)}, bf16[2048,512]{1,0:T(8,128)(2,1)}, u32[]{:S(2)}) copy-start(bf16[2048,512]{1,0:T(8,128)(2,1)} %param.16) | copy-start | bytes 6291460
  1.7 0.5 copy-start.27
  30.1 6.0 %copy-start.14 = (s32[128,6]{0,1:T(8,128)S(1)}, s32[128,6]{0,1:T(8,128)}, u32[]{:S(2)}) copy-start(s32[128,6]{0,1:T(8,128)} %param.26) | copy-start | bytes 9220
  30.1 7.1 %copy-start.17 = (s32[1,128]{1,0:T(1,128)S(1)}, s32[1,128]{1,0:T(1,128)}, u32[]{:S(2)}) copy-start(s32[1,128]{1,0:T(1,128)} %param.22) | copy-start | bytes 1540
  30.1 8.2 %copy-start.3 = (bf16[128,2048]{1,0:T(8,128)(2,1)S(1)}, bf16[128,2048]{1,0:T(8,128)(2,1)}, u32[]{:S(2)}) copy-start(bf16[128,2048]{1,0:T(8,128)(2,1)} %param.14) | copy-start | bytes 1572868
  30.1 8.4 %copy-start.15 = (f32[2048]{0:T(1024)S(1)}, f32[2048]{0:T(1024)}, u32[]{:S(2)}) copy-start(f32[2048]{0:T(1024)} %param.15) | copy-start | bytes 24580
  30.1 97.1 %all-to-all-start.1 = ((bf16[64,1,1,128,256]{4,3,2,1,0:T(8,128)(2,1)}), bf16[64,1,1,128,256]{4,3,2,1,0:T(8,128)(2,1)}, u32[]{:S(2)}, u32[]{:S(2)}) async-start(bf16[64,1,1,128,256]{4,3,2,1,0:T(8,128)(2,1)} %bitcast.194), calls=%async_computation.1 | async-start | bytes 8388608 | tf_op jit(solution)/shard_map/all_to_all | solution.py:135
  38.5 4.6 %copy-start.20 = (f32[128]{0:T(128)}, f32[128]{0:T(128)S(1)}, u32[]{:S(2)}) copy-start(f32[128]{0:T(128)S(1)} %add_rsqrt_fusion) | copy-start | bytes 1540
  57.6 2.4 copy-start.8
  61.1 0.6 copy-start.19
  66.6 4.1 %copy-start.5 = (f32[128,4,128]{2,1,0:T(4,128)S(1)}, f32[128,4,128]{2,1,0:T(4,128)}, u32[]{:S(2)}) copy-start(f32[128,4,128]{2,1,0:T(4,128)} %reshape.993) | copy-start | bytes 786436
  66.6 4.6 %copy-start.26 = (s32[1,32]{1,0:T(1,128)S(1)}, s32[1,32]{1,0:T(1,128)}, u32[]{:S(2)}) copy-start(s32[1,32]{1,0:T(1,128)} %param.24) | copy-start | bytes 388
  66.6 4.6 %copy-start.28 = (s32[32]{0:T(128)S(1)}, s32[32]{0:T(128)}, u32[]{:S(2)}) copy-start(s32[32]{0:T(128)} %copy-done.27) | copy-start | bytes 388
  66.7 4.6 %copy-start.4 = (bf16[128,2048]{1,0:T(8,128)(2,1)S(1)}, bf16[128,2048]{1,0:T(8,128)(2,1)}, u32[]{:S(2)}) copy-start(bf16[128,2048]{1,0:T(8,128)(2,1)} %param.14) | copy-start | bytes 1572868
  66.7 4.6 %copy-start.16 = (f32[2048]{0:T(1024)S(1)}, f32[2048]{0:T(1024)}, u32[]{:S(2)}) copy-start(f32[2048]{0:T(1024)} %param.15) | copy-start | bytes 24580
  66.7 4.6 %copy-start.21 = (f32[128]{0:T(128)S(1)}, f32[128]{0:T(128)}, u32[]{:S(2)}) copy-start(f32[128]{0:T(128)} %copy-done.20) | copy-start | bytes 1540
  69.1 2.1 copy-start.22
  131.4 1.7 copy-start.13
  138.1 7.1 %collective-permute-start = (f32[2,128,512]{1,2,0:T(8,128)S(1)}, f32[2,128,512]{1,2,0:T(8,128)S(1)}, u32[]{:S(2)}, u32[]{:S(2)}) collective-permute-start(f32[2,128,512]{1,2,0:T(8,128)S(1)} %slice.119), channel_id=1, source_target_pairs={{0,1},{1,0},{2,3},{3,2},{4,5},{5,4},{6,7},{7,6},{8,9},{9,8},{10,11... | collective-permute-start | bytes 1572872 | tf_op jit(solution)/shard_map/ppermute | solution.py:76
  145.3 9.1 %collective-permute-start.1 = (f32[128,512]{0,1:T(8,128)S(1)}, f32[128,512]{0,1:T(8,128)S(1)}, u32[]{:S(2)}, u32[]{:S(2)}) collective-permute-start(f32[128,512]{0,1:T(8,128)S(1)} %slice_bitcast_fusion.1), channel_id=1, source_target_pairs={{0,2},{2,0},{1,3},{3,1},{4,6},{6,4},{5,7},{7,5},{8,10},{10,8},{9,1... | collective-permute-start | bytes 786440 | tf_op jit(solution)/shard_map/ppermute | solution.py:78
  148.1 74.9 %copy-start.6 = (bf16[4,512,352]{1,2,0:T(8,128)(2,1)S(1)}, bf16[4,512,352]{1,2,0:T(8,128)(2,1)}, u32[]{:S(2)}) copy-start(bf16[4,512,352]{1,2,0:T(8,128)(2,1)} %gather_fusion.1) | copy-start | bytes 4325380
  154.5 67.6 %copy-start.10 = (bf16[128,512]{0,1:T(8,128)(2,1)}, bf16[128,512]{0,1:T(8,128)(2,1)S(1)}, u32[]{:S(2)}) copy-start(bf16[128,512]{0,1:T(8,128)(2,1)S(1)} %get-tuple-element.20) | copy-start | bytes 393220
  154.5 2.1 collective-permute-start.2
  156.6 3.9 %collective-permute-start.3 = (f32[128,1]{0,1:T(1,128)S(1)}, f32[128,1]{0,1:T(1,128)S(1)}, u32[]{:S(2)}, u32[]{:S(2)}) collective-permute-start(f32[128,1]{0,1:T(1,128)S(1)} %bitcast_add_fusion.1), channel_id=1, source_target_pairs={{0,2},{2,0},{1,3},{3,1},{4,6},{6,4},{5,7},{7,5},{8,10},{10,8},{9,1... | collective-permute-start | bytes 1544 | tf_op jit(solution)/shard_map/ppermute | solution.py:85
  192.5 29.6 %copy-start.12 = (bf16[64,16,512]{2,1,0:T(8,128)(2,1)}, bf16[64,16,512]{2,1,0:T(8,128)(2,1)S(1)}, u32[]{:S(2)}) copy-start(bf16[64,16,512]{2,1,0:T(8,128)(2,1)S(1)} %all_to_all.28) | copy-start | bytes 3145732
  192.5 22.3 %collective-permute-start.4 = (bf16[64,16,512]{2,1,0:T(8,128)(2,1)S(1)}, bf16[64,16,512]{2,1,0:T(8,128)(2,1)S(1)}, u32[]{:S(2)}, u32[]{:S(2)}) collective-permute-start(bf16[64,16,512]{2,1,0:T(8,128)(2,1)S(1)} %all_to_all.28), channel_id=1, source_target_pairs={{0,2},{2,0},{1,3},{3,1},{4,6},{6,4},{5,7},{7,5},{8,10},{10,8},{9,1... | collective-permute-start | bytes 3145736 | tf_op jit(solution)/shard_map/ppermute | solution.py:207
  195.1 24.6 %collective-permute-start.5 = (bf16[64,16,512]{2,1,0:T(8,128)(2,1)S(1)}, bf16[64,16,512]{2,1,0:T(8,128)(2,1)S(1)}, u32[]{:S(2)}, u32[]{:S(2)}) collective-permute-start(bf16[64,16,512]{2,1,0:T(8,128)(2,1)S(1)} %all_to_all.28), channel_id=1, source_target_pairs={{0,1},{1,0},{2,3},{3,2},{4,5},{5,4},{6,7},{7,6},{8,9},{9,8},{10,11... | collective-permute-start | bytes 3145736 | tf_op jit(solution)/shard_map/ppermute | solution.py:206
  214.8 7.2 %copy-start.23 = (bf16[64,16,512]{2,1,0:T(8,128)(2,1)}, bf16[64,16,512]{2,1,0:T(8,128)(2,1)S(1)}, u32[]{:S(2)}) copy-start(bf16[64,16,512]{2,1,0:T(8,128)(2,1)S(1)} %collective-permute-done.4) | copy-start | bytes 3145732
  214.8 7.2 %collective-permute-start.6 = (bf16[64,16,512]{2,1,0:T(8,128)(2,1)S(1)}, bf16[64,16,512]{2,1,0:T(8,128)(2,1)S(1)}, u32[]{:S(2)}, u32[]{:S(2)}) collective-permute-start(bf16[64,16,512]{2,1,0:T(8,128)(2,1)S(1)} %collective-permute-done.4), channel_id=1, source_target_pairs={{0,1},{1,0},{2,3},{3,2},{4,5},{5,4},{6,7},{7,6},{8,9},{9,8},{10,11... | collective-permute-start | bytes 3145736 | tf_op jit(solution)/shard_map/ppermute | solution.py:208
  219.7 2.3 copy-start.24
  222.0 1.0 copy-start.25
  223.0 3.1 copy-start.7
  223.0 3.1 copy-start.9
  233.7 6.1 %copy-start.2 = (bf16[1024,4,512]{2,0,1:T(8,128)(2,1)S(1)}, bf16[1024,4,512]{2,0,1:T(8,128)(2,1)}, u32[]{:S(2)}) copy-start(bf16[1024,4,512]{2,0,1:T(8,128)(2,1)} %convolution_convert_fusion) | copy-start | bytes 12582916
  235.6 4.2 %collective-permute-start.7 = (bf16[1024,2,512]{2,0,1:T(8,128)(2,1)S(1)}, bf16[1024,2,512]{2,0,1:T(8,128)(2,1)S(1)}, u32[]{:S(2)}, u32[]{:S(2)}) collective-permute-start(bf16[1024,2,512]{2,0,1:T(8,128)(2,1)S(1)} %slice.123), channel_id=1, source_target_pairs={{0,1},{1,0},{2,3},{3,2},{4,5},{5,4},{6,7},{7,6},{8,9},{9,8},{10,11... | collective-permute-start | bytes 6291464 | tf_op jit(solution)/shard_map/ppermute | solution.py:219
  240.7 25.9 %collective-permute-start.8 = (bf16[1024,512]{1,0:T(8,128)(2,1)S(1)}, bf16[1024,512]{1,0:T(8,128)(2,1)S(1)}, u32[]{:S(2)}, u32[]{:S(2)}) collective-permute-start(bf16[1024,512]{1,0:T(8,128)(2,1)S(1)} %fusion.19), channel_id=1, source_target_pairs={{0,2},{2,0},{1,3},{3,1},{4,6},{6,4},{5,7},{7,5},{8,10},{10,8},{9,1... | collective-permute-start | bytes 3145736 | tf_op jit(solution)/shard_map/ppermute | solution.py:221
  267.9 33.9 %all-to-all-start.3 = ((bf16[64,16,512]{2,1,0:T(8,128)(2,1)}), bf16[64,16,512]{2,1,0:T(8,128)(2,1)S(1)}, u32[]{:S(2)}, u32[]{:S(2)}) async-start(bf16[64,16,512]{2,1,0:T(8,128)(2,1)} %bitcast.60), calls=%async_computation.3 | async-start | bytes 2097152 | tf_op jit(solution)/shard_map/all_to_all | solution.py:227
  301.8 3.3 %copy-start.18 = (f32[128,6]{0,1:T(8,128)S(1)}, f32[128,6]{0,1:T(8,128)}, u32[]{:S(2)}) copy-start(f32[128,6]{0,1:T(8,128)} %param.27) | copy-start | bytes 9220
  301.8 4.8 %copy-start.11 = (bf16[128,512]{0,1:T(8,128)(2,1)S(1)}, bf16[128,512]{0,1:T(8,128)(2,1)}, u32[]{:S(2)}) copy-start(bf16[128,512]{0,1:T(8,128)(2,1)} %copy-done.10) | copy-start | bytes 393220
  301.8 18.4 %copy-start.1 = (bf16[2048,512]{1,0:T(8,128)(2,1)S(1)}, bf16[2048,512]{1,0:T(8,128)(2,1)}, u32[]{:S(2)}) copy-start(bf16[2048,512]{1,0:T(8,128)(2,1)} %param.16) | copy-start | bytes 6291460
